TPU v7x, 32 devices: a whole 2x2x4 slice. The times are simulated.
32 devices in a mesh: outer: 4 (over y, x), inner: 8 (over z, core).
Axes of the slice: x: 2, y: 2, z: 4, core: 2. Of those that a mesh axis runs over, the one named last changes fastest.
Arguments:
- tokens: bfloat16 [4096, 2048], P(('outer', 'inner')), may hold values from -6 to 6
- cotangent: bfloat16 [4096, 2048], P(('outer', 'inner')), may hold values from -6 to 6
- routes: int32 [4096, 8], P(('outer', 'inner')), may hold values from 0 to 31, all different within a row; in each aligned block of 128 rows (0 to 127, 128 to 255, ...) at most 36 rows name the same one
- router_weight: bfloat16 [2048, 32], replicated, may hold values from -0.125 to 0.125
- gate_saved: bfloat16 [32, 1152, 768], P(('outer', 'inner')), may hold values from -6 to 6
- up_saved: bfloat16 [32, 1152, 768], P(('outer', 'inner')), may hold values from -6 to 6
- gate_weight: bfloat16 [32, 2048, 768], P(('outer', 'inner')), may hold values from -0.125 to 0.125
- up_weight: bfloat16 [32, 2048, 768], P(('outer', 'inner')), may hold values from -0.125 to 0.125
- down_weight: bfloat16 [32, 768, 2048], P(('outer', 'inner')), may hold values from -0.21875 to 0.21875
Outputs:
- grad_tokens: bfloat16 [4096, 2048], P(('outer', 'inner'))
- grad_gate: bfloat16 [32, 2048, 768], P(('outer', 'inner'))
- grad_up: bfloat16 [32, 2048, 768], P(('outer', 'inner'))
- grad_down: bfloat16 [32, 768, 2048], P(('outer', 'inner'))
- grad_router: float32 [2048, 32], replicated
Inputs may be any that keep to these rules, and one draw needn't show every extreme that they name: `routes`: each row names 8 different experts. Among the rows of one device no expert is named more than 36 times, and in every draw some expert is named exactly 36 times by the rows of some device.
All inputs are finite; a program needn't handle non-finite values.
Results may differ from a plain program's by a relative error of at most 0.01.
Values may be sent and summed in bfloat16 or wider, within the bound.
No kernel may reach another device: no remote copies, remote signals or barrier semaphores. Data moves between devices by JAX's collectives and lax.ppermute only.
A program may use at most 192 MiB of HBM per device.

v0:
```python
import math

import jax
import jax.numpy as jnp
from jax import lax
from jax.sharding import PartitionSpec as P

contract_rows = (((0,), (0,)), ((), ()))
contract_cols = (((1,), (1,)), ((), ()))


def route_tables(routes, experts, capacity):
    flat_routes = routes.reshape(-1)
    onehot = (flat_routes[:, None] == jnp.arange(experts, dtype=jnp.int32)[None, :]).astype(
        jnp.int32
    )
    earlier = jnp.cumsum(onehot, axis=0) - onehot
    position = jnp.sum(earlier * onehot, axis=1)
    target = flat_routes * capacity + position
    slot_table = (
        jnp.arange(experts * capacity, dtype=jnp.int32)[:, None] == target[None, :]
    ).astype(jnp.bfloat16)
    token_table = jnp.sum(
        slot_table.reshape(experts * capacity, routes.shape[0], routes.shape[1]), axis=2
    )
    return (slot_table, token_table)


def route_probs(tokens, routes, router_weight):
    router_logits = jnp.dot(tokens, router_weight, preferred_element_type=jnp.float32)
    picked = (
        routes[:, :, None] == jnp.arange(router_weight.shape[1], dtype=jnp.int32)[None, None, :]
    )
    chosen = jnp.sum(jnp.where(picked, router_logits[:, None, :], jnp.float32(0.0)), axis=2)
    exp_terms = jnp.exp(chosen)
    return (picked, exp_terms / jnp.sum(exp_terms, axis=1, keepdims=True))


def dispatch_block(tokens, cotangent, routes, router_weight, capacity):
    picked, probs = route_probs(tokens, routes, router_weight)
    slot_table, token_table = route_tables(routes, router_weight.shape[1], capacity)
    send_tokens = jnp.dot(token_table, tokens, preferred_element_type=jnp.float32).astype(
        jnp.bfloat16
    )
    send_cot = jnp.dot(token_table, cotangent, preferred_element_type=jnp.float32).astype(
        jnp.bfloat16
    )
    probs_low = probs.astype(jnp.bfloat16).reshape(-1)
    send_weight = jnp.dot(slot_table, probs_low, preferred_element_type=jnp.float32).astype(
        jnp.bfloat16
    )
    return (picked, probs, slot_table, token_table, send_tokens, send_cot, send_weight)


def slot_dot(cot_rows, out_rows):
    return jnp.sum(cot_rows.astype(jnp.float32) * out_rows.astype(jnp.float32), axis=1).astype(
        jnp.bfloat16
    )


def expert_backward(
    input_rows, cot_rows, weight_rows, gate_pre, up_pre, gate_matrix, up_matrix, down_matrix
):
    gate_value = gate_pre.astype(jnp.float32)
    up_value = up_pre.astype(jnp.float32)
    sigmoid_gate = jax.nn.sigmoid(gate_value)
    silu_gate = gate_value * sigmoid_gate
    hidden = (silu_gate * up_value).astype(jnp.bfloat16)
    expert_out = jnp.dot(hidden, down_matrix, preferred_element_type=jnp.float32).astype(
        jnp.bfloat16
    )
    scaled_cot = (weight_rows.astype(jnp.float32)[:, None] * cot_rows.astype(jnp.float32)).astype(
        jnp.bfloat16
    )
    grad_hidden = lax.dot_general(
        scaled_cot, down_matrix, contract_cols, preferred_element_type=jnp.float32
    )
    grad_gate_pre = (
        grad_hidden * up_value * sigmoid_gate * (1.0 + gate_value * (1.0 - sigmoid_gate))
    ).astype(jnp.bfloat16)
    grad_up_pre = (grad_hidden * silu_gate).astype(jnp.bfloat16)
    grad_rows = (
        lax.dot_general(
            grad_gate_pre, gate_matrix, contract_cols, preferred_element_type=jnp.float32
        )
        + lax.dot_general(grad_up_pre, up_matrix, contract_cols, preferred_element_type=jnp.float32)
    ).astype(jnp.bfloat16)
    grad_gate_w = lax.dot_general(
        input_rows, grad_gate_pre, contract_rows, preferred_element_type=jnp.float32
    ).astype(jnp.bfloat16)
    grad_up_w = lax.dot_general(
        input_rows, grad_up_pre, contract_rows, preferred_element_type=jnp.float32
    ).astype(jnp.bfloat16)
    grad_down_w = lax.dot_general(
        hidden, scaled_cot, contract_rows, preferred_element_type=jnp.float32
    ).astype(jnp.bfloat16)
    return (grad_rows, expert_out, grad_gate_w, grad_up_w, grad_down_w)


def finish_block(
    tokens, router_weight, picked, probs, slot_table, token_table, back_rows, route_dot
):
    grad_sum = lax.dot_general(
        token_table, back_rows, contract_rows, preferred_element_type=jnp.float32
    )
    route_grad = lax.dot_general(
        slot_table, route_dot, contract_rows, preferred_element_type=jnp.float32
    ).reshape(probs.shape)
    inner_term = jnp.sum(probs * route_grad, axis=1, keepdims=True)
    chosen_grad = probs * (route_grad - inner_term)
    logit_grad = jnp.sum(
        jnp.where(picked, chosen_grad[:, :, None], jnp.float32(0.0)), axis=1
    ).astype(jnp.bfloat16)
    grad_tokens = (
        grad_sum
        + lax.dot_general(
            logit_grad, router_weight, contract_cols, preferred_element_type=jnp.float32
        )
    ).astype(jnp.bfloat16)
    router_part = lax.dot_general(
        tokens, logit_grad, contract_rows, preferred_element_type=jnp.float32
    )
    return (grad_tokens, router_part)


def body(
    tokens,
    cotangent,
    routes,
    router_weight,
    gate_saved,
    up_saved,
    gate_weight,
    up_weight,
    down_weight,
):
    experts = router_weight.shape[1]
    width = tokens.shape[1]
    capacity = gate_saved.shape[1] // experts
    outer_size = lax.axis_size("outer")
    inner_size = lax.axis_size("inner")
    picked, probs, slot_table, token_table, send_tokens, send_cot, send_weight = dispatch_block(
        tokens, cotangent, routes, router_weight, capacity
    )
    grid_tokens = send_tokens.reshape(experts, capacity, width)
    grid_cot = send_cot.reshape(experts, capacity, width)
    grid_weight = send_weight.reshape(experts, capacity)
    got_tokens, got_cot, got_weight = (
        lax.all_to_all(grid_tokens, ("outer", "inner"), split_axis=0, concat_axis=0, tiled=True),
        lax.all_to_all(grid_cot, ("outer", "inner"), split_axis=0, concat_axis=0, tiled=True),
        lax.all_to_all(grid_weight, ("outer", "inner"), split_axis=0, concat_axis=0, tiled=True),
    )
    cot_rows = got_cot.reshape(-1, width)
    grad_rows, expert_out, grad_gate_w, grad_up_w, grad_down_w = expert_backward(
        got_tokens.reshape(-1, width),
        cot_rows,
        got_weight.reshape(-1),
        gate_saved[0],
        up_saved[0],
        gate_weight[0],
        up_weight[0],
        down_weight[0],
    )
    back_grad = grad_rows.reshape(experts, capacity, width)
    extra = expert_out.reshape(experts, capacity, width)
    back_rows, back_extra = (
        lax.all_to_all(back_grad, ("outer", "inner"), split_axis=0, concat_axis=0, tiled=True),
        lax.all_to_all(extra, ("outer", "inner"), split_axis=0, concat_axis=0, tiled=True),
    )
    route_dot = slot_dot(send_cot, back_extra.reshape(-1, width))
    grad_tokens, router_part = finish_block(
        tokens,
        router_weight,
        picked,
        probs,
        slot_table,
        token_table,
        back_rows.reshape(-1, width),
        route_dot,
    )
    total_tokens = tokens.shape[0] * outer_size * inner_size
    grad_router = lax.psum(router_part, ("outer", "inner")) * (1.0 / math.sqrt(total_tokens))
    return (grad_tokens, grad_gate_w[None], grad_up_w[None], grad_down_w[None], grad_router)


def solution(mesh):
    in_specs = (
        P(("outer", "inner"), None),
        P(("outer", "inner"), None),
        P(("outer", "inner"), None),
        P(),
        P(("outer", "inner"), None, None),
        P(("outer", "inner"), None, None),
        P(("outer", "inner"), None, None),
        P(("outer", "inner"), None, None),
        P(("outer", "inner"), None, None),
    )
    out_specs = (
        P(("outer", "inner"), None),
        P(("outer", "inner"), None, None),
        P(("outer", "inner"), None, None),
        P(("outer", "inner"), None, None),
        P(),
    )
    return jax.shard_map(body, mesh=mesh, in_specs=in_specs, out_specs=out_specs, check_vma=False)
```

profile of v0, /device:TPU:0, one launch (start us, length us, event | category | flops | bytes accessed | tf_op | source)
XLA Modules:
  0.0 628.6 jit_solution(13599808058669787535)
XLA Ops:
  9.1 8.1 %convolution_convert_fusion = bf16[1152,2048]{1,0:T(8,128)(2,1)} fusion(bf16[1,768,2048]{2,1,0:T(8,128)(2,1)S(1)} %copy-done, bf16[1,1152,768]{2,1,0:T(8,128)(2,1)} %param.14, bf16[1,1152,768]{2,1,0:T(8,128)(2,1)} %param.13), kind=kOutput, calls=%fused_computation.3 | convolution fusion | flops 3633315840 | bytes 11403264 | tf_op jit(solution)/shard_map/dot_general | solution.py:69
  17.1 7.2 %reshape.153 = bf16[32,36,2048]{2,1,0:T(8,128)(2,1)} reshape(bf16[1152,2048]{1,0:T(8,128)(2,1)} %convolution_convert_fusion) | data formatting | bytes 9437184 | tf_op jit(solution)/shard_map/reshape | solution.py:165
  24.3 7.4 %all-to-all-start.3 = ((bf16[32,36,2048]{2,1,0:T(8,128)(2,1)}), bf16[32,36,2048]{2,1,0:T(8,128)(2,1)}, u32[]{:S(2)}, u32[]{:S(2)}) async-start(bf16[32,36,2048]{2,1,0:T(8,128)(2,1)} %reshape.153), calls=%async_computation.3 | async-start | bytes 10485760 | tf_op jit(solution)/shard_map/all_to_all | solution.py:168
  32.0 9.0 %reduce-window.6 = s32[32,8,128]{2,1,0:T(8,128)S(1)} reduce-window(s32[32,8,128]{2,1,0:T(8,128)S(1)} %fusion.39, s32[]{:T(128)} %constant.5.clone.1), window={size=1x1x128 pad=0_0x0_0x127_0}, to_apply=%region_0.1 | reduce-window | flops 4161536 | bytes 262148 | tf_op jit(solution)/shard_map/reduce-window
  43.1 6.0 fusion.30
  49.1 100.1 %all-to-all-done.3 = bf16[32,36,2048]{2,1,0:T(8,128)(2,1)} async-done(((bf16[32,36,2048]{2,1,0:T(8,128)(2,1)}), bf16[32,36,2048]{2,1,0:T(8,128)(2,1)}, u32[]{:S(2)}, u32[]{:S(2)}) %all-to-all-start.3) | async-done | bytes 4718624 | tf_op jit(solution)/shard_map/all_to_all | solution.py:168
  149.2 8.0 %reshape.160 = f32[1152,2048]{1,0:T(8,128)} reshape(bf16[32,36,2048]{2,1,0:T(8,128)(2,1)} %all-to-all-done.3) | data formatting | bytes 14155776 | tf_op jit(solution)/shard_map/convert_element_type | solution.py:56
  157.2 7.5 %multiply_reduce_fusion = (bf16[1152]{0:T(1024)(128)(2,1)S(1)}, bf16[1152,2048]{1,0:T(8,128)(2,1)}) fusion(f32[1152,2048]{1,0:T(8,128)} %reshape.160, bf16[1152,128]{1,0:T(8,128)(2,1)S(1)} %fusion.30, bf16[128,2048]{1,0:T(8,128)(2,1)} %param.10), kind=kOutput, calls=%fused_computation.1 | convolution fusion | flops 613415808 | bytes 14977280 | tf_op jit(solution)/shard_map/dot_general | solution.py:45
  170.2 7.2 %reshape.150 = bf16[32,36,2048]{2,1,0:T(8,128)(2,1)} reshape(bf16[1152,2048]{1,0:T(8,128)(2,1)} %get-tuple-element.8) | data formatting | bytes 9437184 | tf_op jit(solution)/shard_map/reshape | solution.py:146
  177.4 5.9 all-to-all-start.1
  187.9 7.2 %reshape.155 = bf16[32,36,2048]{2,1,0:T(8,128)(2,1)} reshape(bf16[1152,2048]{1,0:T(8,128)(2,1)} %convolution_convert_fusion.1) | data formatting | bytes 9437184 | tf_op jit(solution)/shard_map/reshape | solution.py:145
  195.1 105.8 %all-to-all-done.1 = bf16[32,36,2048]{2,1,0:T(8,128)(2,1)} async-done(((bf16[32,36,2048]{2,1,0:T(8,128)(2,1)}), bf16[32,36,2048]{2,1,0:T(8,128)(2,1)}, u32[]{:S(2)}, u32[]{:S(2)}) %all-to-all-start.1) | async-done | bytes 4718624 | tf_op jit(solution)/shard_map/all_to_all | solution.py:150
  304.6 5.6 multiply_convert_fusion
  310.3 7.3 %convert_element_type.128 = bf16[1152,2048]{1,0:T(8,128)(2,1)} reshape(bf16[32,36,2048]{2,1,0:T(8,128)(2,1)} %multiply_convert_fusion) | data formatting | bytes 9437184 | tf_op jit(solution)/shard_map/convert_element_type | solution.py:72
  317.6 9.1 %fusion.9 = (bf16[1152,768]{1,0:T(8,128)(2,1)S(1)}, f32[1152,768]{1,0:T(8,128)}) fusion(bf16[1,1152,768]{2,1,0:T(8,128)(2,1)} %param.14, bf16[1,1152,768]{2,1,0:T(8,128)(2,1)} %param.13, bf16[1152,2048]{1,0:T(8,128)(2,1)} %convert_element_type.128, bf16[1,768,2048]{2,1,0:T(8,128)(2,1)S(1)} %copy-done), kind=kOutput, calls=%fused_computation.22 | convolution fusion | flops 3634495488 | bytes 16711680 | tf_op jit(solution)/shard_map/dot_general | solution.py:75
  330.6 8.1 %add_convert_fusion = bf16[1152,2048]{1,0:T(8,128)(2,1)} fusion(f32[1152,2048]{1,0:T(8,128)S(1)} %fusion.21, bf16[1,2048,768]{2,1,0:T(8,128)(2,1)S(1)} %copy-done.8, f32[1152,768]{1,0:T(8,128)} %get-tuple-element.10, bf16[1,1152,768]{2,1,0:T(8,128)(2,1)S(1)} %copy-done.10), kind=kOutput, calls=%fused_computation.2 | convolution fusion | flops 3634790400 | bytes 22609920 | tf_op jit(solution)/shard_map/dot_general | solution.py:86
  338.7 7.2 %reshape.151 = bf16[32,36,2048]{2,1,0:T(8,128)(2,1)} reshape(bf16[1152,2048]{1,0:T(8,128)(2,1)} %add_convert_fusion) | data formatting | bytes 9437184 | tf_op jit(solution)/shard_map/reshape | solution.py:164
  345.9 76.1 %all-to-all-done.4 = bf16[32,36,2048]{2,1,0:T(8,128)(2,1)} async-done(((bf16[32,36,2048]{2,1,0:T(8,128)(2,1)}), bf16[32,36,2048]{2,1,0:T(8,128)(2,1)}, u32[]{:S(2)}, u32[]{:S(2)}) %all-to-all-start.4) | async-done | bytes 4718624 | tf_op jit(solution)/shard_map/all_to_all | solution.py:149
  426.8 7.3 %reshape.156 = bf16[1152,2048]{1,0:T(8,128)(2,1)} reshape(bf16[32,36,2048]{2,1,0:T(8,128)(2,1)} %all-to-all-done.4) | data formatting | bytes 9437184 | tf_op jit(solution)/shard_map/reshape | solution.py:155
  434.0 150.4 %all-reduce.2.cloned.1.call-done = f32[2048,32]{0,1:T(8,128)} async-done(((f32[2048,32]{0,1:T(8,128)}), f32[2048,32]{0,1:T(8,128)}) %all-reduce.2.cloned.1.call-update) | async-done | bytes 262160 | tf_op jit(solution)/shard_map/psum | solution.py:182
  586.1 9.1 %fusion.26 = bf16[1,2048,768]{2,1,0:T(8,128)(2,1)} fusion(bf16[1152,2048]{1,0:T(8,128)(2,1)} %reshape.156, bf16[1152,768]{1,0:T(8,128)(2,1)} %copy-done.13), kind=kOutput, calls=%fused_computation.42 | convolution fusion | flops 3625451520 | bytes 9633792 | tf_op jit(solution)/shard_map/dot_general | solution.py:88
  595.2 8.5 %fusion.28 = bf16[1,768,2048]{2,1,0:T(8,128)(2,1)} fusion(bf16[1152,2048]{1,0:T(8,128)(2,1)} %convert_element_type.128, bf16[1,1152,768]{2,1,0:T(8,128)(2,1)S(1)} %copy-done.9, bf16[1,1152,768]{2,1,0:T(8,128)(2,1)S(1)} %copy-done.11), kind=kOutput, calls=%fused_computation.44 | convolution fusion | flops 3632529408 | bytes 11403264 | tf_op jit(solution)/shard_map/dot_general | solution.py:94
  603.7 6.3 %fusion.27 = bf16[1,2048,768]{2,1,0:T(8,128)(2,1)} fusion(bf16[1152,2048]{1,0:T(8,128)(2,1)S(1)} %copy-done.3, f32[1152,768]{1,0:T(8,128)S(1)} %copy-done.12, bf16[1,1152,768]{2,1,0:T(8,128)(2,1)S(1)} %copy-done.11), kind=kOutput, calls=%fused_computation.43 | convolution fusion | flops 3631644672 | bytes 13172736 | tf_op jit(solution)/shard_map/dot_general | solution.py:91
  609.9 7.4 %reshape.152 = bf16[1152,2048]{1,0:T(8,128)(2,1)} reshape(bf16[32,36,2048]{2,1,0:T(8,128)(2,1)} %all-to-all-done.2) | data formatting | bytes 9437184 | tf_op jit(solution)/shard_map/reshape | solution.py:178
  (71 shorter events, 32.6 us)
Async XLA Ops:
  7.2 1.9 copy-start
  24.3 7.4 %copy-start.6 = (s32[128,8]{0,1:T(8,128)S(1)}, s32[128,8]{0,1:T(8,128)}, u32[]{:S(2)}) copy-start(s32[128,8]{0,1:T(8,128)} %param.11) | copy-start | bytes 12292
  24.3 17.4 %copy-start.4 = (bf16[2048,32]{0,1:T(8,128)(2,1)S(1)}, bf16[2048,32]{0,1:T(8,128)(2,1)}, u32[]{:S(2)}) copy-start(bf16[2048,32]{0,1:T(8,128)(2,1)} %param.12) | copy-start | bytes 393220
  24.3 124.9 %all-to-all-start.3 = ((bf16[32,36,2048]{2,1,0:T(8,128)(2,1)}), bf16[32,36,2048]{2,1,0:T(8,128)(2,1)}, u32[]{:S(2)}, u32[]{:S(2)}) async-start(bf16[32,36,2048]{2,1,0:T(8,128)(2,1)} %reshape.153), calls=%async_computation.3 | async-start | bytes 10485760 | tf_op jit(solution)/shard_map/all_to_all | solution.py:168
  167.6 9.8 %all-to-all-start = ((bf16[32,1,36]{2,1,0:T(2,128)(2,1)}), bf16[32,1,36]{2,1,0:T(2,128)(2,1)S(1)}, u32[]{:S(2)}, u32[]{:S(2)}) async-start(bf16[32,1,36]{2,1,0:T(2,128)(2,1)} %all_to_all.24), calls=%async_computation | async-start | bytes 32768 | tf_op jit(solution)/shard_map/all_to_all | solution.py:151
  177.4 123.5 %all-to-all-start.1 = ((bf16[32,36,2048]{2,1,0:T(8,128)(2,1)}), bf16[32,36,2048]{2,1,0:T(8,128)(2,1)}, u32[]{:S(2)}, u32[]{:S(2)}) async-start(bf16[32,36,2048]{2,1,0:T(8,128)(2,1)} %reshape.150), calls=%async_computation.1 | async-start | bytes 10485760 | tf_op jit(solution)/shard_map/all_to_all | solution.py:150
  300.8 121.1 %all-to-all-start.4 = ((bf16[32,36,2048]{2,1,0:T(8,128)(2,1)}), bf16[32,36,2048]{2,1,0:T(8,128)(2,1)}, u32[]{:S(2)}, u32[]{:S(2)}) async-start(bf16[32,36,2048]{2,1,0:T(8,128)(2,1)} %reshape.155), calls=%async_computation.4 | async-start | bytes 10485760 | tf_op jit(solution)/shard_map/all_to_all | solution.py:149
  317.6 9.1 %copy-start.7 = (bf16[1,2048,768]{2,1,0:T(8,128)(2,1)S(1)}, bf16[1,2048,768]{2,1,0:T(8,128)(2,1)}, u32[]{:S(2)}) copy-start(bf16[1,2048,768]{2,1,0:T(8,128)(2,1)} %param.15) | copy-start | bytes 9437188
  326.6 3.9 copy-start.13
  326.6 3.9 copy-start.8
  326.6 3.9 copy-start.10
  345.9 80.0 %copy-start.2 = (bf16[128,2048]{1,0:T(8,128)(2,1)S(1)}, bf16[128,2048]{1,0:T(8,128)(2,1)}, u32[]{:S(2)}) copy-start(bf16[128,2048]{1,0:T(8,128)(2,1)} %param.9) | copy-start | bytes 1572868
  421.9 188.0 %all-to-all-start.2 = ((bf16[32,36,2048]{2,1,0:T(8,128)(2,1)}), bf16[32,36,2048]{2,1,0:T(8,128)(2,1)}, u32[]{:S(2)}, u32[]{:S(2)}) async-start(bf16[32,36,2048]{2,1,0:T(8,128)(2,1)} %reshape.151), calls=%async_computation.2 | async-start | bytes 10485760 | tf_op jit(solution)/shard_map/all_to_all | solution.py:167
  425.5 158.9 %all-reduce.2.cloned.1.call-start = ((), (), s32[]{:S(2)}) async-start(), calls=%async_computation.5 | async-start | bytes 524288 | tf_op jit(solution)/shard_map/psum | solution.py:182
  586.1 9.1 %copy-start.9 = (bf16[1,1152,768]{2,1,0:T(8,128)(2,1)S(1)}, bf16[1,1152,768]{2,1,0:T(8,128)(2,1)}, u32[]{:S(2)}) copy-start(bf16[1,1152,768]{2,1,0:T(8,128)(2,1)} %param.14) | copy-start | bytes 5308420
  586.1 9.1 %copy-start.11 = (bf16[1,1152,768]{2,1,0:T(8,128)(2,1)S(1)}, bf16[1,1152,768]{2,1,0:T(8,128)(2,1)}, u32[]{:S(2)}) copy-start(bf16[1,1152,768]{2,1,0:T(8,128)(2,1)} %param.13) | copy-start | bytes 5308420
  595.2 8.5 %copy-start.3 = (bf16[1152,2048]{1,0:T(8,128)(2,1)S(1)}, bf16[1152,2048]{1,0:T(8,128)(2,1)}, u32[]{:S(2)}) copy-start(bf16[1152,2048]{1,0:T(8,128)(2,1)} %reshape.156) | copy-start | bytes 14155780
  595.2 8.5 %copy-start.12 = (f32[1152,768]{1,0:T(8,128)S(1)}, f32[1152,768]{1,0:T(8,128)}, u32[]{:S(2)}) copy-start(f32[1152,768]{1,0:T(8,128)} %get-tuple-element.10) | copy-start | bytes 10616836
  609.9 11.8 %copy-start.1 = (bf16[1,768,2048]{2,1,0:T(8,128)(2,1)S(1)}, bf16[1,768,2048]{2,1,0:T(8,128)(2,1)}, u32[]{:S(2)}) copy-start(bf16[1,768,2048]{2,1,0:T(8,128)(2,1)} %param.17) | copy-start | bytes 9437188
  617.3 3.3 copy-start.5
Sparse Core Ops, SparseCore 0:
  432.4 151.9 all-reduce.1
where the time goes:
time: 630 us; the launch traced here: 629 us
  waiting for transfers between devices  432 us (69%)
  matrix products  73.2 us (12%)
  local copies, waits for them, and re-layouts  62.5 us (10%)
  starting transfers between devices  23.5 us (4%)
  other arithmetic  22.7 us (4%)
  between operations  14.3 us (2%)
    psum x1, waiting for transfers between devices, body(): lax.psum(router_part, ('outer', 'inner')) * (1.0 / math.sqrt(total_tokens))  150 us
    all_to_all x1, waiting for transfers between devices, body(): lax.all_to_all(grid_cot, ('outer', 'inner'), split_axis=0, concat_axis=0,...  106 us
    all_to_all x1, waiting for transfers between devices, body(): lax.all_to_all(extra, ('outer', 'inner'), split_axis=0, concat_axis=0, ti...  100 us
    all_to_all x1, waiting for transfers between devices, body(): lax.all_to_all(grid_tokens, ('outer', 'inner'), split_axis=0, concat_axis...  76.1 us
  transfers between devices with their start and end apart: 6, of which 4 were waited for; matrix products, arithmetic and copies ran while one was open for 18% of the time, Pallas kernels for 0%

commit v1 on v0

--- a/solution.py
+++ b/solution.py
@@ -162,12 +162,12 @@
         down_weight[0],
     )
     back_grad = grad_rows.reshape(experts, capacity, width)
-    extra = expert_out.reshape(experts, capacity, width)
-    back_rows, back_extra = (
+    slot_route_dot = slot_dot(cot_rows, expert_out).reshape(experts, capacity)
+    back_rows, back_dot = (
         lax.all_to_all(back_grad, ("outer", "inner"), split_axis=0, concat_axis=0, tiled=True),
-        lax.all_to_all(extra, ("outer", "inner"), split_axis=0, concat_axis=0, tiled=True),
-    )
-    route_dot = slot_dot(send_cot, back_extra.reshape(-1, width))
+        lax.all_to_all(slot_route_dot, ("outer", "inner"), split_axis=0, concat_axis=0, tiled=True),
+    )
+    route_dot = back_dot.reshape(-1)
     grad_tokens, router_part = finish_block(
         tokens,
         router_weight,

time: 630 us -> 520 us (0.83)
  waiting for transfers between devices: 432 us -> 322 us
  local copies, waits for them, and re-layouts: 62.5 us -> 55.3 us
  matrix products: 73.2 us -> 79.9 us
    all_to_all x1, waiting for transfers between devices: 100 us -> 6.87 us  [body(): lax.all_to_all(slot_route_dot, ('outer', 'inner'), split_axis=0, concat_a...]
    psum x1, waiting for transfers between devices: 150 us -> 126 us  [body(): lax.psum(router_part, ('outer', 'inner')) * (1.0 / math.sqrt(total_tokens))]
    all_to_all x1, waiting for transfers between devices: 106 us -> 116 us  [body(): lax.all_to_all(grid_cot, ('outer', 'inner'), split_axis=0, concat_axis=0,...]
    reshape x3 -> x1, local copies, waits for them, and re-layouts: 7.34 us -> 0.12 us  [body(): route_dot = back_dot.reshape(-1)]
where the time goes in v1:
time: 520 us; the launch traced here: 518 us
  waiting for transfers between devices  322 us (62%)
  matrix products  79.9 us (15%)
  local copies, waits for them, and re-layouts  55.3 us (11%)
  other arithmetic  23.5 us (5%)
  starting transfers between devices  22.7 us (4%)
  between operations  14.3 us (3%)
    psum x1, waiting for transfers between devices, body(): lax.psum(router_part, ('outer', 'inner')) * (1.0 / math.sqrt(total_tokens))  126 us
    all_to_all x1, waiting for transfers between devices, body(): lax.all_to_all(grid_cot, ('outer', 'inner'), split_axis=0, concat_axis=0,...  116 us
    all_to_all x1, waiting for transfers between devices, body(): lax.all_to_all(grid_tokens, ('outer', 'inner'), split_axis=0, concat_axis...  73.2 us
  transfers between devices with their start and end apart: 6, of which 4 were waited for; matrix products, arithmetic and copies ran while one was open for 18% of the time, Pallas kernels for 0%

profile of v1, /device:TPU:0, one launch (start us, length us, event | category | flops | bytes accessed | tf_op | source)
XLA Modules:
  0.0 518.3 jit_solution(971619976645461815)
XLA Ops:
  8.3 9.0 %reduce-window.6 = s32[32,8,128]{2,1,0:T(8,128)S(1)} reduce-window(s32[32,8,128]{2,1,0:T(8,128)S(1)} %fusion.43, s32[]{:T(128)} %constant.5.clone.1), window={size=1x1x128 pad=0_0x0_0x127_0}, to_apply=%region_0.1 | reduce-window | flops 4161536 | bytes 262148 | tf_op jit(solution)/shard_map/reduce-window
  18.7 6.0 %fusion.32 = bf16[1152,128]{1,0:T(8,128)(2,1)S(1)} fusion(s32[128,8]{0,1:T(8,128)S(1)} %multiply_add_fusion.1), kind=kLoop, calls=%fused_computation.49 | loop fusion | flops 3391488 | bytes 299008 | tf_op jit(solution)/shard_map/reduce_sum | solution.py:23
  29.3 7.2 %reshape.152 = bf16[32,36,2048]{2,1,0:T(8,128)(2,1)} reshape(bf16[1152,2048]{1,0:T(8,128)(2,1)} %convolution_convert_fusion.2) | data formatting | bytes 9437184 | tf_op jit(solution)/shard_map/reshape | solution.py:146
  36.5 7.4 %all-to-all-start.1 = ((bf16[32,36,2048]{2,1,0:T(8,128)(2,1)}), bf16[32,36,2048]{2,1,0:T(8,128)(2,1)}, u32[]{:S(2)}, u32[]{:S(2)}) async-start(bf16[32,36,2048]{2,1,0:T(8,128)(2,1)} %reshape.152), calls=%async_computation.1 | async-start | bytes 10485760 | tf_op jit(solution)/shard_map/all_to_all | solution.py:150
  45.3 116.1 %all-to-all-done.1 = bf16[32,36,2048]{2,1,0:T(8,128)(2,1)} async-done(((bf16[32,36,2048]{2,1,0:T(8,128)(2,1)}), bf16[32,36,2048]{2,1,0:T(8,128)(2,1)}, u32[]{:S(2)}, u32[]{:S(2)}) %all-to-all-start.1) | async-done | bytes 4718624 | tf_op jit(solution)/shard_map/all_to_all | solution.py:150
  161.4 8.0 %reshape.161 = f32[1152,2048]{1,0:T(8,128)} reshape(bf16[32,36,2048]{2,1,0:T(8,128)(2,1)} %all-to-all-done.1) | data formatting | bytes 14155776 | tf_op jit(solution)/shard_map/convert_element_type | solution.py:72
  169.5 9.9 %multiply_reduce_fusion = bf16[1152]{0:T(1024)(128)(2,1)S(1)} fusion(f32[1152,2048]{1,0:T(8,128)} %reshape.161, bf16[1,768,2048]{2,1,0:T(8,128)(2,1)} %param.17, bf16[1,1152,768]{2,1,0:T(8,128)(2,1)} %param.14, bf16[1,1152,768]{2,1,0:T(8,128)(2,1)} %param.13), kind=kOutput, calls=%fused_computation.1 | convolution fusion | flops 3640392704 | bytes 16124160 | tf_op jit(solution)/shard_map/dot_general | solution.py:69
  182.9 6.9 %all-to-all-done.3 = bf16[32,1,36]{2,1,0:T(2,128)(2,1)S(1)} async-done(((bf16[32,1,36]{2,1,0:T(2,128)(2,1)}), bf16[32,1,36]{2,1,0:T(2,128)(2,1)S(1)}, u32[]{:S(2)}, u32[]{:S(2)}) %all-to-all-start.3) | async-done | bytes 2336 | tf_op jit(solution)/shard_map/all_to_all | solution.py:168
  189.9 5.9 %fusion.6 = f32[1,128,8]{2,0,1:T(1,128)S(1)} fusion(bf16[1152,1,1]{0,1,2:T(2,128)(2,1)S(1)} %reshape.164, s32[1024]{0:T(1024)S(1)} %multiply_add_fusion), kind=kOutput, calls=%fused_computation.18 | convolution fusion | flops 3538944 | bytes 10496 | tf_op jit(solution)/shard_map/dot_general | solution.py:106
  204.9 7.2 %reshape.156 = bf16[32,36,2048]{2,1,0:T(8,128)(2,1)} reshape(bf16[1152,2048]{1,0:T(8,128)(2,1)} %convolution_convert_fusion.1) | data formatting | bytes 9437184 | tf_op jit(solution)/shard_map/reshape | solution.py:145
  212.1 6.2 %all-to-all-start.4 = ((bf16[32,36,2048]{2,1,0:T(8,128)(2,1)}), bf16[32,36,2048]{2,1,0:T(8,128)(2,1)}, u32[]{:S(2)}, u32[]{:S(2)}) async-start(bf16[32,36,2048]{2,1,0:T(8,128)(2,1)} %reshape.156), calls=%async_computation.4 | async-start | bytes 10485760 | tf_op jit(solution)/shard_map/all_to_all | solution.py:149
  218.3 5.7 %multiply_convert_fusion = bf16[32,36,2048]{2,1,0:T(8,128)(2,1)} fusion(f32[32,36]{1,0:T(8,128)S(1)} %bitcast.118, bf16[32,36,2048]{2,1,0:T(8,128)(2,1)} %all-to-all-done.1), kind=kLoop, calls=%fused_computation | loop fusion | flops 7077888 | bytes 9441792 | tf_op jit(solution)/shard_map/convert_element_type | solution.py:72
  224.0 7.2 %convert_element_type.139 = bf16[1152,2048]{1,0:T(8,128)(2,1)} reshape(bf16[32,36,2048]{2,1,0:T(8,128)(2,1)} %multiply_convert_fusion) | data formatting | bytes 9437184 | tf_op jit(solution)/shard_map/convert_element_type | solution.py:72
  231.3 9.1 %fusion.11 = (bf16[1152,768]{1,0:T(8,128)(2,1)S(1)}, f32[1152,768]{1,0:T(8,128)S(1)}) fusion(bf16[1,1152,768]{2,1,0:T(8,128)(2,1)} %param.14, bf16[1,1152,768]{2,1,0:T(8,128)(2,1)} %param.13, bf16[1152,2048]{1,0:T(8,128)(2,1)} %convert_element_type.139, bf16[1,768,2048]{2,1,0:T(8,128)(2,1)} %param.17), kind=kOutput, calls=%fused_computation.24 | convolution fusion | flops 3634495488 | bytes 16711680 | tf_op jit(solution)/shard_map/dot_general | solution.py:75
  240.5 6.3 %fusion.23 = f32[1152,2048]{1,0:T(8,128)} fusion(bf16[1152,768]{1,0:T(8,128)(2,1)S(1)} %get-tuple-element.7, bf16[1,2048,768]{2,1,0:T(8,128)(2,1)S(1)} %copy-done), kind=kOutput, calls=%fused_computation.39 | convolution fusion | flops 3623878656 | bytes 14352384 | tf_op jit(solution)/shard_map/dot_general | solution.py:83
  246.8 8.3 %add_convert_fusion = bf16[1152,2048]{1,0:T(8,128)(2,1)} fusion(f32[1152,2048]{1,0:T(8,128)} %fusion.23, bf16[1,2048,768]{2,1,0:T(8,128)(2,1)S(1)} %copy-done.5, f32[1152,768]{1,0:T(8,128)S(1)} %get-tuple-element.8, bf16[1,1152,768]{2,1,0:T(8,128)(2,1)S(1)} %copy-done.7), kind=kOutput, calls=%fused_computation.2 | convolution fusion | flops 3634790400 | bytes 22609920 | tf_op jit(solution)/shard_map/dot_general | solution.py:86
  255.1 7.2 %reshape.153 = bf16[32,36,2048]{2,1,0:T(8,128)(2,1)} reshape(bf16[1152,2048]{1,0:T(8,128)(2,1)} %add_convert_fusion) | data formatting | bytes 9437184 | tf_op jit(solution)/shard_map/reshape | solution.py:164
  262.4 73.2 %all-to-all-done.4 = bf16[32,36,2048]{2,1,0:T(8,128)(2,1)} async-done(((bf16[32,36,2048]{2,1,0:T(8,128)(2,1)}), bf16[32,36,2048]{2,1,0:T(8,128)(2,1)}, u32[]{:S(2)}, u32[]{:S(2)}) %all-to-all-start.4) | async-done | bytes 4718624 | tf_op jit(solution)/shard_map/all_to_all | solution.py:149
  339.5 7.4 %reshape.157 = bf16[1152,2048]{1,0:T(8,128)(2,1)} reshape(bf16[32,36,2048]{2,1,0:T(8,128)(2,1)} %all-to-all-done.4) | data formatting | bytes 9437184 | tf_op jit(solution)/shard_map/reshape | solution.py:155
  348.0 9.2 %fusion.30 = bf16[1,768,2048]{2,1,0:T(8,128)(2,1)} fusion(bf16[1152,2048]{1,0:T(8,128)(2,1)} %convert_element_type.139, bf16[1,1152,768]{2,1,0:T(8,128)(2,1)S(1)} %copy-done.6, bf16[1,1152,768]{2,1,0:T(8,128)(2,1)} %param.13), kind=kOutput, calls=%fused_computation.46 | convolution fusion | flops 3632529408 | bytes 11403264 | tf_op jit(solution)/shard_map/dot_general | solution.py:94
  357.2 8.6 %fusion.29 = bf16[1,2048,768]{2,1,0:T(8,128)(2,1)} fusion(bf16[1152,2048]{1,0:T(8,128)(2,1)} %reshape.157, f32[1152,768]{1,0:T(8,128)S(1)} %copy-done.10, bf16[1,1152,768]{2,1,0:T(8,128)(2,1)S(1)} %copy-done.8), kind=kOutput, calls=%fused_computation.45 | convolution fusion | flops 3631644672 | bytes 13172736 | tf_op jit(solution)/shard_map/dot_general | solution.py:91
  365.8 5.9 %fusion.28 = bf16[1,2048,768]{2,1,0:T(8,128)(2,1)} fusion(bf16[1152,2048]{1,0:T(8,128)(2,1)S(1)} %bitcast.116, bf16[1152,768]{1,0:T(8,128)(2,1)S(1)} %copy-done.12), kind=kOutput, calls=%fused_computation.44 | convolution fusion | flops 3625451520 | bytes 9633792 | tf_op jit(solution)/shard_map/dot_general | solution.py:88
  371.7 126.3 %all-reduce.2.cloned.1.call-done = f32[2048,32]{0,1:T(8,128)} async-done(((f32[2048,32]{0,1:T(8,128)}), f32[2048,32]{0,1:T(8,128)}) %all-reduce.2.cloned.1.call-update) | async-done | bytes 262160 | tf_op jit(solution)/shard_map/psum | solution.py:182
  499.7 7.4 %reshape.154 = bf16[1152,2048]{1,0:T(8,128)(2,1)} reshape(bf16[32,36,2048]{2,1,0:T(8,128)(2,1)} %all-to-all-done.2) | data formatting | bytes 9437184 | tf_op jit(solution)/shard_map/reshape | solution.py:178
  (74 shorter events, 32.1 us)
Async XLA Ops:
  7.2 233.3 %copy-start = (bf16[1,2048,768]{2,1,0:T(8,128)(2,1)S(1)}, bf16[1,2048,768]{2,1,0:T(8,128)(2,1)}, u32[]{:S(2)}) copy-start(bf16[1,2048,768]{2,1,0:T(8,128)(2,1)} %param.15) | copy-start | bytes 9437188
  36.5 8.8 %copy-start.4 = (s32[128,8]{0,1:T(8,128)S(1)}, s32[128,8]{0,1:T(8,128)}, u32[]{:S(2)}) copy-start(s32[128,8]{0,1:T(8,128)} %param.11) | copy-start | bytes 12292
  36.5 124.9 %all-to-all-start.1 = ((bf16[32,36,2048]{2,1,0:T(8,128)(2,1)}), bf16[32,36,2048]{2,1,0:T(8,128)(2,1)}, u32[]{:S(2)}, u32[]{:S(2)}) async-start(bf16[32,36,2048]{2,1,0:T(8,128)(2,1)} %reshape.152), calls=%async_computation.1 | async-start | bytes 10485760 | tf_op jit(solution)/shard_map/all_to_all | solution.py:150
  180.1 9.6 %all-to-all-start.3 = ((bf16[32,1,36]{2,1,0:T(2,128)(2,1)}), bf16[32,1,36]{2,1,0:T(2,128)(2,1)S(1)}, u32[]{:S(2)}, u32[]{:S(2)}) async-start(bf16[32,1,36]{2,1,0:T(2,128)(2,1)} %convert_element_type.167), calls=%async_computation.3 | async-start | bytes 32768 | tf_op jit(solution)/shard_map/all_to_all | solution.py:168
  197.8 14.3 %all-to-all-start = ((bf16[32,1,36]{2,1,0:T(2,128)(2,1)}), bf16[32,1,36]{2,1,0:T(2,128)(2,1)S(1)}, u32[]{:S(2)}, u32[]{:S(2)}) async-start(bf16[32,1,36]{2,1,0:T(2,128)(2,1)} %all_to_all.25), calls=%async_computation | async-start | bytes 32768 | tf_op jit(solution)/shard_map/all_to_all | solution.py:151
  212.1 123.5 %all-to-all-start.4 = ((bf16[32,36,2048]{2,1,0:T(8,128)(2,1)}), bf16[32,36,2048]{2,1,0:T(8,128)(2,1)}, u32[]{:S(2)}, u32[]{:S(2)}) async-start(bf16[32,36,2048]{2,1,0:T(8,128)(2,1)} %reshape.156), calls=%async_computation.4 | async-start | bytes 10485760 | tf_op jit(solution)/shard_map/all_to_all | solution.py:149
  240.4 6.3 %copy-start.11 = (bf16[1152,768]{1,0:T(8,128)(2,1)}, bf16[1152,768]{1,0:T(8,128)(2,1)S(1)}, u32[]{:S(2)}) copy-start(bf16[1152,768]{1,0:T(8,128)(2,1)S(1)} %get-tuple-element.7) | copy-start | bytes 5308420
  240.4 6.4 %copy-start.9 = (f32[1152,768]{1,0:T(8,128)}, f32[1152,768]{1,0:T(8,128)S(1)}, u32[]{:S(2)}) copy-start(f32[1152,768]{1,0:T(8,128)S(1)} %get-tuple-element.8) | copy-start | bytes 10616836
  240.4 6.4 %copy-start.5 = (bf16[1,2048,768]{2,1,0:T(8,128)(2,1)S(1)}, bf16[1,2048,768]{2,1,0:T(8,128)(2,1)}, u32[]{:S(2)}) copy-start(bf16[1,2048,768]{2,1,0:T(8,128)(2,1)} %param.16) | copy-start | bytes 9437188
  240.5 6.4 %copy-start.7 = (bf16[1,1152,768]{2,1,0:T(8,128)(2,1)S(1)}, bf16[1,1152,768]{2,1,0:T(8,128)(2,1)}, u32[]{:S(2)}) copy-start(bf16[1,1152,768]{2,1,0:T(8,128)(2,1)} %param.13) | copy-start | bytes 5308420
  335.6 164.1 %all-to-all-start.2 = ((bf16[32,36,2048]{2,1,0:T(8,128)(2,1)}), bf16[32,36,2048]{2,1,0:T(8,128)(2,1)}, u32[]{:S(2)}, u32[]{:S(2)}) async-start(bf16[32,36,2048]{2,1,0:T(8,128)(2,1)} %reshape.153), calls=%async_computation.2 | async-start | bytes 10485760 | tf_op jit(solution)/shard_map/all_to_all | solution.py:167
  339.2 7.8 %copy-start.2 = (bf16[128,2048]{1,0:T(8,128)(2,1)S(1)}, bf16[128,2048]{1,0:T(8,128)(2,1)}, u32[]{:S(2)}) copy-start(bf16[128,2048]{1,0:T(8,128)(2,1)} %param.9) | copy-start | bytes 1572868
  339.2 8.7 %copy-start.6 = (bf16[1,1152,768]{2,1,0:T(8,128)(2,1)S(1)}, bf16[1,1152,768]{2,1,0:T(8,128)(2,1)}, u32[]{:S(2)}) copy-start(bf16[1,1152,768]{2,1,0:T(8,128)(2,1)} %param.14) | copy-start | bytes 5308420
  339.2 158.8 %all-reduce.2.cloned.1.call-start = ((), (), s32[]{:S(2)}) async-start(), calls=%async_computation.5 | async-start | bytes 524288 | tf_op jit(solution)/shard_map/psum | solution.py:182
  347.9 9.2 %copy-start.8 = (bf16[1,1152,768]{2,1,0:T(8,128)(2,1)S(1)}, bf16[1,1152,768]{2,1,0:T(8,128)(2,1)}, u32[]{:S(2)}) copy-start(bf16[1,1152,768]{2,1,0:T(8,128)(2,1)} %param.13) | copy-start | bytes 5308420
  347.9 9.2 %copy-start.10 = (f32[1152,768]{1,0:T(8,128)S(1)}, f32[1152,768]{1,0:T(8,128)}, u32[]{:S(2)}) copy-start(f32[1152,768]{1,0:T(8,128)} %copy-done.9) | copy-start | bytes 10616836
  347.9 17.9 %slice-start = ((s8[4718592]{0:T(1024)(128)(4,1)}), s8[4194304]{0:T(1024)(128)(4,1)S(1)}, s32[]{:S(2)}) async-start(s8[4718592]{0:T(1024)(128)(4,1)} %bitcast.115), calls=%async_computation.6 | async-start | bytes 8388608
  357.2 8.7 %slice-start.1 = ((s8[4718592]{0:T(1024)(128)(4,1)}), s8[524288]{0:T(1024)(128)(4,1)S(1)}, s32[]{:S(2)}) async-start(s8[4718592]{0:T(1024)(128)(4,1)} %bitcast.115), calls=%async_computation.7 | async-start | bytes 1048576
  357.2 8.7 %copy-start.12 = (bf16[1152,768]{1,0:T(8,128)(2,1)S(1)}, bf16[1152,768]{1,0:T(8,128)(2,1)}, u32[]{:S(2)}) copy-start(bf16[1152,768]{1,0:T(8,128)(2,1)} %copy-done.11) | copy-start | bytes 5308420
  499.7 11.8 %copy-start.1 = (bf16[1,2048,768]{2,1,0:T(8,128)(2,1)S(1)}, bf16[1,2048,768]{2,1,0:T(8,128)(2,1)}, u32[]{:S(2)}) copy-start(bf16[1,2048,768]{2,1,0:T(8,128)(2,1)} %param.15) | copy-start | bytes 9437188
  507.0 3.3 copy-start.3
Sparse Core Ops, SparseCore 0:
  348.0 149.8 all-reduce.1

commit v2 on v1

--- a/solution.py
+++ b/solution.py
@@ -14,7 +14,13 @@
     onehot = (flat_routes[:, None] == jnp.arange(experts, dtype=jnp.int32)[None, :]).astype(
         jnp.int32
     )
-    earlier = jnp.cumsum(onehot, axis=0) - onehot
+    pairs = flat_routes.shape[0]
+    lower = (
+        jnp.arange(pairs, dtype=jnp.int32)[:, None] > jnp.arange(pairs, dtype=jnp.int32)[None, :]
+    ).astype(jnp.bfloat16)
+    earlier = jnp.dot(
+        lower, onehot.astype(jnp.bfloat16), preferred_element_type=jnp.float32
+    ).astype(jnp.int32)
     position = jnp.sum(earlier * onehot, axis=1)
     target = flat_routes * capacity + position
     slot_table = (
@@ -139,20 +145,25 @@
     capacity = gate_saved.shape[1] // experts
     outer_size = lax.axis_size("outer")
     inner_size = lax.axis_size("inner")
-    picked, probs, slot_table, token_table, send_tokens, send_cot, send_weight = dispatch_block(
-        tokens, cotangent, routes, router_weight, capacity
-    )
-    grid_tokens = send_tokens.reshape(experts, capacity, width)
-    grid_cot = send_cot.reshape(experts, capacity, width)
+    axes = ("outer", "inner")
+    picked, probs = route_probs(tokens, routes, router_weight)
+    slot_table, token_table = route_tables(routes, experts, capacity)
+    both = jnp.concatenate([tokens, cotangent], axis=1)
+    grid_both = jnp.dot(
+        token_table.reshape(experts, capacity, -1), both, preferred_element_type=jnp.float32
+    ).astype(jnp.bfloat16)
+    probs_low = probs.astype(jnp.bfloat16).reshape(-1)
+    send_weight = jnp.dot(slot_table, probs_low, preferred_element_type=jnp.float32).astype(
+        jnp.bfloat16
+    )
     grid_weight = send_weight.reshape(experts, capacity)
-    got_tokens, got_cot, got_weight = (
-        lax.all_to_all(grid_tokens, ("outer", "inner"), split_axis=0, concat_axis=0, tiled=True),
-        lax.all_to_all(grid_cot, ("outer", "inner"), split_axis=0, concat_axis=0, tiled=True),
-        lax.all_to_all(grid_weight, ("outer", "inner"), split_axis=0, concat_axis=0, tiled=True),
-    )
-    cot_rows = got_cot.reshape(-1, width)
+    got_both = lax.all_to_all(grid_both, axes, split_axis=0, concat_axis=0, tiled=True)
+    got_weight = lax.all_to_all(grid_weight, axes, split_axis=0, concat_axis=0, tiled=True)
+    got_both = got_both.reshape(-1, 2 * width)
+    input_rows = got_both[:, :width]
+    cot_rows = got_both[:, width:]
     grad_rows, expert_out, grad_gate_w, grad_up_w, grad_down_w = expert_backward(
-        got_tokens.reshape(-1, width),
+        input_rows,
         cot_rows,
         got_weight.reshape(-1),
         gate_saved[0],
@@ -161,25 +172,34 @@
         up_weight[0],
         down_weight[0],
     )
+    slot_route_dot = slot_dot(cot_rows, expert_out).reshape(experts, capacity)
+    back_dot = lax.all_to_all(slot_route_dot, axes, split_axis=0, concat_axis=0, tiled=True)
+    route_dot = back_dot.reshape(-1)
+    route_grad = lax.dot_general(
+        slot_table, route_dot, contract_rows, preferred_element_type=jnp.float32
+    ).reshape(probs.shape)
+    inner_term = jnp.sum(probs * route_grad, axis=1, keepdims=True)
+    chosen_grad = probs * (route_grad - inner_term)
+    logit_grad = jnp.sum(
+        jnp.where(picked, chosen_grad[:, :, None], jnp.float32(0.0)), axis=1
+    ).astype(jnp.bfloat16)
+    router_part = lax.dot_general(
+        tokens, logit_grad, contract_rows, preferred_element_type=jnp.float32
+    )
+    total_tokens = tokens.shape[0] * outer_size * inner_size
+    grad_router = lax.psum(router_part, axes) * (1.0 / math.sqrt(total_tokens))
     back_grad = grad_rows.reshape(experts, capacity, width)
-    slot_route_dot = slot_dot(cot_rows, expert_out).reshape(experts, capacity)
-    back_rows, back_dot = (
-        lax.all_to_all(back_grad, ("outer", "inner"), split_axis=0, concat_axis=0, tiled=True),
-        lax.all_to_all(slot_route_dot, ("outer", "inner"), split_axis=0, concat_axis=0, tiled=True),
-    )
-    route_dot = back_dot.reshape(-1)
-    grad_tokens, router_part = finish_block(
-        tokens,
-        router_weight,
-        picked,
-        probs,
-        slot_table,
-        token_table,
-        back_rows.reshape(-1, width),
-        route_dot,
-    )
-    total_tokens = tokens.shape[0] * outer_size * inner_size
-    grad_router = lax.psum(router_part, ("outer", "inner")) * (1.0 / math.sqrt(total_tokens))
+    grad_router, back_grad = lax.optimization_barrier((grad_router, back_grad))
+    back_rows = lax.all_to_all(back_grad, axes, split_axis=0, concat_axis=0, tiled=True)
+    grad_sum = lax.dot_general(
+        token_table, back_rows.reshape(-1, width), contract_rows, preferred_element_type=jnp.float32
+    )
+    grad_tokens = (
+        grad_sum
+        + lax.dot_general(
+            logit_grad, router_weight, contract_cols, preferred_element_type=jnp.float32
+        )
+    ).astype(jnp.bfloat16)
     return (grad_tokens, grad_gate_w[None], grad_up_w[None], grad_down_w[None], grad_router)
 
 

time: 520 us -> 580 us (1.12)
  waiting for transfers between devices: 322 us -> 428 us
  local copies, waits for them, and re-layouts: 55.3 us -> 31.9 us
  other arithmetic: 23.5 us -> 8.64 us
  starting transfers between devices: 22.7 us -> 16.7 us
    all_to_all x5 -> x4, waiting for transfers between devices: 196 us -> 333 us  [the longest x1 228 us: body(): lax.all_to_all(grid_both, axes, split_axis=0, concat_axis=0, tiled=True)]
    psum x1, waiting for transfers between devices: 126 us -> 94.8 us  [body(): grad_router = lax.psum(router_part, axes) * (1.0 / math.sqrt(total_tokens))]
    convert_element_type x4 -> x3, local copies, waits for them, and re-layouts: 15.5 us -> 0.33 us  [the longest x2 0.23 us: body(): probs_low = probs.astype(jnp.bfloat16).reshape(-1)]
    another operation x3 -> x0, other arithmetic: 9.15 us -> none
    reshape x3 -> x2, local copies, waits for them, and re-layouts: 21.9 us -> 14 us  [the longest x1 13.2 us: body(): got_both = got_both.reshape(-1, 2 * width)]
    all_to_all x5 -> x4, starting transfers between devices: 22.4 us -> 16.6 us  [the longest x1 7.4 us: body(): lax.all_to_all(grid_both, axes, split_axis=0, concat_axis=0, tiled=True)]
  transfers between devices with their start and end apart: 6 -> 5, of which waited for: 4 -> 5; matrix products, arithmetic and copies ran while one was open for 18% -> 10% of each run, Pallas kernels for 0% -> 0%
where the time goes in v2:
time: 580 us; the launch traced here: 579 us
  waiting for transfers between devices  428 us (74%)
  matrix products  79.9 us (14%)
  local copies, waits for them, and re-layouts  31.9 us (6%)
  starting transfers between devices  16.7 us (3%)
  between operations  14.3 us (2%)
  other arithmetic  8.64 us (1%)
    all_to_all x1, waiting for transfers between devices, body(): lax.all_to_all(grid_both, axes, split_axis=0, concat_axis=0, tiled=True)  228 us
    psum x1, waiting for transfers between devices, body(): grad_router = lax.psum(router_part, axes) * (1.0 / math.sqrt(total_tokens))  94.8 us
    all_to_all x1, waiting for transfers between devices, body(): lax.all_to_all(back_grad, axes, split_axis=0, concat_axis=0, tiled=True)  92.7 us
    reshape x1, local copies, waits for them, and re-layouts, body(): got_both = got_both.reshape(-1, 2 * width)  13.2 us
  transfers between devices with their start and end apart: 5, of which 5 were waited for; matrix products, arithmetic and copies ran while one was open for 10% of the time, Pallas kernels for 0%

profile of v2, /device:TPU:0, one launch (start us, length us, event | category | flops | bytes accessed | tf_op | source)
XLA Modules:
  0.0 579.3 jit_solution(17009639620150459499)
XLA Ops:
  9.6 6.0 %fusion.51 = bf16[1152,128]{1,0:T(8,128)(2,1)S(1)} fusion(s32[128,8]{0,1:T(8,128)S(1)} %multiply_add_fusion.1), kind=kLoop, calls=%fused_computation.57 | loop fusion | flops 3391488 | bytes 299008 | tf_op jit(solution)/shard_map/reduce_sum | solution.py:29
  16.4 8.0 %convolution_convert_fusion = bf16[32,36,4096]{2,1,0:T(8,128)(2,1)} fusion(bf16[32,36,128]{2,1,0:T(8,128)(2,1)} %reshape.116, bf16[128,2048]{1,0:T(8,128)(2,1)} %param.10, bf16[128,2048]{1,0:T(8,128)(2,1)} %param.9), kind=kOutput, calls=%fused_computation.5 | convolution fusion | flops 1214775296 | bytes 10780672 | tf_op jit(solution)/shard_map/dot_general | solution.py:152
  24.4 7.4 %all-to-all-start = ((bf16[32,36,4096]{2,1,0:T(8,128)(2,1)}), bf16[32,36,4096]{2,1,0:T(8,128)(2,1)}, u32[]{:S(2)}, u32[]{:S(2)}) async-start(bf16[32,36,4096]{2,1,0:T(8,128)(2,1)} %convolution_convert_fusion), calls=%async_computation | async-start | bytes 20971520 | tf_op jit(solution)/shard_map/all_to_all | solution.py:160
  33.3 228.5 %all-to-all-done = bf16[32,36,4096]{2,1,0:T(8,128)(2,1)} async-done(((bf16[32,36,4096]{2,1,0:T(8,128)(2,1)}), bf16[32,36,4096]{2,1,0:T(8,128)(2,1)}, u32[]{:S(2)}, u32[]{:S(2)}) %all-to-all-start) | async-done | bytes 9437216 | tf_op jit(solution)/shard_map/all_to_all | solution.py:160
  261.7 13.2 %reshape.117 = bf16[1152,4096]{1,0:T(8,128)(2,1)} reshape(bf16[32,36,4096]{2,1,0:T(8,128)(2,1)} %all-to-all-done) | data formatting | bytes 18874368 | tf_op jit(solution)/shard_map/reshape | solution.py:162
  274.9 8.6 %fusion = bf16[1152]{0:T(1024)(128)(2,1)S(1)} fusion(bf16[1152,4096]{1,0:T(8,128)(2,1)} %reshape.117, bf16[1,768,2048]{2,1,0:T(8,128)(2,1)} %param.17, bf16[1,1152,768]{2,1,0:T(8,128)(2,1)} %param.14, bf16[1,1152,768]{2,1,0:T(8,128)(2,1)} %param.13), kind=kOutput, calls=%fused_computation.2 | convolution fusion | flops 3642752000 | bytes 11405568 | tf_op jit(solution)/shard_map/dot_general | solution.py:75
  284.3 2.7 all-to-all-start.1
  287.1 6.9 %all-to-all-done.1 = bf16[32,1,36]{2,1,0:T(2,128)(2,1)S(1)} async-done(((bf16[32,1,36]{2,1,0:T(2,128)(2,1)}), bf16[32,1,36]{2,1,0:T(2,128)(2,1)S(1)}, u32[]{:S(2)}, u32[]{:S(2)}) %all-to-all-start.1) | async-done | bytes 2336 | tf_op jit(solution)/shard_map/all_to_all | solution.py:176
  294.1 5.9 %fusion.8 = f32[1,128,8]{2,0,1:T(1,128)S(1)} fusion(bf16[1152,1,1]{0,1,2:T(2,128)(2,1)S(1)} %reshape.125, s32[1024]{0:T(1024)S(1)} %multiply_add_fusion), kind=kOutput, calls=%fused_computation.19 | convolution fusion | flops 3538944 | bytes 10496 | tf_op jit(solution)/shard_map/dot_general | solution.py:178
  302.0 2.5 all-to-all-start.2
  304.6 2.0 convolution_bitcast_fusion
  306.6 5.0 all-to-all-done.2
  311.8 9.1 %fusion.19 = (bf16[1152,768]{1,0:T(8,128)(2,1)S(1)}, f32[1152,768]{1,0:T(8,128)S(1)}) fusion(bf16[1,1152,768]{2,1,0:T(8,128)(2,1)} %param.14, bf16[1,1152,768]{2,1,0:T(8,128)(2,1)} %param.13, bf16[1,768,2048]{2,1,0:T(8,128)(2,1)} %param.17, f32[1152]{0:T(1024)S(1)} %reshape.121, bf16[1152,4096]{1,0:T(8,128)(2,1)} %reshape.117), kind=kOutput, calls=%fused_computation.32 | convolution fusion | flops 3641573376 | bytes 16716288 | tf_op jit(solution)/shard_map/dot_general | solution.py:81
  321.0 6.3 %fusion.36 = f32[1152,2048]{1,0:T(8,128)} fusion(bf16[1152,768]{1,0:T(8,128)(2,1)S(1)} %get-tuple-element.11, bf16[1,2048,768]{2,1,0:T(8,128)(2,1)S(1)} %copy-done), kind=kOutput, calls=%fused_computation.47 | convolution fusion | flops 3623878656 | bytes 14352384 | tf_op jit(solution)/shard_map/dot_general | solution.py:89
  327.4 8.4 %add_convert_fusion = bf16[1152,2048]{1,0:T(8,128)(2,1)} fusion(f32[1152,2048]{1,0:T(8,128)} %fusion.36, bf16[1,2048,768]{2,1,0:T(8,128)(2,1)S(1)} %copy-done.4, f32[1152,768]{1,0:T(8,128)S(1)} %get-tuple-element.12, bf16[1,1152,768]{2,1,0:T(8,128)(2,1)S(1)} %copy-done.6), kind=kOutput, calls=%fused_computation.4 | convolution fusion | flops 3634790400 | bytes 22609920 | tf_op jit(solution)/shard_map/dot_general | solution.py:92
  335.8 7.2 %reshape.119 = bf16[32,36,2048]{2,1,0:T(8,128)(2,1)} reshape(bf16[1152,2048]{1,0:T(8,128)(2,1)} %add_convert_fusion) | data formatting | bytes 9437184 | tf_op jit(solution)/shard_map/reshape | solution.py:191
  343.0 94.8 %all-reduce.2.cloned.1.call-done = f32[2048,32]{0,1:T(8,128)} async-done(((f32[2048,32]{0,1:T(8,128)}), f32[2048,32]{0,1:T(8,128)}) %all-reduce.2.cloned.1.call-update) | async-done | bytes 262160 | tf_op jit(solution)/shard_map/psum | solution.py:190
  439.4 4.0 all-to-all-start.3
  443.4 9.1 %fusion.45 = bf16[1,2048,768]{2,1,0:T(8,128)(2,1)} fusion(bf16[1152,768]{1,0:T(8,128)(2,1)} %copy-done.10, bf16[1152,4096]{1,0:T(8,128)(2,1)} %reshape.117), kind=kOutput, calls=%fused_computation.54 | convolution fusion | flops 3625451520 | bytes 9633792 | tf_op jit(solution)/shard_map/dot_general | solution.py:94
  452.5 9.1 %fusion.41 = bf16[1,768,2048]{2,1,0:T(8,128)(2,1)} fusion(bf16[1,1152,768]{2,1,0:T(8,128)(2,1)S(1)} %copy-done.5, bf16[1,1152,768]{2,1,0:T(8,128)(2,1)S(1)} %copy-done.7, f32[1152]{0:T(1024)S(1)} %reshape.121, bf16[1152,4096]{1,0:T(8,128)(2,1)} %reshape.117), kind=kOutput, calls=%fused_computation.52 | convolution fusion | flops 3639607296 | bytes 11407872 | tf_op jit(solution)/shard_map/dot_general | solution.py:100
  461.7 6.3 %fusion.42 = bf16[1,2048,768]{2,1,0:T(8,128)(2,1)} fusion(bf16[1152,4096]{1,0:T(8,128)(2,1)S(1)} %bitcast.97, f32[1152,768]{1,0:T(8,128)S(1)} %copy-done.9, bf16[1,1152,768]{2,1,0:T(8,128)(2,1)S(1)} %copy-done.7), kind=kOutput, calls=%fused_computation.53 | convolution fusion | flops 3631644672 | bytes 13172736 | tf_op jit(solution)/shard_map/dot_general | solution.py:97
  468.0 92.7 %all-to-all-done.3 = bf16[32,36,2048]{2,1,0:T(8,128)(2,1)} async-done(((bf16[32,36,2048]{2,1,0:T(8,128)(2,1)}), bf16[32,36,2048]{2,1,0:T(8,128)(2,1)}, u32[]{:S(2)}, u32[]{:S(2)}) %all-to-all-start.3) | async-done | bytes 4718624 | tf_op jit(solution)/shard_map/all_to_all | solution.py:193
  560.7 7.4 %reshape.120 = bf16[1152,2048]{1,0:T(8,128)(2,1)} reshape(bf16[32,36,2048]{2,1,0:T(8,128)(2,1)} %all-to-all-done.3) | data formatting | bytes 9437184 | tf_op jit(solution)/shard_map/reshape | solution.py:195
  568.1 3.2 fusion.76
  (57 shorter events, 10.6 us)
Async XLA Ops:
  7.2 313.8 %copy-start = (bf16[1,2048,768]{2,1,0:T(8,128)(2,1)S(1)}, bf16[1,2048,768]{2,1,0:T(8,128)(2,1)}, u32[]{:S(2)}) copy-start(bf16[1,2048,768]{2,1,0:T(8,128)(2,1)} %param.15) | copy-start | bytes 9437188
  24.4 8.8 %copy-start.3 = (s32[128,8]{0,1:T(8,128)S(1)}, s32[128,8]{0,1:T(8,128)}, u32[]{:S(2)}) copy-start(s32[128,8]{0,1:T(8,128)} %param.11) | copy-start | bytes 12292
  24.4 237.3 %all-to-all-start = ((bf16[32,36,4096]{2,1,0:T(8,128)(2,1)}), bf16[32,36,4096]{2,1,0:T(8,128)(2,1)}, u32[]{:S(2)}, u32[]{:S(2)}) async-start(bf16[32,36,4096]{2,1,0:T(8,128)(2,1)} %convolution_convert_fusion), calls=%async_computation | async-start | bytes 20971520 | tf_op jit(solution)/shard_map/all_to_all | solution.py:160
  284.3 9.6 %all-to-all-start.1 = ((bf16[32,1,36]{2,1,0:T(2,128)(2,1)}), bf16[32,1,36]{2,1,0:T(2,128)(2,1)S(1)}, u32[]{:S(2)}, u32[]{:S(2)}) async-start(bf16[32,1,36]{2,1,0:T(2,128)(2,1)} %convert_element_type.152), calls=%async_computation.1 | async-start | bytes 32768 | tf_op jit(solution)/shard_map/all_to_all | solution.py:176
  302.0 9.6 %all-to-all-start.2 = ((bf16[32,1,36]{2,1,0:T(2,128)(2,1)}), bf16[32,1,36]{2,1,0:T(2,128)(2,1)S(1)}, u32[]{:S(2)}, u32[]{:S(2)}) async-start(bf16[32,1,36]{2,1,0:T(2,128)(2,1)} %all_to_all.21), calls=%async_computation.2 | async-start | bytes 32768 | tf_op jit(solution)/shard_map/all_to_all | solution.py:161
  304.6 133.2 %all-reduce.2.cloned.1.call-start = ((), (), s32[]{:S(2)}) async-start(), calls=%async_computation.4 | async-start | bytes 524288 | tf_op jit(solution)/shard_map/psum | solution.py:190
  320.9 6.3 %copy-start.10 = (bf16[1152,768]{1,0:T(8,128)(2,1)}, bf16[1152,768]{1,0:T(8,128)(2,1)S(1)}, u32[]{:S(2)}) copy-start(bf16[1152,768]{1,0:T(8,128)(2,1)S(1)} %get-tuple-element.11) | copy-start | bytes 5308420
  320.9 6.4 %copy-start.8 = (f32[1152,768]{1,0:T(8,128)}, f32[1152,768]{1,0:T(8,128)S(1)}, u32[]{:S(2)}) copy-start(f32[1152,768]{1,0:T(8,128)S(1)} %get-tuple-element.12) | copy-start | bytes 10616836
  321.0 6.4 %copy-start.4 = (bf16[1,2048,768]{2,1,0:T(8,128)(2,1)S(1)}, bf16[1,2048,768]{2,1,0:T(8,128)(2,1)}, u32[]{:S(2)}) copy-start(bf16[1,2048,768]{2,1,0:T(8,128)(2,1)} %param.16) | copy-start | bytes 9437188
  321.0 6.4 %copy-start.6 = (bf16[1,1152,768]{2,1,0:T(8,128)(2,1)S(1)}, bf16[1,1152,768]{2,1,0:T(8,128)(2,1)}, u32[]{:S(2)}) copy-start(bf16[1,1152,768]{2,1,0:T(8,128)(2,1)} %param.13) | copy-start | bytes 5308420
  439.4 121.3 %all-to-all-start.3 = ((bf16[32,36,2048]{2,1,0:T(8,128)(2,1)}), bf16[32,36,2048]{2,1,0:T(8,128)(2,1)}, u32[]{:S(2)}, u32[]{:S(2)}) async-start(bf16[32,36,2048]{2,1,0:T(8,128)(2,1)} %reshape.119), calls=%async_computation.3 | async-start | bytes 10485760 | tf_op jit(solution)/shard_map/all_to_all | solution.py:193
  443.4 9.1 %copy-start.5 = (bf16[1,1152,768]{2,1,0:T(8,128)(2,1)S(1)}, bf16[1,1152,768]{2,1,0:T(8,128)(2,1)}, u32[]{:S(2)}) copy-start(bf16[1,1152,768]{2,1,0:T(8,128)(2,1)} %param.14) | copy-start | bytes 5308420
  443.4 9.1 %copy-start.7 = (bf16[1,1152,768]{2,1,0:T(8,128)(2,1)S(1)}, bf16[1,1152,768]{2,1,0:T(8,128)(2,1)}, u32[]{:S(2)}) copy-start(bf16[1,1152,768]{2,1,0:T(8,128)(2,1)} %param.13) | copy-start | bytes 5308420
  443.4 18.2 %slice-start = ((s8[9437184]{0:T(1024)(128)(4,1)}), s8[4194304]{0:T(1024)(128)(4,1)S(1)}, s32[]{:S(2)}) async-start(s8[9437184]{0:T(1024)(128)(4,1)} %bitcast.96), calls=%async_computation.5 | async-start | bytes 8388608
  443.4 18.2 %slice-start.1 = ((s8[9437184]{0:T(1024)(128)(4,1)}), s8[4194304]{0:T(1024)(128)(4,1)S(1)}, s32[]{:S(2)}) async-start(s8[9437184]{0:T(1024)(128)(4,1)} %bitcast.96), calls=%async_computation.6 | async-start | bytes 8388608
  452.5 9.1 %slice-start.2 = ((s8[9437184]{0:T(1024)(128)(4,1)}), s8[1048576]{0:T(1024)(128)(4,1)S(1)}, s32[]{:S(2)}) async-start(s8[9437184]{0:T(1024)(128)(4,1)} %bitcast.96), calls=%async_computation.7 | async-start | bytes 2097152
  452.5 9.1 %copy-start.9 = (f32[1152,768]{1,0:T(8,128)S(1)}, f32[1152,768]{1,0:T(8,128)}, u32[]{:S(2)}) copy-start(f32[1152,768]{1,0:T(8,128)} %copy-done.8) | copy-start | bytes 10616836
  560.7 11.8 %copy-start.1 = (bf16[1,2048,768]{2,1,0:T(8,128)(2,1)S(1)}, bf16[1,2048,768]{2,1,0:T(8,128)(2,1)}, u32[]{:S(2)}) copy-start(bf16[1,2048,768]{2,1,0:T(8,128)(2,1)} %param.15) | copy-start | bytes 9437188
  568.1 3.3 copy-start.2
Sparse Core Ops, SparseCore 0:
  311.5 126.2 all-reduce.1

commit v3 on v2

--- a/solution.py
+++ b/solution.py
@@ -187,7 +187,13 @@
         tokens, logit_grad, contract_rows, preferred_element_type=jnp.float32
     )
     total_tokens = tokens.shape[0] * outer_size * inner_size
-    grad_router = lax.psum(router_part, axes) * (1.0 / math.sqrt(total_tokens))
+    devices = outer_size * inner_size
+    part_rows = router_part.reshape(devices, -1)
+    got_parts = lax.all_to_all(part_rows, axes, split_axis=0, concat_axis=0, tiled=True)
+    chunk_sum = jnp.sum(got_parts, axis=0, keepdims=True)
+    spread = jnp.broadcast_to(chunk_sum, part_rows.shape)
+    got_sums = lax.all_to_all(spread, axes, split_axis=0, concat_axis=0, tiled=True)
+    grad_router = got_sums.reshape(router_part.shape) * (1.0 / math.sqrt(total_tokens))
     back_grad = grad_rows.reshape(experts, capacity, width)
     grad_router, back_grad = lax.optimization_barrier((grad_router, back_grad))
     back_rows = lax.all_to_all(back_grad, axes, split_axis=0, concat_axis=0, tiled=True)

time: 580 us -> 506 us (0.87)
  waiting for transfers between devices: 428 us -> 328 us
  starting transfers between devices: 16.7 us -> 37.6 us
  between operations: 14.3 us -> 1.06 us
  local copies, waits for them, and re-layouts: 31.9 us -> 39.8 us
    psum x1 -> x0, waiting for transfers between devices: 94.8 us -> none  [body(): grad_router = lax.psum(router_part, axes) * (1.0 / math.sqrt(total_tokens))]
    all_to_all x0 -> x2, starting transfers between devices: none -> 18.9 us  [the longest x1 13.4 us: body(): lax.all_to_all(spread, axes, split_axis=0, concat_axis=0, tiled=True)]
  transfers between devices with their start and end apart: 5 -> 6, of which waited for: 5 -> 4; matrix products, arithmetic and copies ran while one was open for 10% -> 14% of each run, Pallas kernels for 0% -> 0%
where the time goes in v3:
time: 506 us; the launch traced here: 501 us
  waiting for transfers between devices  328 us (65%)
  matrix products  85.7 us (17%)
  local copies, waits for them, and re-layouts  39.8 us (8%)
  starting transfers between devices  37.6 us (7%)
  other arithmetic  8.79 us (2%)
    all_to_all x1, waiting for transfers between devices, body(): lax.all_to_all(grid_both, axes, split_axis=0, concat_axis=0, tiled=True)  228 us
    all_to_all x1, waiting for transfers between devices, body(): lax.all_to_all(back_grad, axes, split_axis=0, concat_axis=0, tiled=True)  91.9 us
    all_to_all x1, starting transfers between devices, body(): lax.all_to_all(spread, axes, split_axis=0, concat_axis=0, tiled=True)  13.4 us
    reshape x1, local copies, waits for them, and re-layouts, body(): got_both = got_both.reshape(-1, 2 * width)  13.2 us
    dot_general x1, matrix products, expert_backward(): lax.dot_general(grad_up_pre, up_matrix, contract_cols, preferred_element_...  12.3 us
    dot_general x1, matrix products, expert_backward(): lax.dot_general(scaled_cot, down_matrix, contract_cols, preferred_element...  10.9 us
  transfers between devices with their start and end apart: 6, of which 4 were waited for; matrix products, arithmetic and copies ran while one was open for 14% of the time, Pallas kernels for 0%

profile of v3, /device:TPU:0, one launch (start us, length us, event | category | flops | bytes accessed | tf_op | source)
XLA Modules:
  0.0 500.9 jit_solution(15209796201896563118)
XLA Ops:
  3.1 6.0 %fusion.51 = bf16[1152,128]{1,0:T(8,128)(2,1)S(1)} fusion(s32[128,8]{0,1:T(8,128)S(1)} %multiply_add_fusion.1), kind=kLoop, calls=%fused_computation.57 | loop fusion | flops 3391488 | bytes 299008 | tf_op jit(solution)/shard_map/reduce_sum | solution.py:29
  9.9 8.0 %convolution_convert_fusion = bf16[32,36,4096]{2,1,0:T(8,128)(2,1)} fusion(bf16[32,36,128]{2,1,0:T(8,128)(2,1)} %reshape.130, bf16[128,2048]{1,0:T(8,128)(2,1)} %param.10, bf16[128,2048]{1,0:T(8,128)(2,1)} %param.9), kind=kOutput, calls=%fused_computation.5 | convolution fusion | flops 1214775296 | bytes 10780672 | tf_op jit(solution)/shard_map/dot_general | solution.py:152
  17.9 7.4 %all-to-all-start = ((bf16[32,36,4096]{2,1,0:T(8,128)(2,1)}), bf16[32,36,4096]{2,1,0:T(8,128)(2,1)}, u32[]{:S(2)}, u32[]{:S(2)}) async-start(bf16[32,36,4096]{2,1,0:T(8,128)(2,1)} %convolution_convert_fusion), calls=%async_computation | async-start | bytes 20971520 | tf_op jit(solution)/shard_map/all_to_all | solution.py:160
  26.7 228.5 %all-to-all-done = bf16[32,36,4096]{2,1,0:T(8,128)(2,1)} async-done(((bf16[32,36,4096]{2,1,0:T(8,128)(2,1)}), bf16[32,36,4096]{2,1,0:T(8,128)(2,1)}, u32[]{:S(2)}, u32[]{:S(2)}) %all-to-all-start) | async-done | bytes 9437216 | tf_op jit(solution)/shard_map/all_to_all | solution.py:160
  255.2 13.2 %reshape.131 = bf16[1152,4096]{1,0:T(8,128)(2,1)} reshape(bf16[32,36,4096]{2,1,0:T(8,128)(2,1)} %all-to-all-done) | data formatting | bytes 18874368 | tf_op jit(solution)/shard_map/reshape | solution.py:162
  268.4 8.6 %fusion = bf16[1152]{0:T(1024)(128)(2,1)S(1)} fusion(bf16[1152,4096]{1,0:T(8,128)(2,1)} %reshape.131, bf16[1,768,2048]{2,1,0:T(8,128)(2,1)} %param.17, bf16[1,1152,768]{2,1,0:T(8,128)(2,1)} %param.14, bf16[1,1152,768]{2,1,0:T(8,128)(2,1)} %param.13), kind=kOutput, calls=%fused_computation.2 | convolution fusion | flops 3642752000 | bytes 11405568 | tf_op jit(solution)/shard_map/dot_general | solution.py:75
  277.8 2.8 all-to-all-start.1
  280.6 7.1 %all-to-all-done.1 = bf16[32,1,36]{2,1,0:T(2,128)(2,1)S(1)} async-done(((bf16[32,1,36]{2,1,0:T(2,128)(2,1)}), bf16[32,1,36]{2,1,0:T(2,128)(2,1)S(1)}, u32[]{:S(2)}, u32[]{:S(2)}) %all-to-all-start.1) | async-done | bytes 2336 | tf_op jit(solution)/shard_map/all_to_all | solution.py:176
  287.9 5.9 %fusion.8 = f32[1,128,8]{2,0,1:T(1,128)S(1)} fusion(bf16[1152,1,1]{0,1,2:T(2,128)(2,1)S(1)} %reshape.139, s32[1024]{0:T(1024)S(1)} %multiply_add_fusion), kind=kOutput, calls=%fused_computation.19 | convolution fusion | flops 3538944 | bytes 10496 | tf_op jit(solution)/shard_map/dot_general | solution.py:178
  295.8 2.5 all-to-all-start.4
  302.6 2.4 all_to_all.34
  305.4 5.5 %all-to-all-start.2 = ((f32[32,1,2048]{2,1,0:T(1,128)}), f32[32,1,2048]{2,1,0:T(1,128)}, u32[]{:S(2)}, u32[]{:S(2)}) async-start(f32[32,1,2048]{2,1,0:T(1,128)} %all_to_all.34), calls=%async_computation.2 | async-start | bytes 524288 | tf_op jit(solution)/shard_map/all_to_all | solution.py:192
  311.1 10.9 %fusion.19 = (bf16[1152,768]{1,0:T(8,128)(2,1)S(1)}, f32[1152,768]{1,0:T(8,128)}) fusion(bf16[1,1152,768]{2,1,0:T(8,128)(2,1)} %param.14, bf16[1,1152,768]{2,1,0:T(8,128)(2,1)} %param.13, bf16[1,768,2048]{2,1,0:T(8,128)(2,1)} %param.17, f32[1152]{0:T(1024)S(1)} %reshape.135, bf16[1152,4096]{1,0:T(8,128)(2,1)} %reshape.131), kind=kOutput, calls=%fused_computation.32 | convolution fusion | flops 3641573376 | bytes 16716288 | tf_op jit(solution)/shard_map/dot_general | solution.py:81
  323.2 6.3 %fusion.36 = f32[1152,2048]{1,0:T(8,128)} fusion(bf16[1152,768]{1,0:T(8,128)(2,1)S(1)} %get-tuple-element.31, bf16[1,2048,768]{2,1,0:T(8,128)(2,1)S(1)} %copy-done), kind=kOutput, calls=%fused_computation.47 | convolution fusion | flops 3623878656 | bytes 14352384 | tf_op jit(solution)/shard_map/dot_general | solution.py:89
  331.4 13.4 %all-to-all-start.3 = ((f32[32,1,2048]{2,1,0:T(1,128)}), f32[32,1,2048]{2,1,0:T(1,128)S(1)}, u32[]{:S(2)}, u32[]{:S(2)}) async-start(f32[32,1,2048]{2,1,0:T(1,128)} %broadcast_in_dim.33), calls=%async_computation.3 | async-start | bytes 524288 | tf_op jit(solution)/shard_map/all_to_all | solution.py:195
  344.8 12.3 %add_convert_fusion = bf16[1152,2048]{1,0:T(8,128)(2,1)} fusion(f32[1152,2048]{1,0:T(8,128)} %fusion.36, bf16[1,2048,768]{2,1,0:T(8,128)(2,1)} %param.16, f32[1152,768]{1,0:T(8,128)} %get-tuple-element.32, bf16[1,1152,768]{2,1,0:T(8,128)(2,1)} %param.13), kind=kOutput, calls=%fused_computation.4 | convolution fusion | flops 3634790400 | bytes 22609920 | tf_op jit(solution)/shard_map/dot_general | solution.py:92
  357.2 7.2 %reshape.133 = bf16[32,36,2048]{2,1,0:T(8,128)(2,1)} reshape(bf16[1152,2048]{1,0:T(8,128)(2,1)} %add_convert_fusion) | data formatting | bytes 9437184 | tf_op jit(solution)/shard_map/reshape | solution.py:197
  365.5 6.0 %all-to-all-start.5 = ((bf16[32,36,2048]{2,1,0:T(8,128)(2,1)}), bf16[32,36,2048]{2,1,0:T(8,128)(2,1)}, u32[]{:S(2)}, u32[]{:S(2)}) async-start(bf16[32,36,2048]{2,1,0:T(8,128)(2,1)} %reshape.133), calls=%async_computation.5 | async-start | bytes 10485760 | tf_op jit(solution)/shard_map/all_to_all | solution.py:199
  371.5 9.1 %fusion.45 = bf16[1,2048,768]{2,1,0:T(8,128)(2,1)} fusion(bf16[1152,768]{1,0:T(8,128)(2,1)} %copy-done.7, bf16[1152,4096]{1,0:T(8,128)(2,1)} %reshape.131), kind=kOutput, calls=%fused_computation.54 | convolution fusion | flops 3625451520 | bytes 9633792 | tf_op jit(solution)/shard_map/dot_general | solution.py:94
  380.5 9.2 %fusion.41 = bf16[1,768,2048]{2,1,0:T(8,128)(2,1)} fusion(bf16[1,1152,768]{2,1,0:T(8,128)(2,1)S(1)} %copy-done.4, bf16[1,1152,768]{2,1,0:T(8,128)(2,1)S(1)} %copy-done.5, f32[1152]{0:T(1024)S(1)} %reshape.135, bf16[1152,4096]{1,0:T(8,128)(2,1)} %reshape.131), kind=kOutput, calls=%fused_computation.52 | convolution fusion | flops 3639607296 | bytes 11407872 | tf_op jit(solution)/shard_map/dot_general | solution.py:100
  389.7 6.3 %fusion.42 = bf16[1,2048,768]{2,1,0:T(8,128)(2,1)} fusion(bf16[1152,4096]{1,0:T(8,128)(2,1)S(1)} %bitcast.97, f32[1152,768]{1,0:T(8,128)S(1)} %copy-done.6, bf16[1,1152,768]{2,1,0:T(8,128)(2,1)S(1)} %copy-done.5), kind=kOutput, calls=%fused_computation.53 | convolution fusion | flops 3631644672 | bytes 13172736 | tf_op jit(solution)/shard_map/dot_general | solution.py:97
  397.1 91.9 %all-to-all-done.5 = bf16[32,36,2048]{2,1,0:T(8,128)(2,1)} async-done(((bf16[32,36,2048]{2,1,0:T(8,128)(2,1)}), bf16[32,36,2048]{2,1,0:T(8,128)(2,1)}, u32[]{:S(2)}, u32[]{:S(2)}) %all-to-all-start.5) | async-done | bytes 4718624 | tf_op jit(solution)/shard_map/all_to_all | solution.py:199
  488.9 7.4 %reshape.134 = bf16[1152,2048]{1,0:T(8,128)(2,1)} reshape(bf16[32,36,2048]{2,1,0:T(8,128)(2,1)} %all-to-all-done.5) | data formatting | bytes 9437184 | tf_op jit(solution)/shard_map/reshape | solution.py:201
  496.3 3.2 fusion.76
  (58 shorter events, 18.7 us)
Async XLA Ops:
  0.6 322.6 %copy-start = (bf16[1,2048,768]{2,1,0:T(8,128)(2,1)S(1)}, bf16[1,2048,768]{2,1,0:T(8,128)(2,1)}, u32[]{:S(2)}) copy-start(bf16[1,2048,768]{2,1,0:T(8,128)(2,1)} %param.15) | copy-start | bytes 9437188
  17.9 8.8 %copy-start.3 = (s32[128,8]{0,1:T(8,128)S(1)}, s32[128,8]{0,1:T(8,128)}, u32[]{:S(2)}) copy-start(s32[128,8]{0,1:T(8,128)} %param.11) | copy-start | bytes 12292
  17.9 237.3 %all-to-all-start = ((bf16[32,36,4096]{2,1,0:T(8,128)(2,1)}), bf16[32,36,4096]{2,1,0:T(8,128)(2,1)}, u32[]{:S(2)}, u32[]{:S(2)}) async-start(bf16[32,36,4096]{2,1,0:T(8,128)(2,1)} %convolution_convert_fusion), calls=%async_computation | async-start | bytes 20971520 | tf_op jit(solution)/shard_map/all_to_all | solution.py:160
  277.8 9.9 %all-to-all-start.1 = ((bf16[32,1,36]{2,1,0:T(2,128)(2,1)}), bf16[32,1,36]{2,1,0:T(2,128)(2,1)S(1)}, u32[]{:S(2)}, u32[]{:S(2)}) async-start(bf16[32,1,36]{2,1,0:T(2,128)(2,1)} %convert_element_type.152), calls=%async_computation.1 | async-start | bytes 32768 | tf_op jit(solution)/shard_map/all_to_all | solution.py:176
  295.8 9.6 %all-to-all-start.4 = ((bf16[32,1,36]{2,1,0:T(2,128)(2,1)}), bf16[32,1,36]{2,1,0:T(2,128)(2,1)S(1)}, u32[]{:S(2)}, u32[]{:S(2)}) async-start(bf16[32,1,36]{2,1,0:T(2,128)(2,1)} %all_to_all.35), calls=%async_computation.4 | async-start | bytes 32768 | tf_op jit(solution)/shard_map/all_to_all | solution.py:161
  305.4 24.1 %all-to-all-start.2 = ((f32[32,1,2048]{2,1,0:T(1,128)}), f32[32,1,2048]{2,1,0:T(1,128)}, u32[]{:S(2)}, u32[]{:S(2)}) async-start(f32[32,1,2048]{2,1,0:T(1,128)} %all_to_all.34), calls=%async_computation.2 | async-start | bytes 524288 | tf_op jit(solution)/shard_map/all_to_all | solution.py:192
  322.0 1.2 copy-start.7
  331.4 33.0 %all-to-all-start.3 = ((f32[32,1,2048]{2,1,0:T(1,128)}), f32[32,1,2048]{2,1,0:T(1,128)S(1)}, u32[]{:S(2)}, u32[]{:S(2)}) async-start(f32[32,1,2048]{2,1,0:T(1,128)} %broadcast_in_dim.33), calls=%async_computation.3 | async-start | bytes 524288 | tf_op jit(solution)/shard_map/all_to_all | solution.py:195
  365.5 123.5 %all-to-all-start.5 = ((bf16[32,36,2048]{2,1,0:T(8,128)(2,1)}), bf16[32,36,2048]{2,1,0:T(8,128)(2,1)}, u32[]{:S(2)}, u32[]{:S(2)}) async-start(bf16[32,36,2048]{2,1,0:T(8,128)(2,1)} %reshape.133), calls=%async_computation.5 | async-start | bytes 10485760 | tf_op jit(solution)/shard_map/all_to_all | solution.py:199
  371.4 9.1 %copy-start.4 = (bf16[1,1152,768]{2,1,0:T(8,128)(2,1)S(1)}, bf16[1,1152,768]{2,1,0:T(8,128)(2,1)}, u32[]{:S(2)}) copy-start(bf16[1,1152,768]{2,1,0:T(8,128)(2,1)} %param.14) | copy-start | bytes 5308420
  371.4 9.1 %copy-start.5 = (bf16[1,1152,768]{2,1,0:T(8,128)(2,1)S(1)}, bf16[1,1152,768]{2,1,0:T(8,128)(2,1)}, u32[]{:S(2)}) copy-start(bf16[1,1152,768]{2,1,0:T(8,128)(2,1)} %param.13) | copy-start | bytes 5308420
  371.4 18.3 %slice-start = ((s8[9437184]{0:T(1024)(128)(4,1)}), s8[4194304]{0:T(1024)(128)(4,1)S(1)}, s32[]{:S(2)}) async-start(s8[9437184]{0:T(1024)(128)(4,1)} %bitcast.96), calls=%async_computation.6 | async-start | bytes 8388608
  371.5 18.3 %slice-start.1 = ((s8[9437184]{0:T(1024)(128)(4,1)}), s8[4194304]{0:T(1024)(128)(4,1)S(1)}, s32[]{:S(2)}) async-start(s8[9437184]{0:T(1024)(128)(4,1)} %bitcast.96), calls=%async_computation.7 | async-start | bytes 8388608
  380.5 9.2 %slice-start.2 = ((s8[9437184]{0:T(1024)(128)(4,1)}), s8[1048576]{0:T(1024)(128)(4,1)S(1)}, s32[]{:S(2)}) async-start(s8[9437184]{0:T(1024)(128)(4,1)} %bitcast.96), calls=%async_computation.8 | async-start | bytes 2097152
  380.5 9.2 %copy-start.6 = (f32[1152,768]{1,0:T(8,128)S(1)}, f32[1152,768]{1,0:T(8,128)}, u32[]{:S(2)}) copy-start(f32[1152,768]{1,0:T(8,128)} %get-tuple-element.32) | copy-start | bytes 10616836
  488.9 11.8 %copy-start.1 = (bf16[1,2048,768]{2,1,0:T(8,128)(2,1)S(1)}, bf16[1,2048,768]{2,1,0:T(8,128)(2,1)}, u32[]{:S(2)}) copy-start(bf16[1,2048,768]{2,1,0:T(8,128)(2,1)} %param.15) | copy-start | bytes 9437188
  496.3 3.3 copy-start.2

commit v4 on v3

--- a/solution.py
+++ b/solution.py
@@ -127,6 +127,37 @@
         tokens, logit_grad, contract_rows, preferred_element_type=jnp.float32
     )
     return (grad_tokens, router_part)
+
+
+def expert_from_cot(cot_rows, weight_rows, gate_pre, up_pre, gate_matrix, up_matrix, down_matrix):
+    gate_value = gate_pre.astype(jnp.float32)
+    up_value = up_pre.astype(jnp.float32)
+    sigmoid_gate = jax.nn.sigmoid(gate_value)
+    silu_gate = gate_value * sigmoid_gate
+    hidden = (silu_gate * up_value).astype(jnp.bfloat16)
+    expert_out = jnp.dot(hidden, down_matrix, preferred_element_type=jnp.float32).astype(
+        jnp.bfloat16
+    )
+    scaled_cot = (weight_rows.astype(jnp.float32)[:, None] * cot_rows.astype(jnp.float32)).astype(
+        jnp.bfloat16
+    )
+    grad_hidden = lax.dot_general(
+        scaled_cot, down_matrix, contract_cols, preferred_element_type=jnp.float32
+    )
+    grad_gate_pre = (
+        grad_hidden * up_value * sigmoid_gate * (1.0 + gate_value * (1.0 - sigmoid_gate))
+    ).astype(jnp.bfloat16)
+    grad_up_pre = (grad_hidden * silu_gate).astype(jnp.bfloat16)
+    grad_rows = (
+        lax.dot_general(
+            grad_gate_pre, gate_matrix, contract_cols, preferred_element_type=jnp.float32
+        )
+        + lax.dot_general(grad_up_pre, up_matrix, contract_cols, preferred_element_type=jnp.float32)
+    ).astype(jnp.bfloat16)
+    grad_down_w = lax.dot_general(
+        hidden, scaled_cot, contract_rows, preferred_element_type=jnp.float32
+    ).astype(jnp.bfloat16)
+    return (grad_rows, expert_out, grad_gate_pre, grad_up_pre, grad_down_w)
 
 
 def body(
@@ -148,22 +179,25 @@
     axes = ("outer", "inner")
     picked, probs = route_probs(tokens, routes, router_weight)
     slot_table, token_table = route_tables(routes, experts, capacity)
-    both = jnp.concatenate([tokens, cotangent], axis=1)
-    grid_both = jnp.dot(
-        token_table.reshape(experts, capacity, -1), both, preferred_element_type=jnp.float32
-    ).astype(jnp.bfloat16)
+    grid_table = token_table.reshape(experts, capacity, -1)
     probs_low = probs.astype(jnp.bfloat16).reshape(-1)
     send_weight = jnp.dot(slot_table, probs_low, preferred_element_type=jnp.float32).astype(
         jnp.bfloat16
     )
-    grid_weight = send_weight.reshape(experts, capacity)
-    got_both = lax.all_to_all(grid_both, axes, split_axis=0, concat_axis=0, tiled=True)
-    got_weight = lax.all_to_all(grid_weight, axes, split_axis=0, concat_axis=0, tiled=True)
-    got_both = got_both.reshape(-1, 2 * width)
-    input_rows = got_both[:, :width]
-    cot_rows = got_both[:, width:]
-    grad_rows, expert_out, grad_gate_w, grad_up_w, grad_down_w = expert_backward(
-        input_rows,
+    got_weight = lax.all_to_all(
+        send_weight.reshape(experts, capacity), axes, split_axis=0, concat_axis=0, tiled=True
+    )
+    grid_cot = jnp.dot(grid_table, cotangent, preferred_element_type=jnp.float32).astype(
+        jnp.bfloat16
+    )
+    got_cot = lax.all_to_all(grid_cot, axes, split_axis=0, concat_axis=0, tiled=True)
+    grid_tokens = jnp.dot(grid_table, tokens, preferred_element_type=jnp.float32).astype(
+        jnp.bfloat16
+    )
+    got_cot, grid_tokens = lax.optimization_barrier((got_cot, grid_tokens))
+    got_tokens = lax.all_to_all(grid_tokens, axes, split_axis=0, concat_axis=0, tiled=True)
+    cot_rows = got_cot.reshape(-1, width)
+    grad_rows, expert_out, grad_gate_pre, grad_up_pre, grad_down_w = expert_from_cot(
         cot_rows,
         got_weight.reshape(-1),
         gate_saved[0],
@@ -195,10 +229,17 @@
     got_sums = lax.all_to_all(spread, axes, split_axis=0, concat_axis=0, tiled=True)
     grad_router = got_sums.reshape(router_part.shape) * (1.0 / math.sqrt(total_tokens))
     back_grad = grad_rows.reshape(experts, capacity, width)
-    grad_router, back_grad = lax.optimization_barrier((grad_router, back_grad))
+    back_grad, got_tokens = lax.optimization_barrier((back_grad, got_tokens))
     back_rows = lax.all_to_all(back_grad, axes, split_axis=0, concat_axis=0, tiled=True)
+    input_rows = got_tokens.reshape(-1, width)
+    grad_gate_w = lax.dot_general(
+        input_rows, grad_gate_pre, contract_rows, preferred_element_type=jnp.float32
+    ).astype(jnp.bfloat16)
+    grad_up_w = lax.dot_general(
+        input_rows, grad_up_pre, contract_rows, preferred_element_type=jnp.float32
+    ).astype(jnp.bfloat16)
     grad_sum = lax.dot_general(
-        token_table, back_rows.reshape(-1, width), contract_rows, preferred_element_type=jnp.float32
+        grid_table, back_rows, (((0, 1), (0, 1)), ((), ())), preferred_element_type=jnp.float32
     )
     grad_tokens = (
         grad_sum

time: 506 us -> 487 us (0.962)
  waiting for transfers between devices: 328 us -> 287 us
  blocking collectives: 0 us -> 15.9 us
  starting transfers between devices: 37.6 us -> 25.3 us
  other arithmetic: 8.79 us -> 17.6 us
    all_to_all x3, waiting for transfers between devices: 229 us -> 196 us  [the longest x1 111 us: body(): lax.all_to_all(grid_cot, axes, split_axis=0, concat_axis=0, tiled=True)]
    all_to_all x0 -> x1, blocking collectives: none -> 15.9 us  [body(): lax.all_to_all(part_rows, axes, split_axis=0, concat_axis=0, tiled=True)]
    convert_element_type x1 -> x2, local copies, waits for them, and re-layouts: 0.1 us -> 15.3 us  [the longest x1 8.01 us: expert_from_cot(): cot_rows.astype(jnp.float32)]
    reshape x3 -> x2, local copies, waits for them, and re-layouts: 21.4 us -> 8.39 us  [the longest x1 7.38 us: body(): input_rows = got_tokens.reshape(-1, width)]
    all_to_all x1, starting transfers between devices: 13.4 us -> 2.59 us  [body(): lax.all_to_all(spread, axes, split_axis=0, concat_axis=0, tiled=True)]
    all_to_all x1, waiting for transfers between devices: 91.9 us -> 84.3 us  [body(): lax.all_to_all(back_grad, axes, split_axis=0, concat_axis=0, tiled=True)]
    convert_element_type x2, other arithmetic: 0.06 us -> 5.73 us  [the longest x1 5.71 us: expert_from_cot(): (weight_rows.astype(jnp.float32)[:, None] * cot_rows.astype(jnp.float32))...]
    dot_general x9 -> x10, matrix products: 74 us -> 76.2 us  [the longest x1 12.3 us: expert_from_cot(): lax.dot_general(grad_up_pre, up_matrix, contract_cols, preferred_element_...]
  transfers between devices with their start and end apart: 6 -> 6, of which waited for: 4 -> 5; matrix products, arithmetic and copies ran while one was open for 14% -> 20% of each run, Pallas kernels for 0% -> 0%
where the time goes in v4:
time: 487 us; the launch traced here: 478 us
  waiting for transfers between devices  287 us (59%)
  matrix products  89.3 us (18%)
  local copies, waits for them, and re-layouts  42 us (9%)
  starting transfers between devices  25.3 us (5%)
  other arithmetic  17.6 us (4%)
  blocking collectives  15.9 us (3%)
    all_to_all x1, waiting for transfers between devices, body(): lax.all_to_all(grid_cot, axes, split_axis=0, concat_axis=0, tiled=True)  111 us
    all_to_all x1, waiting for transfers between devices, body(): lax.all_to_all(grid_tokens, axes, split_axis=0, concat_axis=0, tiled=True)  85 us
    all_to_all x1, waiting for transfers between devices, body(): lax.all_to_all(back_grad, axes, split_axis=0, concat_axis=0, tiled=True)  84.3 us
    all_to_all x1, blocking collectives, body(): lax.all_to_all(part_rows, axes, split_axis=0, concat_axis=0, tiled=True)  15.9 us
    dot_general x1, matrix products, expert_from_cot(): lax.dot_general(grad_up_pre, up_matrix, contract_cols, preferred_element_...  12.3 us
    dot_general x1, matrix products, expert_from_cot(): lax.dot_general(scaled_cot, down_matrix, contract_cols, preferred_element...  10.9 us
    dot_general x1, matrix products, expert_from_cot(): jnp.dot(hidden, down_matrix, preferred_element_type=jnp.float32)  9.94 us
  transfers between devices with their start and end apart: 6, of which 5 were waited for; matrix products, arithmetic and copies ran while one was open for 20% of the time, Pallas kernels for 0%

profile of v4, /device:TPU:0, one launch (start us, length us, event | category | flops | bytes accessed | tf_op | source)
XLA Modules:
  0.0 478.4 jit_solution(7034006524218996219)
XLA Ops:
  3.1 6.7 %fusion.33 = bf16[1152,128]{1,0:T(8,128)(2,1)} fusion(s32[128,8]{0,1:T(8,128)S(1)} %multiply_add_fusion.1), kind=kLoop, calls=%fused_computation.52 | loop fusion | flops 3391488 | bytes 299008 | tf_op jit(solution)/shard_map/reduce_sum | solution.py:29
  10.8 4.9 %convolution_convert_fusion.2 = bf16[32,36,2048]{2,1,0:T(8,128)(2,1)} fusion(bf16[32,36,128]{2,1,0:T(8,128)(2,1)S(1)} %reshape.143, bf16[128,2048]{1,0:T(8,128)(2,1)} %param.10), kind=kOutput, calls=%fused_computation.22 | convolution fusion | flops 606339072 | bytes 5537792 | tf_op jit(solution)/shard_map/dot_general | solution.py:190
  15.7 7.4 %all-to-all-start.1 = ((bf16[32,36,2048]{2,1,0:T(8,128)(2,1)}), bf16[32,36,2048]{2,1,0:T(8,128)(2,1)}, u32[]{:S(2)}, u32[]{:S(2)}) async-start(bf16[32,36,2048]{2,1,0:T(8,128)(2,1)} %convolution_convert_fusion.2), calls=%async_computation.1 | async-start | bytes 10485760 | tf_op jit(solution)/shard_map/all_to_all | solution.py:193
  25.1 4.8 %convolution_convert_fusion.1 = bf16[32,36,2048]{2,1,0:T(8,128)(2,1)} fusion(bf16[32,36,128]{2,1,0:T(8,128)(2,1)S(1)} %reshape.143, bf16[128,2048]{1,0:T(8,128)(2,1)} %param.9), kind=kOutput, calls=%fused_computation.21 | convolution fusion | flops 606339072 | bytes 5537792 | tf_op jit(solution)/shard_map/dot_general | solution.py:194
  30.0 110.7 %all-to-all-done.1 = bf16[32,36,2048]{2,1,0:T(8,128)(2,1)} async-done(((bf16[32,36,2048]{2,1,0:T(8,128)(2,1)}), bf16[32,36,2048]{2,1,0:T(8,128)(2,1)}, u32[]{:S(2)}, u32[]{:S(2)}) %all-to-all-start.1) | async-done | bytes 4718624 | tf_op jit(solution)/shard_map/all_to_all | solution.py:193
  140.6 8.0 %reshape.150 = f32[1152,2048]{1,0:T(8,128)} reshape(bf16[32,36,2048]{2,1,0:T(8,128)(2,1)} %all-to-all-done.1) | data formatting | bytes 14155776 | tf_op jit(solution)/shard_map/convert_element_type | solution.py:141
  148.6 9.9 %multiply_reduce_fusion = bf16[1152]{0:T(1024)(128)(2,1)S(1)} fusion(f32[1152,2048]{1,0:T(8,128)} %reshape.150, bf16[1,768,2048]{2,1,0:T(8,128)(2,1)} %param.17, bf16[1,1152,768]{2,1,0:T(8,128)(2,1)} %param.14, bf16[1,1152,768]{2,1,0:T(8,128)(2,1)} %param.13), kind=kOutput, calls=%fused_computation.1 | convolution fusion | flops 3640392704 | bytes 16124160 | tf_op jit(solution)/shard_map/dot_general | solution.py:138
  162.6 6.6 %all-to-all-done.4 = bf16[32,1,36]{2,1,0:T(2,128)(2,1)S(1)} async-done(((bf16[32,1,36]{2,1,0:T(2,128)(2,1)}), bf16[32,1,36]{2,1,0:T(2,128)(2,1)S(1)}, u32[]{:S(2)}, u32[]{:S(2)}) %all-to-all-start.4) | async-done | bytes 2336 | tf_op jit(solution)/shard_map/all_to_all | solution.py:210
  169.3 6.6 %fusion.6 = f32[1,128,8]{2,0,1:T(1,128)S(1)} fusion(bf16[1152,1,1]{0,1,2:T(2,128)(2,1)S(1)} %reshape.156, s32[1024]{0:T(1024)} %multiply_add_fusion), kind=kOutput, calls=%fused_computation.16 | convolution fusion | flops 3538944 | bytes 10496 | tf_op jit(solution)/shard_map/dot_general | solution.py:212
  189.6 15.9 %all_to_all.47 = f32[32,1,2048]{2,1,0:T(1,128)} all-to-all(f32[32,1,2048]{2,1,0:T(1,128)} %all_to_all.39), channel_id=1, replica_groups=mesh['outer'=4,'inner'=8] {'outer','inner'}, dimensions={0} | all-to-all | bytes 524288 | tf_op jit(solution)/shard_map/all_to_all | solution.py:226
  205.4 3.8 all-to-all-start.2
  209.3 5.7 %multiply_convert_fusion = bf16[32,36,2048]{2,1,0:T(8,128)(2,1)} fusion(f32[32,36]{1,0:T(8,128)S(1)} %bitcast.103, bf16[32,36,2048]{2,1,0:T(8,128)(2,1)} %all-to-all-done.1), kind=kLoop, calls=%fused_computation | loop fusion | flops 7077888 | bytes 9441792 | tf_op jit(solution)/shard_map/convert_element_type | solution.py:141
  215.0 7.2 %convert_element_type.144 = bf16[1152,2048]{1,0:T(8,128)(2,1)} reshape(bf16[32,36,2048]{2,1,0:T(8,128)(2,1)} %multiply_convert_fusion) | data formatting | bytes 9437184 | tf_op jit(solution)/shard_map/convert_element_type | solution.py:141
  222.2 10.9 %fusion.12 = (bf16[1152,768]{1,0:T(8,128)(2,1)S(1)}, f32[1152,768]{1,0:T(8,128)}) fusion(bf16[1,1152,768]{2,1,0:T(8,128)(2,1)} %param.14, bf16[1,1152,768]{2,1,0:T(8,128)(2,1)} %param.13, bf16[1152,2048]{1,0:T(8,128)(2,1)} %convert_element_type.144, bf16[1,768,2048]{2,1,0:T(8,128)(2,1)} %param.17), kind=kOutput, calls=%fused_computation.26 | convolution fusion | flops 3634495488 | bytes 16711680 | tf_op jit(solution)/shard_map/dot_general | solution.py:144
  234.3 6.3 %fusion.24 = f32[1152,2048]{1,0:T(8,128)} fusion(bf16[1152,768]{1,0:T(8,128)(2,1)S(1)} %get-tuple-element.40, bf16[1,2048,768]{2,1,0:T(8,128)(2,1)S(1)} %copy-done), kind=kOutput, calls=%fused_computation.41 | convolution fusion | flops 3623878656 | bytes 14352384 | tf_op jit(solution)/shard_map/dot_general | solution.py:152
  241.7 85.0 %all-to-all-done.2 = bf16[32,36,2048]{2,1,0:T(8,128)(2,1)} async-done(((bf16[32,36,2048]{2,1,0:T(8,128)(2,1)}), bf16[32,36,2048]{2,1,0:T(8,128)(2,1)}, u32[]{:S(2)}, u32[]{:S(2)}) %all-to-all-start.2) | async-done | bytes 4718624 | tf_op jit(solution)/shard_map/all_to_all | solution.py:198
  330.2 12.3 %add_convert_fusion = bf16[1152,2048]{1,0:T(8,128)(2,1)} fusion(f32[1152,2048]{1,0:T(8,128)} %fusion.24, bf16[1,2048,768]{2,1,0:T(8,128)(2,1)} %param.16, f32[1152,768]{1,0:T(8,128)} %get-tuple-element.41, bf16[1,1152,768]{2,1,0:T(8,128)(2,1)} %param.13), kind=kOutput, calls=%fused_computation.2 | convolution fusion | flops 3634790400 | bytes 22609920 | tf_op jit(solution)/shard_map/dot_general | solution.py:155
  342.5 7.2 %reshape.144 = bf16[32,36,2048]{2,1,0:T(8,128)(2,1)} reshape(bf16[1152,2048]{1,0:T(8,128)(2,1)} %add_convert_fusion) | data formatting | bytes 9437184 | tf_op jit(solution)/shard_map/reshape | solution.py:231
  349.7 6.2 %all-to-all-start.3 = ((bf16[32,36,2048]{2,1,0:T(8,128)(2,1)}), bf16[32,36,2048]{2,1,0:T(8,128)(2,1)}, u32[]{:S(2)}, u32[]{:S(2)}) async-start(bf16[32,36,2048]{2,1,0:T(8,128)(2,1)} %reshape.144), calls=%async_computation.3 | async-start | bytes 10485760 | tf_op jit(solution)/shard_map/all_to_all | solution.py:233
  355.9 9.1 %fusion.31 = bf16[1,768,2048]{2,1,0:T(8,128)(2,1)} fusion(bf16[1152,2048]{1,0:T(8,128)(2,1)} %convert_element_type.144, bf16[1,1152,768]{2,1,0:T(8,128)(2,1)S(1)} %copy-done.5, bf16[1,1152,768]{2,1,0:T(8,128)(2,1)} %param.13), kind=kOutput, calls=%fused_computation.48 | convolution fusion | flops 3632529408 | bytes 11403264 | tf_op jit(solution)/shard_map/dot_general | solution.py:157
  367.1 7.4 %reshape.146 = bf16[1152,2048]{1,0:T(8,128)(2,1)} reshape(bf16[32,36,2048]{2,1,0:T(8,128)(2,1)} %all-to-all-done.2) | data formatting | bytes 9437184 | tf_op jit(solution)/shard_map/reshape | solution.py:234
  374.5 8.3 %fusion.29 = bf16[1,2048,768]{2,1,0:T(8,128)(2,1)} fusion(bf16[1152,2048]{1,0:T(8,128)(2,1)} %reshape.146, bf16[1152,768]{1,0:T(8,128)(2,1)S(1)} %copy-done.9), kind=kOutput, calls=%fused_computation.46 | convolution fusion | flops 3625451520 | bytes 9633792 | tf_op jit(solution)/shard_map/dot_general | solution.py:235
  382.7 6.3 %fusion.30 = bf16[1,2048,768]{2,1,0:T(8,128)(2,1)} fusion(bf16[1152,2048]{1,0:T(8,128)(2,1)S(1)} %copy-done.2, f32[1152,768]{1,0:T(8,128)S(1)} %copy-done.7, bf16[1,1152,768]{2,1,0:T(8,128)(2,1)S(1)} %copy-done.6), kind=kOutput, calls=%fused_computation.47 | convolution fusion | flops 3631644672 | bytes 13172736 | tf_op jit(solution)/shard_map/dot_general | solution.py:238
  389.1 84.3 %all-to-all-done.3 = bf16[32,36,2048]{2,1,0:T(8,128)(2,1)} async-done(((bf16[32,36,2048]{2,1,0:T(8,128)(2,1)}), bf16[32,36,2048]{2,1,0:T(8,128)(2,1)}, u32[]{:S(2)}, u32[]{:S(2)}) %all-to-all-start.3) | async-done | bytes 4718624 | tf_op jit(solution)/shard_map/all_to_all | solution.py:233
  (58 shorter events, 35.5 us)
Async XLA Ops:
  0.6 233.7 %copy-start = (bf16[1,2048,768]{2,1,0:T(8,128)(2,1)S(1)}, bf16[1,2048,768]{2,1,0:T(8,128)(2,1)}, u32[]{:S(2)}) copy-start(bf16[1,2048,768]{2,1,0:T(8,128)(2,1)} %param.15) | copy-start | bytes 9437188
  15.7 8.8 %copy-start.4 = (s32[128,8]{0,1:T(8,128)S(1)}, s32[128,8]{0,1:T(8,128)}, u32[]{:S(2)}) copy-start(s32[128,8]{0,1:T(8,128)} %param.11) | copy-start | bytes 12292
  15.7 124.9 %all-to-all-start.1 = ((bf16[32,36,2048]{2,1,0:T(8,128)(2,1)}), bf16[32,36,2048]{2,1,0:T(8,128)(2,1)}, u32[]{:S(2)}, u32[]{:S(2)}) async-start(bf16[32,36,2048]{2,1,0:T(8,128)(2,1)} %convolution_convert_fusion.2), calls=%async_computation.1 | async-start | bytes 10485760 | tf_op jit(solution)/shard_map/all_to_all | solution.py:193
  159.3 9.8 %all-to-all-start.4 = ((bf16[32,1,36]{2,1,0:T(2,128)(2,1)}), bf16[32,1,36]{2,1,0:T(2,128)(2,1)S(1)}, u32[]{:S(2)}, u32[]{:S(2)}) async-start(bf16[32,1,36]{2,1,0:T(2,128)(2,1)} %convert_element_type.171), calls=%async_computation.4 | async-start | bytes 32768 | tf_op jit(solution)/shard_map/all_to_all | solution.py:210
  179.9 9.6 %all-to-all-start = ((bf16[32,1,36]{2,1,0:T(2,128)(2,1)}), bf16[32,1,36]{2,1,0:T(2,128)(2,1)S(1)}, u32[]{:S(2)}, u32[]{:S(2)}) async-start(bf16[32,1,36]{2,1,0:T(2,128)(2,1)} %all_to_all.38), calls=%async_computation | async-start | bytes 32768 | tf_op jit(solution)/shard_map/all_to_all | solution.py:187
  205.4 121.3 %all-to-all-start.2 = ((bf16[32,36,2048]{2,1,0:T(8,128)(2,1)}), bf16[32,36,2048]{2,1,0:T(8,128)(2,1)}, u32[]{:S(2)}, u32[]{:S(2)}) async-start(bf16[32,36,2048]{2,1,0:T(8,128)(2,1)} %convolution_convert_fusion.1), calls=%async_computation.2 | async-start | bytes 10485760 | tf_op jit(solution)/shard_map/all_to_all | solution.py:198
  233.1 1.2 copy-start.8
  327.6 22.1 %all-to-all-start.6 = ((f32[32,1,2048]{2,1,0:T(1,128)}), f32[32,1,2048]{2,1,0:T(1,128)S(1)}, u32[]{:S(2)}, u32[]{:S(2)}) async-start(f32[32,1,2048]{2,1,0:T(1,128)} %broadcast_in_dim.55), calls=%async_computation.6 | async-start | bytes 524288 | tf_op jit(solution)/shard_map/all_to_all | solution.py:229
  349.7 6.2 %copy-start.5 = (bf16[1,1152,768]{2,1,0:T(8,128)(2,1)S(1)}, bf16[1,1152,768]{2,1,0:T(8,128)(2,1)}, u32[]{:S(2)}) copy-start(bf16[1,1152,768]{2,1,0:T(8,128)(2,1)} %param.14) | copy-start | bytes 5308420
  349.7 123.7 %all-to-all-start.3 = ((bf16[32,36,2048]{2,1,0:T(8,128)(2,1)}), bf16[32,36,2048]{2,1,0:T(8,128)(2,1)}, u32[]{:S(2)}, u32[]{:S(2)}) async-start(bf16[32,36,2048]{2,1,0:T(8,128)(2,1)} %reshape.144), calls=%async_computation.3 | async-start | bytes 10485760 | tf_op jit(solution)/shard_map/all_to_all | solution.py:233
  367.1 7.4 %copy-start.9 = (bf16[1152,768]{1,0:T(8,128)(2,1)S(1)}, bf16[1152,768]{1,0:T(8,128)(2,1)}, u32[]{:S(2)}) copy-start(bf16[1152,768]{1,0:T(8,128)(2,1)} %copy-done.8) | copy-start | bytes 5308420
  374.4 8.3 %copy-start.2 = (bf16[1152,2048]{1,0:T(8,128)(2,1)S(1)}, bf16[1152,2048]{1,0:T(8,128)(2,1)}, u32[]{:S(2)}) copy-start(bf16[1152,2048]{1,0:T(8,128)(2,1)} %reshape.146) | copy-start | bytes 14155780
  374.4 8.3 %copy-start.6 = (bf16[1,1152,768]{2,1,0:T(8,128)(2,1)S(1)}, bf16[1,1152,768]{2,1,0:T(8,128)(2,1)}, u32[]{:S(2)}) copy-start(bf16[1,1152,768]{2,1,0:T(8,128)(2,1)} %param.13) | copy-start | bytes 5308420
  374.5 8.3 %copy-start.7 = (f32[1152,768]{1,0:T(8,128)S(1)}, f32[1152,768]{1,0:T(8,128)}, u32[]{:S(2)}) copy-start(f32[1152,768]{1,0:T(8,128)} %get-tuple-element.41) | copy-start | bytes 10616836
  382.7 95.2 %copy-start.1 = (bf16[1,2048,768]{2,1,0:T(8,128)(2,1)S(1)}, bf16[1,2048,768]{2,1,0:T(8,128)(2,1)}, u32[]{:S(2)}) copy-start(bf16[1,2048,768]{2,1,0:T(8,128)(2,1)} %param.15) | copy-start | bytes 9437188
  473.4 3.4 copy-start.3

commit v5 on v4

--- a/solution.py
+++ b/solution.py
@@ -190,6 +190,7 @@
     grid_cot = jnp.dot(grid_table, cotangent, preferred_element_type=jnp.float32).astype(
         jnp.bfloat16
     )
+    got_weight, grid_cot = lax.optimization_barrier((got_weight, grid_cot))
     got_cot = lax.all_to_all(grid_cot, axes, split_axis=0, concat_axis=0, tiled=True)
     grid_tokens = jnp.dot(grid_table, tokens, preferred_element_type=jnp.float32).astype(
         jnp.bfloat16
@@ -207,6 +208,7 @@
         down_weight[0],
     )
     slot_route_dot = slot_dot(cot_rows, expert_out).reshape(experts, capacity)
+    slot_route_dot, got_tokens = lax.optimization_barrier((slot_route_dot, got_tokens))
     back_dot = lax.all_to_all(slot_route_dot, axes, split_axis=0, concat_axis=0, tiled=True)
     route_dot = back_dot.reshape(-1)
     route_grad = lax.dot_general(
@@ -229,7 +231,7 @@
     got_sums = lax.all_to_all(spread, axes, split_axis=0, concat_axis=0, tiled=True)
     grad_router = got_sums.reshape(router_part.shape) * (1.0 / math.sqrt(total_tokens))
     back_grad = grad_rows.reshape(experts, capacity, width)
-    back_grad, got_tokens = lax.optimization_barrier((back_grad, got_tokens))
+    back_grad, grad_router = lax.optimization_barrier((back_grad, grad_router))
     back_rows = lax.all_to_all(back_grad, axes, split_axis=0, concat_axis=0, tiled=True)
     input_rows = got_tokens.reshape(-1, width)
     grad_gate_w = lax.dot_general(

time: 487 us -> 485 us (level); the launches traced: 478 us -> 483 us
  starting transfers between devices: 25.3 us -> 46.6 us
  blocking collectives: 15.9 us -> 0 us
    all_to_all x1 -> x0, blocking collectives: 15.9 us -> none  [body(): lax.all_to_all(part_rows, axes, split_axis=0, concat_axis=0, tiled=True)]
    all_to_all x1, starting transfers between devices: 2.59 us -> 15.1 us  [body(): lax.all_to_all(spread, axes, split_axis=0, concat_axis=0, tiled=True)]
    all_to_all x1, waiting for transfers between devices: 6.59 us -> 0.01 us  [body(): lax.all_to_all(slot_route_dot, axes, split_axis=0, concat_axis=0, tiled=T...]
    all_to_all x0 -> x1, starting transfers between devices: none -> 5.96 us  [body(): lax.all_to_all(part_rows, axes, split_axis=0, concat_axis=0, tiled=True)]
  transfers between devices with their start and end apart: 6 -> 7, of which waited for: 5 -> 4; matrix products, arithmetic and copies ran while one was open for 20% -> 25% of each run, Pallas kernels for 0% -> 0%
where the time goes in v5:
time: 485 us; the launch traced here: 483 us
  waiting for transfers between devices  285 us (59%)
  matrix products  91.5 us (19%)
  starting transfers between devices  46.6 us (10%)
  local copies, waits for them, and re-layouts  43.6 us (9%)
  other arithmetic  15.3 us (3%)
    all_to_all x1, waiting for transfers between devices, body(): lax.all_to_all(grid_cot, axes, split_axis=0, concat_axis=0, tiled=True)  113 us
    all_to_all x1, waiting for transfers between devices, body(): lax.all_to_all(grid_tokens, axes, split_axis=0, concat_axis=0, tiled=True)  86.4 us
    all_to_all x1, waiting for transfers between devices, body(): lax.all_to_all(back_grad, axes, split_axis=0, concat_axis=0, tiled=True)  83.4 us
    all_to_all x1, starting transfers between devices, body(): lax.all_to_all(spread, axes, split_axis=0, concat_axis=0, tiled=True)  15.1 us
    dot_general x1, matrix products, expert_from_cot(): lax.dot_general(grad_up_pre, up_matrix, contract_cols, preferred_element_...  12.3 us
    dot_general x1, matrix products, expert_from_cot(): lax.dot_general(scaled_cot, down_matrix, contract_cols, preferred_element...  11.4 us
    dot_general x1, matrix products, expert_from_cot(): jnp.dot(hidden, down_matrix, preferred_element_type=jnp.float32)  9.93 us
  transfers between devices with their start and end apart: 7, of which 4 were waited for; matrix products, arithmetic and copies ran while one was open for 25% of the time, Pallas kernels for 0%

profile of v5, /device:TPU:0, one launch (start us, length us, event | category | flops | bytes accessed | tf_op | source)
XLA Modules:
  0.0 483.0 jit_solution(5454829992675713506)
XLA Ops:
  6.2 7.3 %all-to-all-start = ((bf16[32,1,36]{2,1,0:T(2,128)(2,1)}), bf16[32,1,36]{2,1,0:T(2,128)(2,1)S(1)}, u32[]{:S(2)}, u32[]{:S(2)}) async-start(bf16[32,1,36]{2,1,0:T(2,128)(2,1)} %all_to_all.44), calls=%async_computation | async-start | bytes 32768 | tf_op jit(solution)/shard_map/all_to_all | solution.py:187
  13.7 6.8 %fusion.33 = bf16[1152,128]{1,0:T(8,128)(2,1)} fusion(s32[128,8]{0,1:T(8,128)S(1)} %multiply_add_fusion.1), kind=kLoop, calls=%fused_computation.52 | loop fusion | flops 3391488 | bytes 299008 | tf_op jit(solution)/shard_map/reduce_sum | solution.py:29
  21.5 4.9 %convolution_convert_fusion.2 = bf16[32,36,2048]{2,1,0:T(8,128)(2,1)} fusion(bf16[32,36,128]{2,1,0:T(8,128)(2,1)S(1)} %reshape.129, bf16[128,2048]{1,0:T(8,128)(2,1)} %param.10), kind=kOutput, calls=%fused_computation.22 | convolution fusion | flops 606339072 | bytes 5537792 | tf_op jit(solution)/shard_map/dot_general | solution.py:190
  26.3 5.9 %all-to-all-start.1 = ((bf16[32,36,2048]{2,1,0:T(8,128)(2,1)}), bf16[32,36,2048]{2,1,0:T(8,128)(2,1)}, u32[]{:S(2)}, u32[]{:S(2)}) async-start(bf16[32,36,2048]{2,1,0:T(8,128)(2,1)} %convolution_convert_fusion.2), calls=%async_computation.1 | async-start | bytes 10485760 | tf_op jit(solution)/shard_map/all_to_all | solution.py:194
  32.3 4.8 %convolution_convert_fusion.1 = bf16[32,36,2048]{2,1,0:T(8,128)(2,1)} fusion(bf16[32,36,128]{2,1,0:T(8,128)(2,1)S(1)} %reshape.129, bf16[128,2048]{1,0:T(8,128)(2,1)} %param.9), kind=kOutput, calls=%fused_computation.21 | convolution fusion | flops 606339072 | bytes 5537792 | tf_op jit(solution)/shard_map/dot_general | solution.py:195
  37.1 112.7 %all-to-all-done.1 = bf16[32,36,2048]{2,1,0:T(8,128)(2,1)} async-done(((bf16[32,36,2048]{2,1,0:T(8,128)(2,1)}), bf16[32,36,2048]{2,1,0:T(8,128)(2,1)}, u32[]{:S(2)}, u32[]{:S(2)}) %all-to-all-start.1) | async-done | bytes 4718624 | tf_op jit(solution)/shard_map/all_to_all | solution.py:194
  153.7 8.0 %reshape.135 = f32[1152,2048]{1,0:T(8,128)} reshape(bf16[32,36,2048]{2,1,0:T(8,128)(2,1)} %all-to-all-done.1) | data formatting | bytes 14155776 | tf_op jit(solution)/shard_map/convert_element_type | solution.py:141
  161.7 5.8 %multiply_convert_fusion = bf16[32,36,2048]{2,1,0:T(8,128)(2,1)} fusion(f32[32,36]{1,0:T(8,128)S(1)} %convert_element_type.129, bf16[32,36,2048]{2,1,0:T(8,128)(2,1)} %all-to-all-done.1), kind=kLoop, calls=%fused_computation | loop fusion | flops 7077888 | bytes 9441792 | tf_op jit(solution)/shard_map/convert_element_type | solution.py:141
  167.5 7.2 %convert_element_type.133 = bf16[1152,2048]{1,0:T(8,128)(2,1)} reshape(bf16[32,36,2048]{2,1,0:T(8,128)(2,1)} %multiply_convert_fusion) | data formatting | bytes 9437184 | tf_op jit(solution)/shard_map/convert_element_type | solution.py:141
  174.7 9.9 %multiply_reduce_fusion = bf16[1152]{0:T(1024)(128)(2,1)S(1)} fusion(f32[1152,2048]{1,0:T(8,128)} %reshape.135, bf16[1,768,2048]{2,1,0:T(8,128)(2,1)} %param.17, bf16[1,1152,768]{2,1,0:T(8,128)(2,1)} %param.14, bf16[1,1152,768]{2,1,0:T(8,128)(2,1)} %param.13), kind=kOutput, calls=%fused_computation.1 | convolution fusion | flops 3640392704 | bytes 16124160 | tf_op jit(solution)/shard_map/dot_general | solution.py:138
  184.8 86.4 %all-to-all-done.2 = bf16[32,36,2048]{2,1,0:T(8,128)(2,1)} async-done(((bf16[32,36,2048]{2,1,0:T(8,128)(2,1)}), bf16[32,36,2048]{2,1,0:T(8,128)(2,1)}, u32[]{:S(2)}, u32[]{:S(2)}) %all-to-all-start.2) | async-done | bytes 4718624 | tf_op jit(solution)/shard_map/all_to_all | solution.py:199
  274.3 11.4 %fusion.12 = (bf16[1152,768]{1,0:T(8,128)(2,1)}, f32[1152,768]{1,0:T(8,128)}) fusion(bf16[1,1152,768]{2,1,0:T(8,128)(2,1)} %param.14, bf16[1,1152,768]{2,1,0:T(8,128)(2,1)} %param.13, bf16[1152,2048]{1,0:T(8,128)(2,1)} %convert_element_type.133, bf16[1,768,2048]{2,1,0:T(8,128)(2,1)} %param.17), kind=kOutput, calls=%fused_computation.26 | convolution fusion | flops 3634495488 | bytes 16711680 | tf_op jit(solution)/shard_map/dot_general | solution.py:144
  286.5 6.6 %fusion.6 = f32[1,128,8]{2,0,1:T(1,128)S(1)} fusion(bf16[1152,1,1]{0,1,2:T(2,128)(2,1)} %reshape.140, s32[1024]{0:T(1024)S(1)} %multiply_add_fusion), kind=kOutput, calls=%fused_computation.16 | convolution fusion | flops 3538944 | bytes 10496 | tf_op jit(solution)/shard_map/dot_general | solution.py:214
  299.9 6.0 %all-to-all-start.4 = ((f32[32,1,2048]{2,1,0:T(1,128)}), f32[32,1,2048]{2,1,0:T(1,128)}, u32[]{:S(2)}, u32[]{:S(2)}) async-start(f32[32,1,2048]{2,1,0:T(1,128)} %all_to_all.45), calls=%async_computation.4 | async-start | bytes 524288 | tf_op jit(solution)/shard_map/all_to_all | solution.py:228
  305.9 7.7 %fusion.24 = f32[1152,2048]{1,0:T(8,128)} fusion(bf16[1152,768]{1,0:T(8,128)(2,1)} %get-tuple-element.46, bf16[1,2048,768]{2,1,0:T(8,128)(2,1)S(1)} %copy-done), kind=kOutput, calls=%fused_computation.41 | convolution fusion | flops 3623878656 | bytes 14352384 | tf_op jit(solution)/shard_map/dot_general | solution.py:152
  318.2 15.1 %all-to-all-start.5 = ((f32[32,1,2048]{2,1,0:T(1,128)}), f32[32,1,2048]{2,1,0:T(1,128)S(1)}, u32[]{:S(2)}, u32[]{:S(2)}) async-start(f32[32,1,2048]{2,1,0:T(1,128)} %broadcast_in_dim.33), calls=%async_computation.5 | async-start | bytes 524288 | tf_op jit(solution)/shard_map/all_to_all | solution.py:231
  333.3 12.3 %add_convert_fusion = bf16[1152,2048]{1,0:T(8,128)(2,1)} fusion(f32[1152,2048]{1,0:T(8,128)} %fusion.24, bf16[1,2048,768]{2,1,0:T(8,128)(2,1)} %param.16, f32[1152,768]{1,0:T(8,128)} %get-tuple-element.47, bf16[1,1152,768]{2,1,0:T(8,128)(2,1)} %param.13), kind=kOutput, calls=%fused_computation.2 | convolution fusion | flops 3634790400 | bytes 22609920 | tf_op jit(solution)/shard_map/dot_general | solution.py:155
  345.6 7.2 %reshape.130 = bf16[32,36,2048]{2,1,0:T(8,128)(2,1)} reshape(bf16[1152,2048]{1,0:T(8,128)(2,1)} %add_convert_fusion) | data formatting | bytes 9437184 | tf_op jit(solution)/shard_map/reshape | solution.py:233
  354.9 5.8 %all-to-all-start.6 = ((bf16[32,36,2048]{2,1,0:T(8,128)(2,1)}), bf16[32,36,2048]{2,1,0:T(8,128)(2,1)}, u32[]{:S(2)}, u32[]{:S(2)}) async-start(bf16[32,36,2048]{2,1,0:T(8,128)(2,1)} %reshape.130), calls=%async_computation.6 | async-start | bytes 10485760 | tf_op jit(solution)/shard_map/all_to_all | solution.py:235
  360.8 9.1 %fusion.31 = bf16[1,768,2048]{2,1,0:T(8,128)(2,1)} fusion(bf16[1152,2048]{1,0:T(8,128)(2,1)} %convert_element_type.133, bf16[1,1152,768]{2,1,0:T(8,128)(2,1)S(1)} %copy-done.5, bf16[1,1152,768]{2,1,0:T(8,128)(2,1)} %param.13), kind=kOutput, calls=%fused_computation.48 | convolution fusion | flops 3632529408 | bytes 11403264 | tf_op jit(solution)/shard_map/dot_general | solution.py:157
  369.9 7.2 %reshape.132 = bf16[1152,2048]{1,0:T(8,128)(2,1)} reshape(bf16[32,36,2048]{2,1,0:T(8,128)(2,1)} %all-to-all-done.2) | data formatting | bytes 9437184 | tf_op jit(solution)/shard_map/reshape | solution.py:236
  377.1 9.1 %fusion.29 = bf16[1,2048,768]{2,1,0:T(8,128)(2,1)} fusion(bf16[1152,2048]{1,0:T(8,128)(2,1)} %reshape.132, bf16[1152,768]{1,0:T(8,128)(2,1)} %get-tuple-element.46), kind=kOutput, calls=%fused_computation.46 | convolution fusion | flops 3625451520 | bytes 9633792 | tf_op jit(solution)/shard_map/dot_general | solution.py:237
  386.2 6.3 %fusion.30 = bf16[1,2048,768]{2,1,0:T(8,128)(2,1)} fusion(bf16[1152,2048]{1,0:T(8,128)(2,1)S(1)} %copy-done.2, f32[1152,768]{1,0:T(8,128)S(1)} %copy-done.7, bf16[1,1152,768]{2,1,0:T(8,128)(2,1)S(1)} %copy-done.6), kind=kOutput, calls=%fused_computation.47 | convolution fusion | flops 3631644672 | bytes 13172736 | tf_op jit(solution)/shard_map/dot_general | solution.py:240
  394.9 83.4 %all-to-all-done.6 = bf16[32,36,2048]{2,1,0:T(8,128)(2,1)} async-done(((bf16[32,36,2048]{2,1,0:T(8,128)(2,1)}), bf16[32,36,2048]{2,1,0:T(8,128)(2,1)}, u32[]{:S(2)}, u32[]{:S(2)}) %all-to-all-start.6) | async-done | bytes 4718624 | tf_op jit(solution)/shard_map/all_to_all | solution.py:235
  (58 shorter events, 34.9 us)
Async XLA Ops:
  0.6 305.2 %copy-start = (bf16[1,2048,768]{2,1,0:T(8,128)(2,1)S(1)}, bf16[1,2048,768]{2,1,0:T(8,128)(2,1)}, u32[]{:S(2)}) copy-start(bf16[1,2048,768]{2,1,0:T(8,128)(2,1)} %param.15) | copy-start | bytes 9437188
  0.6 13.0 %copy-start.4 = (s32[128,8]{0,1:T(8,128)S(1)}, s32[128,8]{0,1:T(8,128)}, u32[]{:S(2)}) copy-start(s32[128,8]{0,1:T(8,128)} %param.11) | copy-start | bytes 12292
  6.2 20.1 %all-to-all-start = ((bf16[32,1,36]{2,1,0:T(2,128)(2,1)}), bf16[32,1,36]{2,1,0:T(2,128)(2,1)S(1)}, u32[]{:S(2)}, u32[]{:S(2)}) async-start(bf16[32,1,36]{2,1,0:T(2,128)(2,1)} %all_to_all.44), calls=%async_computation | async-start | bytes 32768 | tf_op jit(solution)/shard_map/all_to_all | solution.py:187
  26.3 123.5 %all-to-all-start.1 = ((bf16[32,36,2048]{2,1,0:T(8,128)(2,1)}), bf16[32,36,2048]{2,1,0:T(8,128)(2,1)}, u32[]{:S(2)}, u32[]{:S(2)}) async-start(bf16[32,36,2048]{2,1,0:T(8,128)(2,1)} %convolution_convert_fusion.2), calls=%async_computation.1 | async-start | bytes 10485760 | tf_op jit(solution)/shard_map/all_to_all | solution.py:194
  149.8 121.4 %all-to-all-start.2 = ((bf16[32,36,2048]{2,1,0:T(8,128)(2,1)}), bf16[32,36,2048]{2,1,0:T(8,128)(2,1)}, u32[]{:S(2)}, u32[]{:S(2)}) async-start(bf16[32,36,2048]{2,1,0:T(8,128)(2,1)} %convolution_convert_fusion.1), calls=%async_computation.2 | async-start | bytes 10485760 | tf_op jit(solution)/shard_map/all_to_all | solution.py:199
  271.8 14.0 %all-to-all-start.3 = ((bf16[32,1,36]{2,1,0:T(2,128)(2,1)}), bf16[32,1,36]{2,1,0:T(2,128)(2,1)S(1)}, u32[]{:S(2)}, u32[]{:S(2)}) async-start(bf16[32,1,36]{2,1,0:T(2,128)(2,1)} %copy.56), calls=%async_computation.3 | async-start | bytes 32768 | tf_op jit(solution)/shard_map/all_to_all | solution.py:212
  299.9 16.3 %all-to-all-start.4 = ((f32[32,1,2048]{2,1,0:T(1,128)}), f32[32,1,2048]{2,1,0:T(1,128)}, u32[]{:S(2)}, u32[]{:S(2)}) async-start(f32[32,1,2048]{2,1,0:T(1,128)} %all_to_all.45), calls=%async_computation.4 | async-start | bytes 524288 | tf_op jit(solution)/shard_map/all_to_all | solution.py:228
  318.2 34.7 %all-to-all-start.5 = ((f32[32,1,2048]{2,1,0:T(1,128)}), f32[32,1,2048]{2,1,0:T(1,128)S(1)}, u32[]{:S(2)}, u32[]{:S(2)}) async-start(f32[32,1,2048]{2,1,0:T(1,128)} %broadcast_in_dim.33), calls=%async_computation.5 | async-start | bytes 524288 | tf_op jit(solution)/shard_map/all_to_all | solution.py:231
  354.9 5.8 %copy-start.5 = (bf16[1,1152,768]{2,1,0:T(8,128)(2,1)S(1)}, bf16[1,1152,768]{2,1,0:T(8,128)(2,1)}, u32[]{:S(2)}) copy-start(bf16[1,1152,768]{2,1,0:T(8,128)(2,1)} %param.14) | copy-start | bytes 5308420
  354.9 123.3 %all-to-all-start.6 = ((bf16[32,36,2048]{2,1,0:T(8,128)(2,1)}), bf16[32,36,2048]{2,1,0:T(8,128)(2,1)}, u32[]{:S(2)}, u32[]{:S(2)}) async-start(bf16[32,36,2048]{2,1,0:T(8,128)(2,1)} %reshape.130), calls=%async_computation.6 | async-start | bytes 10485760 | tf_op jit(solution)/shard_map/all_to_all | solution.py:235
  377.1 9.1 %copy-start.2 = (bf16[1152,2048]{1,0:T(8,128)(2,1)S(1)}, bf16[1152,2048]{1,0:T(8,128)(2,1)}, u32[]{:S(2)}) copy-start(bf16[1152,2048]{1,0:T(8,128)(2,1)} %reshape.132) | copy-start | bytes 14155780
  377.1 9.1 %copy-start.6 = (bf16[1,1152,768]{2,1,0:T(8,128)(2,1)S(1)}, bf16[1,1152,768]{2,1,0:T(8,128)(2,1)}, u32[]{:S(2)}) copy-start(bf16[1,1152,768]{2,1,0:T(8,128)(2,1)} %param.13) | copy-start | bytes 5308420
  377.1 9.1 %copy-start.7 = (f32[1152,768]{1,0:T(8,128)S(1)}, f32[1152,768]{1,0:T(8,128)}, u32[]{:S(2)}) copy-start(f32[1152,768]{1,0:T(8,128)} %get-tuple-element.47) | copy-start | bytes 10616836
  392.5 90.3 %copy-start.1 = (bf16[1,2048,768]{2,1,0:T(8,128)(2,1)S(1)}, bf16[1,2048,768]{2,1,0:T(8,128)(2,1)}, u32[]{:S(2)}) copy-start(bf16[1,2048,768]{2,1,0:T(8,128)(2,1)} %param.15) | copy-start | bytes 9437188
  478.3 3.4 copy-start.3

commit v6 on v5

--- a/solution.py
+++ b/solution.py
@@ -130,32 +130,33 @@
 
 
 def expert_from_cot(cot_rows, weight_rows, gate_pre, up_pre, gate_matrix, up_matrix, down_matrix):
+    last = (((2,), (0,)), ((), ()))
+    last_t = (((2,), (1,)), ((), ()))
+    grid_rows = (((0, 1), (0, 1)), ((), ()))
     gate_value = gate_pre.astype(jnp.float32)
     up_value = up_pre.astype(jnp.float32)
     sigmoid_gate = jax.nn.sigmoid(gate_value)
     silu_gate = gate_value * sigmoid_gate
     hidden = (silu_gate * up_value).astype(jnp.bfloat16)
-    expert_out = jnp.dot(hidden, down_matrix, preferred_element_type=jnp.float32).astype(
-        jnp.bfloat16
-    )
-    scaled_cot = (weight_rows.astype(jnp.float32)[:, None] * cot_rows.astype(jnp.float32)).astype(
-        jnp.bfloat16
-    )
+    expert_out = lax.dot_general(
+        hidden, down_matrix, last, preferred_element_type=jnp.float32
+    ).astype(jnp.bfloat16)
+    scaled_cot = (
+        weight_rows.astype(jnp.float32)[:, :, None] * cot_rows.astype(jnp.float32)
+    ).astype(jnp.bfloat16)
     grad_hidden = lax.dot_general(
-        scaled_cot, down_matrix, contract_cols, preferred_element_type=jnp.float32
+        scaled_cot, down_matrix, last_t, preferred_element_type=jnp.float32
     )
     grad_gate_pre = (
         grad_hidden * up_value * sigmoid_gate * (1.0 + gate_value * (1.0 - sigmoid_gate))
     ).astype(jnp.bfloat16)
     grad_up_pre = (grad_hidden * silu_gate).astype(jnp.bfloat16)
     grad_rows = (
-        lax.dot_general(
-            grad_gate_pre, gate_matrix, contract_cols, preferred_element_type=jnp.float32
-        )
-        + lax.dot_general(grad_up_pre, up_matrix, contract_cols, preferred_element_type=jnp.float32)
+        lax.dot_general(grad_gate_pre, gate_matrix, last_t, preferred_element_type=jnp.float32)
+        + lax.dot_general(grad_up_pre, up_matrix, last_t, preferred_element_type=jnp.float32)
     ).astype(jnp.bfloat16)
     grad_down_w = lax.dot_general(
-        hidden, scaled_cot, contract_rows, preferred_element_type=jnp.float32
+        hidden, scaled_cot, grid_rows, preferred_element_type=jnp.float32
     ).astype(jnp.bfloat16)
     return (grad_rows, expert_out, grad_gate_pre, grad_up_pre, grad_down_w)
 
@@ -197,17 +198,19 @@
     )
     got_cot, grid_tokens = lax.optimization_barrier((got_cot, grid_tokens))
     got_tokens = lax.all_to_all(grid_tokens, axes, split_axis=0, concat_axis=0, tiled=True)
-    cot_rows = got_cot.reshape(-1, width)
+    cot_rows = got_cot
     grad_rows, expert_out, grad_gate_pre, grad_up_pre, grad_down_w = expert_from_cot(
         cot_rows,
-        got_weight.reshape(-1),
-        gate_saved[0],
-        up_saved[0],
+        got_weight,
+        gate_saved[0].reshape(experts, capacity, -1),
+        up_saved[0].reshape(experts, capacity, -1),
         gate_weight[0],
         up_weight[0],
         down_weight[0],
     )
-    slot_route_dot = slot_dot(cot_rows, expert_out).reshape(experts, capacity)
+    slot_route_dot = jnp.sum(
+        cot_rows.astype(jnp.float32) * expert_out.astype(jnp.float32), axis=2
+    ).astype(jnp.bfloat16)
     slot_route_dot, got_tokens = lax.optimization_barrier((slot_route_dot, got_tokens))
     back_dot = lax.all_to_all(slot_route_dot, axes, split_axis=0, concat_axis=0, tiled=True)
     route_dot = back_dot.reshape(-1)
@@ -230,15 +233,16 @@
     spread = jnp.broadcast_to(chunk_sum, part_rows.shape)
     got_sums = lax.all_to_all(spread, axes, split_axis=0, concat_axis=0, tiled=True)
     grad_router = got_sums.reshape(router_part.shape) * (1.0 / math.sqrt(total_tokens))
-    back_grad = grad_rows.reshape(experts, capacity, width)
+    back_grad = grad_rows
     back_grad, grad_router = lax.optimization_barrier((back_grad, grad_router))
     back_rows = lax.all_to_all(back_grad, axes, split_axis=0, concat_axis=0, tiled=True)
-    input_rows = got_tokens.reshape(-1, width)
+    input_rows = got_tokens
+    grid_rows = (((0, 1), (0, 1)), ((), ()))
     grad_gate_w = lax.dot_general(
-        input_rows, grad_gate_pre, contract_rows, preferred_element_type=jnp.float32
+        input_rows, grad_gate_pre, grid_rows, preferred_element_type=jnp.float32
     ).astype(jnp.bfloat16)
     grad_up_w = lax.dot_general(
-        input_rows, grad_up_pre, contract_rows, preferred_element_type=jnp.float32
+        input_rows, grad_up_pre, grid_rows, preferred_element_type=jnp.float32
     ).astype(jnp.bfloat16)
     grad_sum = lax.dot_general(
         grid_table, back_rows, (((0, 1), (0, 1)), ((), ())), preferred_element_type=jnp.float32

time: 485 us -> 475 us (0.979); the launches traced: 483 us -> 468 us
  local copies, waits for them, and re-layouts: 43.6 us -> 25.2 us
  starting transfers between devices: 46.6 us -> 36.6 us
  waiting for transfers between devices: 285 us -> 295 us
    reshape x2 -> x0, local copies, waits for them, and re-layouts: 14.5 us -> none  [the longest x1 7.25 us: body(): input_rows = got_tokens.reshape(-1, width)]
    all_to_all x1, starting transfers between devices: 15.1 us -> 4.07 us  [body(): lax.all_to_all(spread, axes, split_axis=0, concat_axis=0, tiled=True)]
    all_to_all x1, waiting for transfers between devices: 86.4 us -> 93.3 us  [body(): lax.all_to_all(grid_tokens, axes, split_axis=0, concat_axis=0, tiled=True)]
  transfers between devices with their start and end apart: 7 -> 7, of which waited for: 4 -> 4; matrix products, arithmetic and copies ran while one was open for 25% -> 23% of each run, Pallas kernels for 0% -> 0%
where the time goes in v6:
time: 475 us; the launch traced here: 468 us
  waiting for transfers between devices  295 us (62%)
  matrix products  95.9 us (20%)
  starting transfers between devices  36.6 us (8%)
  local copies, waits for them, and re-layouts  25.2 us (5%)
  other arithmetic  14.5 us (3%)
    all_to_all x1, waiting for transfers between devices, body(): lax.all_to_all(grid_cot, axes, split_axis=0, concat_axis=0, tiled=True)  113 us
    all_to_all x1, waiting for transfers between devices, body(): lax.all_to_all(grid_tokens, axes, split_axis=0, concat_axis=0, tiled=True)  93.3 us
    all_to_all x1, waiting for transfers between devices, body(): lax.all_to_all(back_grad, axes, split_axis=0, concat_axis=0, tiled=True)  86.9 us
    dot_general x1, matrix products, expert_from_cot(): lax.dot_general(scaled_cot, down_matrix, last_t, preferred_element_type=j...  13.1 us
    dot_general x1, matrix products, expert_from_cot(): lax.dot_general(grad_up_pre, up_matrix, last_t, preferred_element_type=jn...  12.2 us
    dot_general x1, matrix products, expert_from_cot(): lax.dot_general(hidden, scaled_cot, grid_rows, preferred_element_type=jnp...  11.5 us
  transfers between devices with their start and end apart: 7, of which 4 were waited for; matrix products, arithmetic and copies ran while one was open for 23% of the time, Pallas kernels for 0%

profile of v6, /device:TPU:0, one launch (start us, length us, event | category | flops | bytes accessed | tf_op | source)
XLA Modules:
  0.0 468.1 jit_solution(17225965892688839001)
XLA Ops:
  6.2 7.3 %all-to-all-start = ((bf16[32,1,36]{2,1,0:T(2,128)(2,1)}), bf16[32,1,36]{2,1,0:T(2,128)(2,1)S(1)}, u32[]{:S(2)}, u32[]{:S(2)}) async-start(bf16[32,1,36]{2,1,0:T(2,128)(2,1)} %all_to_all.44), calls=%async_computation | async-start | bytes 32768 | tf_op jit(solution)/shard_map/all_to_all | solution.py:188
  14.4 6.7 %fusion.26 = bf16[1152,128]{1,0:T(8,128)(2,1)} fusion(s32[128,8]{0,1:T(8,128)S(1)} %multiply_add_fusion.1), kind=kLoop, calls=%fused_computation.38 | loop fusion | flops 3391488 | bytes 299008 | tf_op jit(solution)/shard_map/reduce_sum | solution.py:29
  22.1 4.9 %convolution_convert_fusion.1 = bf16[32,36,2048]{2,1,0:T(8,128)(2,1)} fusion(bf16[32,36,128]{2,1,0:T(8,128)(2,1)S(1)} %reshape.100, bf16[128,2048]{1,0:T(8,128)(2,1)} %param.10), kind=kOutput, calls=%fused_computation.20 | convolution fusion | flops 606339072 | bytes 5537792 | tf_op jit(solution)/shard_map/dot_general | solution.py:191
  27.0 5.9 %all-to-all-start.1 = ((bf16[32,36,2048]{2,1,0:T(8,128)(2,1)}), bf16[32,36,2048]{2,1,0:T(8,128)(2,1)}, u32[]{:S(2)}, u32[]{:S(2)}) async-start(bf16[32,36,2048]{2,1,0:T(8,128)(2,1)} %convolution_convert_fusion.1), calls=%async_computation.1 | async-start | bytes 10485760 | tf_op jit(solution)/shard_map/all_to_all | solution.py:195
  33.0 4.9 %convolution_convert_fusion = bf16[32,36,2048]{2,1,0:T(8,128)(2,1)} fusion(bf16[32,36,128]{2,1,0:T(8,128)(2,1)S(1)} %reshape.100, bf16[128,2048]{1,0:T(8,128)(2,1)} %param.9), kind=kOutput, calls=%fused_computation.19 | convolution fusion | flops 606339072 | bytes 5537792 | tf_op jit(solution)/shard_map/dot_general | solution.py:196
  37.9 112.6 %all-to-all-done.1 = bf16[32,36,2048]{2,1,0:T(8,128)(2,1)} async-done(((bf16[32,36,2048]{2,1,0:T(8,128)(2,1)}), bf16[32,36,2048]{2,1,0:T(8,128)(2,1)}, u32[]{:S(2)}, u32[]{:S(2)}) %all-to-all-start.1) | async-done | bytes 4718624 | tf_op jit(solution)/shard_map/all_to_all | solution.py:195
  150.5 4.1 all-to-all-start.2
  154.6 3.9 reshape.103
  158.5 3.9 reshape.102
  162.4 4.3 multiply_convert_fusion.3
  166.7 3.6 convert_element_type.123
  170.3 8.5 %fusion.1 = bf16[32,36]{1,0:T(8,128)(2,1)S(1)} fusion(bf16[32,36,2048]{2,1,0:T(8,128)(2,1)} %all-to-all-done.1, bf16[32,36,768]{2,1,0:T(8,128)(2,1)} %convert_element_type.123, bf16[1,768,2048]{2,1,0:T(8,128)(2,1)} %param.17), kind=kOutput, calls=%fused_computation.3 | convolution fusion | flops 3635674112 | bytes 9636096 | tf_op jit(solution)/shard_map/dot_general | solution.py:141
  178.8 93.3 %all-to-all-done.2 = bf16[32,36,2048]{2,1,0:T(8,128)(2,1)} async-done(((bf16[32,36,2048]{2,1,0:T(8,128)(2,1)}), bf16[32,36,2048]{2,1,0:T(8,128)(2,1)}, u32[]{:S(2)}, u32[]{:S(2)}) %all-to-all-start.2) | async-done | bytes 4718624 | tf_op jit(solution)/shard_map/all_to_all | solution.py:200
  275.5 13.1 %multiply_convert_fusion.1 = (bf16[32,36,768]{2,1,0:T(8,128)(2,1)}, bf16[32,36,768]{2,1,0:T(8,128)(2,1)}) fusion(f32[32,36,768]{2,1,0:T(8,128)} %reshape.103, f32[32,36,768]{2,1,0:T(8,128)} %reshape.102, bf16[1,768,2048]{2,1,0:T(8,128)(2,1)} %param.17, bf16[32,36,2048]{2,1,0:T(8,128)(2,1)} %all-to-all-done.1, f32[32,36]{1,0:T(8,128)S(1)} %convert_element_type.109), kind=kOutput, calls=%fused_computation.22 | convolution fusion | flops 3642458112 | bytes 18485760 | tf_op jit(solution)/shard_map/dot_general | solution.py:147
  289.3 6.6 %fusion.5 = f32[1,128,8]{2,0,1:T(1,128)S(1)} fusion(bf16[1152,1,1]{0,1,2:T(2,128)(2,1)} %reshape.111, s32[1024]{0:T(1024)S(1)} %multiply_add_fusion), kind=kOutput, calls=%fused_computation.14 | convolution fusion | flops 3538944 | bytes 10496 | tf_op jit(solution)/shard_map/dot_general | solution.py:217
  302.7 6.3 %all-to-all-start.4 = ((f32[32,1,2048]{2,1,0:T(1,128)}), f32[32,1,2048]{2,1,0:T(1,128)}, u32[]{:S(2)}, u32[]{:S(2)}) async-start(f32[32,1,2048]{2,1,0:T(1,128)} %all_to_all.45), calls=%async_computation.4 | async-start | bytes 524288 | tf_op jit(solution)/shard_map/all_to_all | solution.py:231
  309.0 8.5 %fusion.16 = f32[32,36,2048]{2,1,0:T(8,128)} fusion(bf16[32,36,768]{2,1,0:T(8,128)(2,1)} %get-tuple-element.47, bf16[1,2048,768]{2,1,0:T(8,128)(2,1)S(1)} %copy-done), kind=kOutput, calls=%fused_computation.28 | convolution fusion | flops 3623878656 | bytes 14352384 | tf_op jit(solution)/shard_map/dot_general | solution.py:155
  321.3 4.1 all-to-all-start.5
  325.3 12.2 %add_convert_fusion = bf16[32,36,2048]{2,1,0:T(8,128)(2,1)} fusion(f32[32,36,2048]{2,1,0:T(8,128)} %fusion.16, bf16[32,36,768]{2,1,0:T(8,128)(2,1)} %get-tuple-element.46, bf16[1,2048,768]{2,1,0:T(8,128)(2,1)} %param.16), kind=kOutput, calls=%fused_computation.4 | convolution fusion | flops 3628597248 | bytes 19070976 | tf_op jit(solution)/shard_map/dot_general | solution.py:156
  339.6 6.2 %all-to-all-start.6 = ((bf16[32,36,2048]{2,1,0:T(8,128)(2,1)}), bf16[32,36,2048]{2,1,0:T(8,128)(2,1)}, u32[]{:S(2)}, u32[]{:S(2)}) async-start(bf16[32,36,2048]{2,1,0:T(8,128)(2,1)} %add_convert_fusion), calls=%async_computation.6 | async-start | bytes 10485760 | tf_op jit(solution)/shard_map/all_to_all | solution.py:238
  345.8 11.5 %fusion.22 = bf16[1,768,2048]{2,1,0:T(8,128)(2,1)} fusion(bf16[32,36,2048]{2,1,0:T(8,128)(2,1)} %all-to-all-done.1, f32[32,36]{1,0:T(8,128)S(1)} %copy-done.5, f32[32,36,768]{2,1,0:T(8,128)} %reshape.102, f32[32,36,768]{2,1,0:T(8,128)} %reshape.103), kind=kOutput, calls=%fused_computation.34 | convolution fusion | flops 3637837824 | bytes 14946816 | tf_op jit(solution)/shard_map/dot_general | solution.py:158
  357.3 8.4 %fusion.21 = bf16[1,2048,768]{2,1,0:T(8,128)(2,1)} fusion(bf16[32,36,2048]{2,1,0:T(8,128)(2,1)} %all-to-all-done.2, bf16[32,36,768]{2,1,0:T(8,128)(2,1)S(1)} %copy-done.6), kind=kOutput, calls=%fused_computation.33 | convolution fusion | flops 3625451520 | bytes 9633792 | tf_op jit(solution)/shard_map/dot_general | solution.py:244
  365.7 8.3 %fusion.20 = bf16[1,2048,768]{2,1,0:T(8,128)(2,1)} fusion(bf16[32,36,2048]{2,1,0:T(8,128)(2,1)} %all-to-all-done.2, bf16[32,36,768]{2,1,0:T(8,128)(2,1)S(1)} %copy-done.7), kind=kOutput, calls=%fused_computation.32 | convolution fusion | flops 3625451520 | bytes 9633792 | tf_op jit(solution)/shard_map/dot_general | solution.py:241
  376.4 86.9 %all-to-all-done.6 = bf16[32,36,2048]{2,1,0:T(8,128)(2,1)} async-done(((bf16[32,36,2048]{2,1,0:T(8,128)(2,1)}), bf16[32,36,2048]{2,1,0:T(8,128)(2,1)}, u32[]{:S(2)}, u32[]{:S(2)}) %all-to-all-start.6) | async-done | bytes 4718624 | tf_op jit(solution)/shard_map/all_to_all | solution.py:238
  (56 shorter events, 31.1 us)
Async XLA Ops:
  0.6 308.3 %copy-start = (bf16[1,2048,768]{2,1,0:T(8,128)(2,1)S(1)}, bf16[1,2048,768]{2,1,0:T(8,128)(2,1)}, u32[]{:S(2)}) copy-start(bf16[1,2048,768]{2,1,0:T(8,128)(2,1)} %param.15) | copy-start | bytes 9437188
  6.2 20.8 %all-to-all-start = ((bf16[32,1,36]{2,1,0:T(2,128)(2,1)}), bf16[32,1,36]{2,1,0:T(2,128)(2,1)S(1)}, u32[]{:S(2)}, u32[]{:S(2)}) async-start(bf16[32,1,36]{2,1,0:T(2,128)(2,1)} %all_to_all.44), calls=%async_computation | async-start | bytes 32768 | tf_op jit(solution)/shard_map/all_to_all | solution.py:188
  27.0 123.5 %all-to-all-start.1 = ((bf16[32,36,2048]{2,1,0:T(8,128)(2,1)}), bf16[32,36,2048]{2,1,0:T(8,128)(2,1)}, u32[]{:S(2)}, u32[]{:S(2)}) async-start(bf16[32,36,2048]{2,1,0:T(8,128)(2,1)} %convolution_convert_fusion.1), calls=%async_computation.1 | async-start | bytes 10485760 | tf_op jit(solution)/shard_map/all_to_all | solution.py:195
  150.5 121.6 %all-to-all-start.2 = ((bf16[32,36,2048]{2,1,0:T(8,128)(2,1)}), bf16[32,36,2048]{2,1,0:T(8,128)(2,1)}, u32[]{:S(2)}, u32[]{:S(2)}) async-start(bf16[32,36,2048]{2,1,0:T(8,128)(2,1)} %convolution_convert_fusion), calls=%async_computation.2 | async-start | bytes 10485760 | tf_op jit(solution)/shard_map/all_to_all | solution.py:200
  170.3 105.1 %copy-start.4 = (f32[32,36]{1,0:T(8,128)}, f32[32,36]{1,0:T(8,128)S(1)}, u32[]{:S(2)}) copy-start(f32[32,36]{1,0:T(8,128)S(1)} %convert_element_type.109) | copy-start | bytes 13828
  272.7 15.8 %all-to-all-start.3 = ((bf16[32,1,36]{2,1,0:T(2,128)(2,1)}), bf16[32,1,36]{2,1,0:T(2,128)(2,1)S(1)}, u32[]{:S(2)}, u32[]{:S(2)}) async-start(bf16[32,1,36]{2,1,0:T(2,128)(2,1)} %copy.56), calls=%async_computation.3 | async-start | bytes 32768 | tf_op jit(solution)/shard_map/all_to_all | solution.py:215
  275.5 20.6 %copy-start.3 = (s32[128,8]{0,1:T(8,128)S(1)}, s32[128,8]{0,1:T(8,128)}, u32[]{:S(2)}) copy-start(s32[128,8]{0,1:T(8,128)} %param.11) | copy-start | bytes 12292
  302.7 16.6 %all-to-all-start.4 = ((f32[32,1,2048]{2,1,0:T(1,128)}), f32[32,1,2048]{2,1,0:T(1,128)}, u32[]{:S(2)}, u32[]{:S(2)}) async-start(f32[32,1,2048]{2,1,0:T(1,128)} %all_to_all.45), calls=%async_computation.4 | async-start | bytes 524288 | tf_op jit(solution)/shard_map/all_to_all | solution.py:231
  321.3 16.2 %all-to-all-start.5 = ((f32[32,1,2048]{2,1,0:T(1,128)}), f32[32,1,2048]{2,1,0:T(1,128)S(1)}, u32[]{:S(2)}, u32[]{:S(2)}) async-start(f32[32,1,2048]{2,1,0:T(1,128)} %broadcast_in_dim.33), calls=%async_computation.5 | async-start | bytes 524288 | tf_op jit(solution)/shard_map/all_to_all | solution.py:234
  339.6 6.2 %copy-start.5 = (f32[32,36]{1,0:T(8,128)S(1)}, f32[32,36]{1,0:T(8,128)}, u32[]{:S(2)}) copy-start(f32[32,36]{1,0:T(8,128)} %copy-done.4) | copy-start | bytes 13828
  339.6 123.7 %all-to-all-start.6 = ((bf16[32,36,2048]{2,1,0:T(8,128)(2,1)}), bf16[32,36,2048]{2,1,0:T(8,128)(2,1)}, u32[]{:S(2)}, u32[]{:S(2)}) async-start(bf16[32,36,2048]{2,1,0:T(8,128)(2,1)} %add_convert_fusion), calls=%async_computation.6 | async-start | bytes 10485760 | tf_op jit(solution)/shard_map/all_to_all | solution.py:238
  345.8 11.5 %copy-start.6 = (bf16[32,36,768]{2,1,0:T(8,128)(2,1)S(1)}, bf16[32,36,768]{2,1,0:T(8,128)(2,1)}, u32[]{:S(2)}) copy-start(bf16[32,36,768]{2,1,0:T(8,128)(2,1)} %get-tuple-element.46) | copy-start | bytes 5308420
  357.3 8.4 %copy-start.7 = (bf16[32,36,768]{2,1,0:T(8,128)(2,1)S(1)}, bf16[32,36,768]{2,1,0:T(8,128)(2,1)}, u32[]{:S(2)}) copy-start(bf16[32,36,768]{2,1,0:T(8,128)(2,1)} %get-tuple-element.47) | copy-start | bytes 5308420
  374.0 93.9 %copy-start.1 = (bf16[1,2048,768]{2,1,0:T(8,128)(2,1)S(1)}, bf16[1,2048,768]{2,1,0:T(8,128)(2,1)}, u32[]{:S(2)}) copy-start(bf16[1,2048,768]{2,1,0:T(8,128)(2,1)} %param.15) | copy-start | bytes 9437188
  463.3 3.4 copy-start.2

commit v7 on v6

--- a/solution.py
+++ b/solution.py
@@ -197,7 +197,13 @@
         jnp.bfloat16
     )
     got_cot, grid_tokens = lax.optimization_barrier((got_cot, grid_tokens))
-    got_tokens = lax.all_to_all(grid_tokens, axes, split_axis=0, concat_axis=0, tiled=True)
+    half = width // 2
+    got_tokens_a = lax.all_to_all(
+        grid_tokens[:, :, :half], axes, split_axis=0, concat_axis=0, tiled=True
+    )
+    got_tokens_b = lax.all_to_all(
+        grid_tokens[:, :, half:], axes, split_axis=0, concat_axis=0, tiled=True
+    )
     cot_rows = got_cot
     grad_rows, expert_out, grad_gate_pre, grad_up_pre, grad_down_w = expert_from_cot(
         cot_rows,
@@ -211,7 +217,7 @@
     slot_route_dot = jnp.sum(
         cot_rows.astype(jnp.float32) * expert_out.astype(jnp.float32), axis=2
     ).astype(jnp.bfloat16)
-    slot_route_dot, got_tokens = lax.optimization_barrier((slot_route_dot, got_tokens))
+    slot_route_dot, got_tokens_b = lax.optimization_barrier((slot_route_dot, got_tokens_b))
     back_dot = lax.all_to_all(slot_route_dot, axes, split_axis=0, concat_axis=0, tiled=True)
     route_dot = back_dot.reshape(-1)
     route_grad = lax.dot_general(
@@ -236,14 +242,19 @@
     back_grad = grad_rows
     back_grad, grad_router = lax.optimization_barrier((back_grad, grad_router))
     back_rows = lax.all_to_all(back_grad, axes, split_axis=0, concat_axis=0, tiled=True)
-    input_rows = got_tokens
     grid_rows = (((0, 1), (0, 1)), ((), ()))
-    grad_gate_w = lax.dot_general(
-        input_rows, grad_gate_pre, grid_rows, preferred_element_type=jnp.float32
-    ).astype(jnp.bfloat16)
-    grad_up_w = lax.dot_general(
-        input_rows, grad_up_pre, grid_rows, preferred_element_type=jnp.float32
-    ).astype(jnp.bfloat16)
+
+    def by_rows(pre):
+        return jnp.concatenate(
+            [
+                lax.dot_general(got_tokens_a, pre, grid_rows, preferred_element_type=jnp.float32),
+                lax.dot_general(got_tokens_b, pre, grid_rows, preferred_element_type=jnp.float32),
+            ],
+            axis=0,
+        ).astype(jnp.bfloat16)
+
+    grad_gate_w = by_rows(grad_gate_pre)
+    grad_up_w = by_rows(grad_up_pre)
     grad_sum = lax.dot_general(
         grid_table, back_rows, (((0, 1), (0, 1)), ((), ())), preferred_element_type=jnp.float32
     )

time: 475 us -> 465 us (0.979)
  blocking collectives: 0 us -> 34.4 us
  waiting for transfers between devices: 295 us -> 266 us
  starting transfers between devices: 36.6 us -> 24.7 us
  matrix products: 95.9 us -> 87.9 us
    all_to_all x0 -> x3, blocking collectives: none -> 34.4 us  [the longest x1 12.8 us: body(): lax.all_to_all(part_rows, axes, split_axis=0, concat_axis=0, tiled=True)]
    all_to_all x4 -> x2, waiting for transfers between devices: 95.2 us -> 69.3 us  [the longest x1 44.9 us: body(): lax.all_to_all(grid_tokens[:, :, half:], axes, split_axis=0, concat_axis=...]
    all_to_all x4 -> x2, starting transfers between devices: 17.2 us -> 7.44 us  [the longest x1 3.74 us: body(): lax.all_to_all(grid_tokens[:, :, :half], axes, split_axis=0, concat_axis=...]
    slice x0 -> x1, local copies, waits for them, and re-layouts: none -> 5.49 us  [body(): grid_tokens[:, :, :half]]
    dot_general x2 -> x4, matrix products: 16.7 us -> 16.5 us  [the longest x2 8.26 us: by_rows(): lax.dot_general(got_tokens_a, pre, grid_rows, preferred_element_type=jnp....]
  transfers between devices with their start and end apart: 7 -> 5, of which waited for: 4 -> 4; matrix products, arithmetic and copies ran while one was open for 23% -> 23% of each run, Pallas kernels for 0% -> 0%
where the time goes in v7:
time: 465 us; the launch traced here: 458 us
  waiting for transfers between devices  266 us (57%)
  matrix products  87.9 us (19%)
  blocking collectives  34.4 us (7%)
  local copies, waits for them, and re-layouts  27.1 us (6%)
  starting transfers between devices  24.7 us (5%)
  other arithmetic  16.9 us (4%)
    all_to_all x1, waiting for transfers between devices, body(): lax.all_to_all(grid_cot, axes, split_axis=0, concat_axis=0, tiled=True)  113 us
    all_to_all x1, waiting for transfers between devices, body(): lax.all_to_all(back_grad, axes, split_axis=0, concat_axis=0, tiled=True)  83.7 us
    all_to_all x1, waiting for transfers between devices, body(): lax.all_to_all(grid_tokens[:, :, half:], axes, split_axis=0, concat_axis=...  44.9 us
    all_to_all x1, waiting for transfers between devices, body(): lax.all_to_all(grid_tokens[:, :, :half], axes, split_axis=0, concat_axis=...  24.4 us
    dot_general x1, matrix products, expert_from_cot(): lax.dot_general(scaled_cot, down_matrix, last_t, preferred_element_type=j...  13.1 us
    all_to_all x1, blocking collectives, body(): lax.all_to_all(part_rows, axes, split_axis=0, concat_axis=0, tiled=True)  12.8 us
    all_to_all x1, blocking collectives, body(): lax.all_to_all(spread, axes, split_axis=0, concat_axis=0, tiled=True)  12.6 us
    dot_general x1, matrix products, expert_from_cot(): lax.dot_general(hidden, scaled_cot, grid_rows, preferred_element_type=jnp...  11.5 us
  transfers between devices with their start and end apart: 5, of which 4 were waited for; matrix products, arithmetic and copies ran while one was open for 23% of the time, Pallas kernels for 0%

profile of v7, /device:TPU:0, one launch (start us, length us, event | category | flops | bytes accessed | tf_op | source)
XLA Modules:
  0.0 457.6 jit_solution(7402882991788671433)
XLA Ops:
  6.2 7.3 %all-to-all-start = ((bf16[32,1,36]{2,1,0:T(2,128)(2,1)}), bf16[32,1,36]{2,1,0:T(2,128)(2,1)S(1)}, u32[]{:S(2)}, u32[]{:S(2)}) async-start(bf16[32,1,36]{2,1,0:T(2,128)(2,1)} %all_to_all.48), calls=%async_computation | async-start | bytes 32768 | tf_op jit(solution)/shard_map/all_to_all | solution.py:188
  13.7 6.8 %fusion.24 = bf16[1152,128]{1,0:T(8,128)(2,1)} fusion(s32[128,8]{0,1:T(8,128)S(1)} %multiply_add_fusion.1), kind=kLoop, calls=%fused_computation.40 | loop fusion | flops 3391488 | bytes 299008 | tf_op jit(solution)/shard_map/reduce_sum | solution.py:29
  21.5 5.0 %convolution_convert_fusion.1 = bf16[32,36,2048]{2,1,0:T(8,128)(2,1)} fusion(bf16[32,36,128]{2,1,0:T(8,128)(2,1)S(1)} %reshape.162, bf16[128,2048]{1,0:T(8,128)(2,1)} %param.10), kind=kOutput, calls=%fused_computation.18 | convolution fusion | flops 606339072 | bytes 5537792 | tf_op jit(solution)/shard_map/dot_general | solution.py:191
  26.5 5.9 %all-to-all-start.1 = ((bf16[32,36,2048]{2,1,0:T(8,128)(2,1)}), bf16[32,36,2048]{2,1,0:T(8,128)(2,1)}, u32[]{:S(2)}, u32[]{:S(2)}) async-start(bf16[32,36,2048]{2,1,0:T(8,128)(2,1)} %convolution_convert_fusion.1), calls=%async_computation.1 | async-start | bytes 10485760 | tf_op jit(solution)/shard_map/all_to_all | solution.py:195
  32.5 4.9 %convolution_convert_fusion = bf16[32,36,2048]{2,1,0:T(8,128)(2,1)} fusion(bf16[32,36,128]{2,1,0:T(8,128)(2,1)S(1)} %reshape.162, bf16[128,2048]{1,0:T(8,128)(2,1)} %param.9), kind=kOutput, calls=%fused_computation.17 | convolution fusion | flops 606339072 | bytes 5537792 | tf_op jit(solution)/shard_map/dot_general | solution.py:196
  37.4 112.6 %all-to-all-done.1 = bf16[32,36,2048]{2,1,0:T(8,128)(2,1)} async-done(((bf16[32,36,2048]{2,1,0:T(8,128)(2,1)}), bf16[32,36,2048]{2,1,0:T(8,128)(2,1)}, u32[]{:S(2)}, u32[]{:S(2)}) %all-to-all-start.1) | async-done | bytes 4718624 | tf_op jit(solution)/shard_map/all_to_all | solution.py:195
  150.0 5.5 %fusion.45 = (bf16[32,36,1024]{2,1,0:T(8,128)(2,1)}, bf16[32,36,1024]{2,1,0:T(8,128)(2,1)}) fusion(bf16[32,36,2048]{2,1,0:T(8,128)(2,1)} %convolution_convert_fusion), kind=kLoop, calls=%fused_computation.74 | loop fusion | bytes 9437184 | tf_op jit(solution)/shard_map/slice | solution.py:202
  159.2 4.4 multiply_convert_fusion.3
  167.1 8.5 %fusion.1 = bf16[32,36]{1,0:T(8,128)(2,1)S(1)} fusion(bf16[32,36,2048]{2,1,0:T(8,128)(2,1)} %all-to-all-done.1, bf16[32,36,768]{2,1,0:T(8,128)(2,1)} %convert_element_type.133, bf16[1,768,2048]{2,1,0:T(8,128)(2,1)} %param.17), kind=kOutput, calls=%fused_computation.3 | convolution fusion | flops 3635674112 | bytes 9636096 | tf_op jit(solution)/shard_map/dot_general | solution.py:141
  175.6 44.9 %all-to-all-done.2 = bf16[32,36,1024]{2,1,0:T(8,128)(2,1)} async-done(((bf16[32,36,1024]{2,1,0:T(8,128)(2,1)}), bf16[32,36,1024]{2,1,0:T(8,128)(2,1)}, u32[]{:S(2)}, u32[]{:S(2)}) %all-to-all-start.2) | async-done | bytes 2359328 | tf_op jit(solution)/shard_map/all_to_all | solution.py:204
  220.5 9.0 %all_to_all.58 = bf16[32,1,36]{2,1,0:T(2,128)(2,1)S(1)} all-to-all(bf16[32,1,36]{2,1,0:T(2,128)(2,1)S(1)} %copy.56), channel_id=1, replica_groups=mesh['outer'=4,'inner'=8] {'outer','inner'}, dimensions={0} | all-to-all | bytes 4608 | tf_op jit(solution)/shard_map/all_to_all | solution.py:221
  229.8 5.9 %fusion.5 = f32[1,128,8]{2,0,1:T(1,128)S(1)} fusion(bf16[1152,1,1]{0,1,2:T(2,128)(2,1)S(1)} %reshape.173, s32[1024]{0:T(1024)S(1)} %multiply_add_fusion), kind=kOutput, calls=%fused_computation.12 | convolution fusion | flops 3538944 | bytes 10496 | tf_op jit(solution)/shard_map/dot_general | solution.py:223
  240.1 12.8 %all_to_all.59 = f32[32,1,2048]{2,1,0:T(1,128)} all-to-all(f32[32,1,2048]{2,1,0:T(1,128)S(1)} %all_to_all.49), channel_id=1, replica_groups=mesh['outer'=4,'inner'=8] {'outer','inner'}, dimensions={0} | all-to-all | bytes 524288 | tf_op jit(solution)/shard_map/all_to_all | solution.py:237
  254.1 12.6 %all_to_all.60 = f32[32,1,2048]{2,1,0:T(1,128)S(1)} all-to-all(f32[32,1,2048]{2,1,0:T(1,128)S(1)} %broadcast_in_dim.29), channel_id=1, replica_groups=mesh['outer'=4,'inner'=8] {'outer','inner'}, dimensions={0} | all-to-all | bytes 524288 | tf_op jit(solution)/shard_map/all_to_all | solution.py:240
  278.2 13.1 %multiply_convert_fusion.1 = (bf16[32,36,768]{2,1,0:T(8,128)(2,1)}, bf16[32,36,768]{2,1,0:T(8,128)(2,1)}) fusion(f32[32,36,768]{2,1,0:T(8,128)} %reshape.165, f32[32,36,768]{2,1,0:T(8,128)} %reshape.164, bf16[1,768,2048]{2,1,0:T(8,128)(2,1)} %param.17, bf16[32,36,2048]{2,1,0:T(8,128)(2,1)} %all-to-all-done.1, f32[32,36]{1,0:T(8,128)S(1)} %convert_element_type.119), kind=kOutput, calls=%fused_computation.20 | convolution fusion | flops 3642458112 | bytes 18485760 | tf_op jit(solution)/shard_map/dot_general | solution.py:147
  291.3 6.0 %fusion.16 = f32[32,36,2048]{2,1,0:T(8,128)S(1)} fusion(bf16[32,36,768]{2,1,0:T(8,128)(2,1)} %get-tuple-element.47, bf16[1,2048,768]{2,1,0:T(8,128)(2,1)S(1)} %copy-done), kind=kOutput, calls=%fused_computation.32 | convolution fusion | flops 3623878656 | bytes 14352384 | tf_op jit(solution)/shard_map/dot_general | solution.py:155
  297.4 8.0 %add_convert_fusion = bf16[32,36,2048]{2,1,0:T(8,128)(2,1)} fusion(f32[32,36,2048]{2,1,0:T(8,128)S(1)} %fusion.16, bf16[32,36,768]{2,1,0:T(8,128)(2,1)} %get-tuple-element.46, bf16[1,2048,768]{2,1,0:T(8,128)(2,1)S(1)} %copy-done.6), kind=kOutput, calls=%fused_computation.4 | convolution fusion | flops 3628597248 | bytes 19070976 | tf_op jit(solution)/shard_map/dot_general | solution.py:156
  307.4 24.4 %all-to-all-done.7 = bf16[32,36,1024]{2,1,0:T(8,128)(2,1)} async-done(((bf16[32,36,1024]{2,1,0:T(8,128)(2,1)}), bf16[32,36,1024]{2,1,0:T(8,128)(2,1)}, u32[]{:S(2)}, u32[]{:S(2)}) %all-to-all-start.7) | async-done | bytes 2359328 | tf_op jit(solution)/shard_map/all_to_all | solution.py:201
  335.8 11.5 %fusion.20 = bf16[1,768,2048]{2,1,0:T(8,128)(2,1)} fusion(bf16[32,36,2048]{2,1,0:T(8,128)(2,1)} %all-to-all-done.1, f32[32,36]{1,0:T(8,128)S(1)} %convert_element_type.119, f32[32,36,768]{2,1,0:T(8,128)} %reshape.164, f32[32,36,768]{2,1,0:T(8,128)} %reshape.165), kind=kOutput, calls=%fused_computation.36 | convolution fusion | flops 3637837824 | bytes 14946816 | tf_op jit(solution)/shard_map/dot_general | solution.py:158
  347.3 4.2 fusion.30
  351.5 4.1 fusion.28
  355.5 4.0 fusion.29
  359.6 4.3 fusion.27
  369.3 83.7 %all-to-all-done.6 = bf16[32,36,2048]{2,1,0:T(8,128)(2,1)} async-done(((bf16[32,36,2048]{2,1,0:T(8,128)(2,1)}), bf16[32,36,2048]{2,1,0:T(8,128)(2,1)}, u32[]{:S(2)}, u32[]{:S(2)}) %all-to-all-start.6) | async-done | bytes 4718624 | tf_op jit(solution)/shard_map/all_to_all | solution.py:244
  (61 shorter events, 47.3 us)
Async XLA Ops:
  0.6 290.7 %copy-start = (bf16[1,2048,768]{2,1,0:T(8,128)(2,1)S(1)}, bf16[1,2048,768]{2,1,0:T(8,128)(2,1)}, u32[]{:S(2)}) copy-start(bf16[1,2048,768]{2,1,0:T(8,128)(2,1)} %param.15) | copy-start | bytes 9437188
  0.6 13.0 %copy-start.5 = (s32[128,8]{0,1:T(8,128)S(1)}, s32[128,8]{0,1:T(8,128)}, u32[]{:S(2)}) copy-start(s32[128,8]{0,1:T(8,128)} %param.11) | copy-start | bytes 12292
  6.2 20.3 %all-to-all-start = ((bf16[32,1,36]{2,1,0:T(2,128)(2,1)}), bf16[32,1,36]{2,1,0:T(2,128)(2,1)S(1)}, u32[]{:S(2)}, u32[]{:S(2)}) async-start(bf16[32,1,36]{2,1,0:T(2,128)(2,1)} %all_to_all.48), calls=%async_computation | async-start | bytes 32768 | tf_op jit(solution)/shard_map/all_to_all | solution.py:188
  21.5 11.0 %copy-start.2 = (bf16[32,36,128]{2,1,0:T(8,128)(2,1)}, bf16[32,36,128]{2,1,0:T(8,128)(2,1)S(1)}, u32[]{:S(2)}) copy-start(bf16[32,36,128]{2,1,0:T(8,128)(2,1)S(1)} %reshape.162) | copy-start | bytes 884740
  26.5 123.5 %all-to-all-start.1 = ((bf16[32,36,2048]{2,1,0:T(8,128)(2,1)}), bf16[32,36,2048]{2,1,0:T(8,128)(2,1)}, u32[]{:S(2)}, u32[]{:S(2)}) async-start(bf16[32,36,2048]{2,1,0:T(8,128)(2,1)} %convolution_convert_fusion.1), calls=%async_computation.1 | async-start | bytes 10485760 | tf_op jit(solution)/shard_map/all_to_all | solution.py:195
  155.5 65.1 %all-to-all-start.2 = ((bf16[32,36,1024]{2,1,0:T(8,128)(2,1)}), bf16[32,36,1024]{2,1,0:T(8,128)(2,1)}, u32[]{:S(2)}, u32[]{:S(2)}) async-start(bf16[32,36,1024]{2,1,0:T(8,128)(2,1)} %get-tuple-element.49), calls=%async_computation.2 | async-start | bytes 5242880 | tf_op jit(solution)/shard_map/all_to_all | solution.py:204
  266.7 65.1 %all-to-all-start.7 = ((bf16[32,36,1024]{2,1,0:T(8,128)(2,1)}), bf16[32,36,1024]{2,1,0:T(8,128)(2,1)}, u32[]{:S(2)}, u32[]{:S(2)}) async-start(bf16[32,36,1024]{2,1,0:T(8,128)(2,1)} %get-tuple-element.48), calls=%async_computation.7 | async-start | bytes 5242880 | tf_op jit(solution)/shard_map/all_to_all | solution.py:201
  291.3 6.1 %copy-start.6 = (bf16[1,2048,768]{2,1,0:T(8,128)(2,1)S(1)}, bf16[1,2048,768]{2,1,0:T(8,128)(2,1)}, u32[]{:S(2)}) copy-start(bf16[1,2048,768]{2,1,0:T(8,128)(2,1)} %param.16) | copy-start | bytes 9437188
  331.8 121.1 %all-to-all-start.6 = ((bf16[32,36,2048]{2,1,0:T(8,128)(2,1)}), bf16[32,36,2048]{2,1,0:T(8,128)(2,1)}, u32[]{:S(2)}, u32[]{:S(2)}) async-start(bf16[32,36,2048]{2,1,0:T(8,128)(2,1)} %add_convert_fusion), calls=%async_computation.6 | async-start | bytes 10485760 | tf_op jit(solution)/shard_map/all_to_all | solution.py:244
  335.8 11.5 %copy-start.7 = (bf16[32,36,768]{2,1,0:T(8,128)(2,1)S(1)}, bf16[32,36,768]{2,1,0:T(8,128)(2,1)}, u32[]{:S(2)}) copy-start(bf16[32,36,768]{2,1,0:T(8,128)(2,1)} %get-tuple-element.46) | copy-start | bytes 5308420
  347.3 4.2 copy-start.8
  363.8 89.1 %copy-start.3 = (bf16[32,36,128]{2,1,0:T(8,128)(2,1)S(1)}, bf16[32,36,128]{2,1,0:T(8,128)(2,1)}, u32[]{:S(2)}) copy-start(bf16[32,36,128]{2,1,0:T(8,128)(2,1)} %copy-done.2) | copy-start | bytes 884740
  366.9 90.6 %copy-start.1 = (bf16[1,2048,768]{2,1,0:T(8,128)(2,1)S(1)}, bf16[1,2048,768]{2,1,0:T(8,128)(2,1)}, u32[]{:S(2)}) copy-start(bf16[1,2048,768]{2,1,0:T(8,128)(2,1)} %param.15) | copy-start | bytes 9437188
  452.9 3.4 copy-start.4

commit v8 on v7

--- a/solution.py
+++ b/solution.py
@@ -177,6 +177,7 @@
     capacity = gate_saved.shape[1] // experts
     outer_size = lax.axis_size("outer")
     inner_size = lax.axis_size("inner")
+    devices = outer_size * inner_size
     axes = ("outer", "inner")
     picked, probs = route_probs(tokens, routes, router_weight)
     slot_table, token_table = route_tables(routes, experts, capacity)
@@ -200,9 +201,6 @@
     half = width // 2
     got_tokens_a = lax.all_to_all(
         grid_tokens[:, :, :half], axes, split_axis=0, concat_axis=0, tiled=True
-    )
-    got_tokens_b = lax.all_to_all(
-        grid_tokens[:, :, half:], axes, split_axis=0, concat_axis=0, tiled=True
     )
     cot_rows = got_cot
     grad_rows, expert_out, grad_gate_pre, grad_up_pre, grad_down_w = expert_from_cot(
@@ -217,9 +215,11 @@
     slot_route_dot = jnp.sum(
         cot_rows.astype(jnp.float32) * expert_out.astype(jnp.float32), axis=2
     ).astype(jnp.bfloat16)
-    slot_route_dot, got_tokens_b = lax.optimization_barrier((slot_route_dot, got_tokens_b))
-    back_dot = lax.all_to_all(slot_route_dot, axes, split_axis=0, concat_axis=0, tiled=True)
-    route_dot = back_dot.reshape(-1)
+    dot_row = jnp.pad(slot_route_dot, ((0, 0), (0, half - capacity)))[:, None, :]
+    send_b = jnp.concatenate([grid_tokens[:, :, half:], dot_row], axis=1)
+    got_b = lax.all_to_all(send_b, axes, split_axis=0, concat_axis=0, tiled=True)
+    got_tokens_b = got_b[:, :capacity, :]
+    route_dot = got_b[:, capacity, :capacity].reshape(-1)
     route_grad = lax.dot_general(
         slot_table, route_dot, contract_rows, preferred_element_type=jnp.float32
     ).reshape(probs.shape)
@@ -231,17 +231,20 @@
     router_part = lax.dot_general(
         tokens, logit_grad, contract_rows, preferred_element_type=jnp.float32
     )
-    total_tokens = tokens.shape[0] * outer_size * inner_size
-    devices = outer_size * inner_size
-    part_rows = router_part.reshape(devices, -1)
-    got_parts = lax.all_to_all(part_rows, axes, split_axis=0, concat_axis=0, tiled=True)
+    part_rows = router_part.reshape(devices, 1, -1)
+    part_high = part_rows.astype(jnp.bfloat16)
+    part_low = (part_rows - part_high.astype(jnp.float32)).astype(jnp.bfloat16)
+    send_back = jnp.concatenate([grad_rows, part_high, part_low], axis=1)
+    got_back = lax.all_to_all(send_back, axes, split_axis=0, concat_axis=0, tiled=True)
+    back_rows = got_back[:, :capacity, :]
+    got_parts = got_back[:, capacity, :].astype(jnp.float32) + got_back[:, capacity + 1, :].astype(
+        jnp.float32
+    )
     chunk_sum = jnp.sum(got_parts, axis=0, keepdims=True)
-    spread = jnp.broadcast_to(chunk_sum, part_rows.shape)
+    spread = jnp.broadcast_to(chunk_sum, got_parts.shape)
     got_sums = lax.all_to_all(spread, axes, split_axis=0, concat_axis=0, tiled=True)
+    total_tokens = tokens.shape[0] * devices
     grad_router = got_sums.reshape(router_part.shape) * (1.0 / math.sqrt(total_tokens))
-    back_grad = grad_rows
-    back_grad, grad_router = lax.optimization_barrier((back_grad, grad_router))
-    back_rows = lax.all_to_all(back_grad, axes, split_axis=0, concat_axis=0, tiled=True)
     grid_rows = (((0, 1), (0, 1)), ((), ()))
 
     def by_rows(pre):

time: 465 us -> 443 us (0.953)
  blocking collectives: 34.4 us -> 0 us
  other arithmetic: 16.9 us -> 27.6 us
    all_to_all x3 -> x0, blocking collectives: 34.4 us -> none  [the longest x1 12.8 us: body(): lax.all_to_all(part_rows, axes, split_axis=0, concat_axis=0, tiled=True)]
    all_to_all x2 -> x3, waiting for transfers between devices: 129 us -> 146 us  [the longest x1 86.3 us: body(): lax.all_to_all(send_back, axes, split_axis=0, concat_axis=0, tiled=True)]
    concatenate x0 -> x2, other arithmetic: none -> 8.46 us  [the longest x1 6.48 us: body(): send_back = jnp.concatenate([grad_rows, part_high, part_low], axis=1)]
    all_to_all x1, waiting for transfers between devices: 113 us -> 105 us  [body(): lax.all_to_all(grid_cot, axes, split_axis=0, concat_axis=0, tiled=True)]
    all_to_all x1, waiting for transfers between devices: 24.4 us -> 18.9 us  [body(): lax.all_to_all(grid_tokens[:, :, :half], axes, split_axis=0, concat_axis=...]
    all_to_all x2 -> x3, starting transfers between devices: 7.69 us -> 10.6 us  [the longest x1 3.75 us: body(): lax.all_to_all(send_back, axes, split_axis=0, concat_axis=0, tiled=True)]
  transfers between devices with their start and end apart: 5 -> 6, of which waited for: 4 -> 5; matrix products, arithmetic and copies ran while one was open for 23% -> 26% of each run, Pallas kernels for 0% -> 0%
where the time goes in v8:
time: 443 us; the launch traced here: 437 us
  waiting for transfers between devices  269 us (61%)
  matrix products  85.5 us (19%)
  starting transfers between devices  27.8 us (6%)
  other arithmetic  27.6 us (6%)
  local copies, waits for them, and re-layouts  25.8 us (6%)
    all_to_all x1, waiting for transfers between devices, body(): lax.all_to_all(grid_cot, axes, split_axis=0, concat_axis=0, tiled=True)  105 us
    all_to_all x1, waiting for transfers between devices, body(): lax.all_to_all(send_back, axes, split_axis=0, concat_axis=0, tiled=True)  86.3 us
    all_to_all x1, waiting for transfers between devices, body(): lax.all_to_all(send_b, axes, split_axis=0, concat_axis=0, tiled=True)  53.6 us
    all_to_all x1, waiting for transfers between devices, body(): lax.all_to_all(grid_tokens[:, :, :half], axes, split_axis=0, concat_axis=...  18.9 us
    dot_general x1, matrix products, expert_from_cot(): lax.dot_general(scaled_cot, down_matrix, last_t, preferred_element_type=j...  13.1 us
    dot_general x1, matrix products, expert_from_cot(): lax.dot_general(hidden, scaled_cot, grid_rows, preferred_element_type=jnp...  11.5 us
  transfers between devices with their start and end apart: 6, of which 5 were waited for; matrix products, arithmetic and copies ran while one was open for 26% of the time, Pallas kernels for 0%

profile of v8, /device:TPU:0, one launch (start us, length us, event | category | flops | bytes accessed | tf_op | source)
XLA Modules:
  0.0 436.9 jit_solution(864017203627845303)
XLA Ops:
  6.2 7.3 %all-to-all-start = ((bf16[32,1,36]{2,1,0:T(2,128)(2,1)}), bf16[32,1,36]{2,1,0:T(2,128)(2,1)S(1)}, u32[]{:S(2)}, u32[]{:S(2)}) async-start(bf16[32,1,36]{2,1,0:T(2,128)(2,1)} %all_to_all.32), calls=%async_computation | async-start | bytes 32768 | tf_op jit(solution)/shard_map/all_to_all | solution.py:189
  13.7 6.8 %fusion.29 = bf16[1152,128]{1,0:T(8,128)(2,1)} fusion(s32[128,8]{0,1:T(8,128)S(1)} %multiply_add_fusion.1), kind=kLoop, calls=%fused_computation.44 | loop fusion | flops 3391488 | bytes 299008 | tf_op jit(solution)/shard_map/reduce_sum | solution.py:29
  21.5 5.0 %convolution_convert_fusion.1 = bf16[32,36,2048]{2,1,0:T(8,128)(2,1)} fusion(bf16[32,36,128]{2,1,0:T(8,128)(2,1)S(1)} %reshape.194, bf16[128,2048]{1,0:T(8,128)(2,1)} %param.10), kind=kOutput, calls=%fused_computation.21 | convolution fusion | flops 606339072 | bytes 5537792 | tf_op jit(solution)/shard_map/dot_general | solution.py:192
  26.5 6.2 %all-to-all-start.1 = ((bf16[32,36,2048]{2,1,0:T(8,128)(2,1)}), bf16[32,36,2048]{2,1,0:T(8,128)(2,1)}, u32[]{:S(2)}, u32[]{:S(2)}) async-start(bf16[32,36,2048]{2,1,0:T(8,128)(2,1)} %convolution_convert_fusion.1), calls=%async_computation.1 | async-start | bytes 10485760 | tf_op jit(solution)/shard_map/all_to_all | solution.py:196
  32.7 4.3 multiply_convert_fusion.3
  40.6 4.9 %convolution_convert_fusion = bf16[32,36,2048]{2,1,0:T(8,128)(2,1)} fusion(bf16[32,36,128]{2,1,0:T(8,128)(2,1)S(1)} %reshape.194, bf16[128,2048]{1,0:T(8,128)(2,1)} %param.9), kind=kOutput, calls=%fused_computation.20 | convolution fusion | flops 606339072 | bytes 5537792 | tf_op jit(solution)/shard_map/dot_general | solution.py:197
  45.5 104.7 %all-to-all-done.1 = bf16[32,36,2048]{2,1,0:T(8,128)(2,1)} async-done(((bf16[32,36,2048]{2,1,0:T(8,128)(2,1)}), bf16[32,36,2048]{2,1,0:T(8,128)(2,1)}, u32[]{:S(2)}, u32[]{:S(2)}) %all-to-all-start.1) | async-done | bytes 4718624 | tf_op jit(solution)/shard_map/all_to_all | solution.py:196
  150.2 4.8 %fusion.64 = (bf16[32,36,1024]{2,1,0:T(8,128)(2,1)}, bf16[32,36,1024]{2,1,0:T(8,128)(2,1)S(1)}) fusion(bf16[32,36,2048]{2,1,0:T(8,128)(2,1)} %convolution_convert_fusion), kind=kLoop, calls=%fused_computation.89 | loop fusion | bytes 9437184 | tf_op jit(solution)/shard_map/slice | solution.py:203
  155.0 6.4 %fusion.1 = bf16[32,36]{1,0:T(8,128)(2,1)S(1)} fusion(bf16[32,36,2048]{2,1,0:T(8,128)(2,1)} %all-to-all-done.1, bf16[32,36,768]{2,1,0:T(8,128)(2,1)S(1)} %copy-done.5, bf16[1,768,2048]{2,1,0:T(8,128)(2,1)S(1)} %copy-done.8), kind=kOutput, calls=%fused_computation.3 | convolution fusion | flops 3635674112 | bytes 9636096 | tf_op jit(solution)/shard_map/dot_general | solution.py:141
  170.9 3.9 reshape.196
  174.8 53.6 %all-to-all-done.2 = bf16[32,37,1024]{2,1,0:T(8,128)(2,1)} async-done(((bf16[32,37,1024]{2,1,0:T(8,128)(2,1)}), bf16[32,37,1024]{2,1,0:T(8,128)(2,1)}, u32[]{:S(2)}, u32[]{:S(2)}) %all-to-all-start.2) | async-done | bytes 2424864 | tf_op jit(solution)/shard_map/all_to_all | solution.py:220
  232.2 13.1 %multiply_convert_fusion.1 = (bf16[32,36,768]{2,1,0:T(8,128)(2,1)}, bf16[32,36,768]{2,1,0:T(8,128)(2,1)}) fusion(f32[32,36,768]{2,1,0:T(8,128)} %reshape.197, f32[32,36,768]{2,1,0:T(8,128)} %reshape.196, bf16[1,768,2048]{2,1,0:T(8,128)(2,1)} %param.17, bf16[32,36,2048]{2,1,0:T(8,128)(2,1)} %all-to-all-done.1, f32[32,36]{1,0:T(8,128)S(1)} %convert_element_type.166), kind=kOutput, calls=%fused_computation.23 | convolution fusion | flops 3642458112 | bytes 18485760 | tf_op jit(solution)/shard_map/dot_general | solution.py:147
  245.3 6.0 %fusion.18 = f32[32,36,2048]{2,1,0:T(8,128)S(1)} fusion(bf16[32,36,768]{2,1,0:T(8,128)(2,1)} %get-tuple-element.39, bf16[1,2048,768]{2,1,0:T(8,128)(2,1)S(1)} %copy-done), kind=kOutput, calls=%fused_computation.35 | convolution fusion | flops 3623878656 | bytes 14352384 | tf_op jit(solution)/shard_map/dot_general | solution.py:155
  251.3 8.4 %add_convert_fusion = bf16[32,36,2048]{2,1,0:T(8,128)(2,1)} fusion(f32[32,36,2048]{2,1,0:T(8,128)S(1)} %fusion.18, bf16[32,36,768]{2,1,0:T(8,128)(2,1)} %get-tuple-element.38, bf16[1,2048,768]{2,1,0:T(8,128)(2,1)S(1)} %copy-done.9), kind=kOutput, calls=%fused_computation.4 | convolution fusion | flops 3628597248 | bytes 19070976 | tf_op jit(solution)/shard_map/dot_general | solution.py:156
  260.8 5.9 %fusion.7 = f32[1,128,8]{2,0,1:T(1,128)S(1)} fusion(bf16[1152,1,1]{0,1,2:T(2,128)(2,1)S(1)} %reshape.205, s32[1024]{0:T(1024)S(1)} %multiply_add_fusion), kind=kOutput, calls=%fused_computation.15 | convolution fusion | flops 3538944 | bytes 10496 | tf_op jit(solution)/shard_map/dot_general | solution.py:223
  268.2 6.5 %pad_maximum_fusion = bf16[32,38,2048]{2,1,0:T(8,128)(2,1)} fusion(bf16[32,1,2048]{2,1,0:T(2,128)(2,1)S(1)} %get-tuple-element.43, bf16[32,1,2048]{2,1,0:T(2,128)(2,1)S(1)} %get-tuple-element.42, bf16[32,36,2048]{2,1,0:T(8,128)(2,1)} %add_convert_fusion), kind=kLoop, calls=%fused_computation.8 | loop fusion | flops 14942208 | bytes 9961472 | tf_op jit(solution)/shard_map/concatenate | solution.py:237
  274.7 18.9 %all-to-all-done.4 = bf16[32,36,1024]{2,1,0:T(8,128)(2,1)} async-done(((bf16[32,36,1024]{2,1,0:T(8,128)(2,1)}), bf16[32,36,1024]{2,1,0:T(8,128)(2,1)}, u32[]{:S(2)}, u32[]{:S(2)}) %all-to-all-start.4) | async-done | bytes 2359328 | tf_op jit(solution)/shard_map/all_to_all | solution.py:202
  297.3 11.5 %fusion.22 = bf16[1,768,2048]{2,1,0:T(8,128)(2,1)} fusion(bf16[32,36,2048]{2,1,0:T(8,128)(2,1)} %all-to-all-done.1, f32[32,36]{1,0:T(8,128)S(1)} %convert_element_type.166, f32[32,36,768]{2,1,0:T(8,128)} %reshape.196, f32[32,36,768]{2,1,0:T(8,128)} %reshape.197), kind=kOutput, calls=%fused_computation.39 | convolution fusion | flops 3637837824 | bytes 14946816 | tf_op jit(solution)/shard_map/dot_general | solution.py:158
  308.8 4.1 fusion.44
  313.0 4.1 fusion.40
  317.0 4.0 fusion.45
  321.0 4.3 fusion.41
  328.4 86.3 %all-to-all-done.3 = bf16[32,38,2048]{2,1,0:T(8,128)(2,1)} async-done(((bf16[32,38,2048]{2,1,0:T(8,128)(2,1)}), bf16[32,38,2048]{2,1,0:T(8,128)(2,1)}, u32[]{:S(2)}, u32[]{:S(2)}) %all-to-all-start.3) | async-done | bytes 4980768 | tf_op jit(solution)/shard_map/all_to_all | solution.py:238
  425.7 5.7 %all-to-all-done.5 = f32[32,1,2048]{2,1,0:T(1,128)} async-done(((f32[32,1,2048]{2,1,0:T(1,128)}), f32[32,1,2048]{2,1,0:T(1,128)}, u32[]{:S(2)}, u32[]{:S(2)}) %all-to-all-start.5) | async-done | bytes 262176 | tf_op jit(solution)/shard_map/all_to_all | solution.py:245
  (70 shorter events, 49.1 us)
Async XLA Ops:
  0.6 244.6 %copy-start = (bf16[1,2048,768]{2,1,0:T(8,128)(2,1)S(1)}, bf16[1,2048,768]{2,1,0:T(8,128)(2,1)}, u32[]{:S(2)}) copy-start(bf16[1,2048,768]{2,1,0:T(8,128)(2,1)} %param.15) | copy-start | bytes 9437188
  0.6 13.0 %copy-start.7 = (s32[128,8]{0,1:T(8,128)S(1)}, s32[128,8]{0,1:T(8,128)}, u32[]{:S(2)}) copy-start(s32[128,8]{0,1:T(8,128)} %param.11) | copy-start | bytes 12292
  6.2 20.3 %all-to-all-start = ((bf16[32,1,36]{2,1,0:T(2,128)(2,1)}), bf16[32,1,36]{2,1,0:T(2,128)(2,1)S(1)}, u32[]{:S(2)}, u32[]{:S(2)}) async-start(bf16[32,1,36]{2,1,0:T(2,128)(2,1)} %all_to_all.32), calls=%async_computation | async-start | bytes 32768 | tf_op jit(solution)/shard_map/all_to_all | solution.py:189
  21.5 19.1 %copy-start.2 = (bf16[32,36,128]{2,1,0:T(8,128)(2,1)}, bf16[32,36,128]{2,1,0:T(8,128)(2,1)S(1)}, u32[]{:S(2)}) copy-start(bf16[32,36,128]{2,1,0:T(8,128)(2,1)S(1)} %reshape.194) | copy-start | bytes 884740
  26.5 123.7 %all-to-all-start.1 = ((bf16[32,36,2048]{2,1,0:T(8,128)(2,1)}), bf16[32,36,2048]{2,1,0:T(8,128)(2,1)}, u32[]{:S(2)}, u32[]{:S(2)}) async-start(bf16[32,36,2048]{2,1,0:T(8,128)(2,1)} %convolution_convert_fusion.1), calls=%async_computation.1 | async-start | bytes 10485760 | tf_op jit(solution)/shard_map/all_to_all | solution.py:196
  150.2 4.8 %copy-start.5 = (bf16[32,36,768]{2,1,0:T(8,128)(2,1)S(1)}, bf16[32,36,768]{2,1,0:T(8,128)(2,1)}, u32[]{:S(2)}) copy-start(bf16[32,36,768]{2,1,0:T(8,128)(2,1)} %convert_element_type.180) | copy-start | bytes 5308420
  150.2 4.8 %copy-start.8 = (bf16[1,768,2048]{2,1,0:T(8,128)(2,1)S(1)}, bf16[1,768,2048]{2,1,0:T(8,128)(2,1)}, u32[]{:S(2)}) copy-start(bf16[1,768,2048]{2,1,0:T(8,128)(2,1)} %param.17) | copy-start | bytes 9437188
  163.5 64.9 %all-to-all-start.2 = ((bf16[32,37,1024]{2,1,0:T(8,128)(2,1)}), bf16[32,37,1024]{2,1,0:T(8,128)(2,1)}, u32[]{:S(2)}, u32[]{:S(2)}) async-start(bf16[32,37,1024]{2,1,0:T(8,128)(2,1)} %pad_maximum_fusion.3), calls=%async_computation.2 | async-start | bytes 5242880 | tf_op jit(solution)/shard_map/all_to_all | solution.py:220
  228.4 65.1 %all-to-all-start.4 = ((bf16[32,36,1024]{2,1,0:T(8,128)(2,1)}), bf16[32,36,1024]{2,1,0:T(8,128)(2,1)}, u32[]{:S(2)}, u32[]{:S(2)}) async-start(bf16[32,36,1024]{2,1,0:T(8,128)(2,1)} %get-tuple-element.40), calls=%async_computation.4 | async-start | bytes 5242880 | tf_op jit(solution)/shard_map/all_to_all | solution.py:202
  245.3 6.1 %copy-start.9 = (bf16[1,2048,768]{2,1,0:T(8,128)(2,1)S(1)}, bf16[1,2048,768]{2,1,0:T(8,128)(2,1)}, u32[]{:S(2)}) copy-start(bf16[1,2048,768]{2,1,0:T(8,128)(2,1)} %param.16) | copy-start | bytes 9437188
  251.3 15.6 %copy-start.4 = (bf16[128,2048]{1,0:T(8,128)(2,1)S(1)}, bf16[128,2048]{1,0:T(8,128)(2,1)}, u32[]{:S(2)}) copy-start(bf16[128,2048]{1,0:T(8,128)(2,1)} %param.9) | copy-start | bytes 1572868
  293.6 121.1 %all-to-all-start.3 = ((bf16[32,38,2048]{2,1,0:T(8,128)(2,1)}), bf16[32,38,2048]{2,1,0:T(8,128)(2,1)}, u32[]{:S(2)}, u32[]{:S(2)}) async-start(bf16[32,38,2048]{2,1,0:T(8,128)(2,1)} %pad_maximum_fusion), calls=%async_computation.3 | async-start | bytes 10485760 | tf_op jit(solution)/shard_map/all_to_all | solution.py:238
  297.3 11.5 %copy-start.10 = (bf16[32,36,768]{2,1,0:T(8,128)(2,1)S(1)}, bf16[32,36,768]{2,1,0:T(8,128)(2,1)}, u32[]{:S(2)}) copy-start(bf16[32,36,768]{2,1,0:T(8,128)(2,1)} %get-tuple-element.38) | copy-start | bytes 5308420
  308.8 4.2 copy-start.11
  325.3 95.7 %copy-start.3 = (bf16[32,36,128]{2,1,0:T(8,128)(2,1)S(1)}, bf16[32,36,128]{2,1,0:T(8,128)(2,1)}, u32[]{:S(2)}) copy-start(bf16[32,36,128]{2,1,0:T(8,128)(2,1)} %copy-done.2) | copy-start | bytes 884740
  417.7 13.7 %all-to-all-start.5 = ((f32[32,1,2048]{2,1,0:T(1,128)}), f32[32,1,2048]{2,1,0:T(1,128)}, u32[]{:S(2)}, u32[]{:S(2)}) async-start(f32[32,1,2048]{2,1,0:T(1,128)} %broadcast_in_dim.33), calls=%async_computation.5 | async-start | bytes 524288 | tf_op jit(solution)/shard_map/all_to_all | solution.py:245
  421.0 3.5 copy-start.6
  421.0 15.6 %copy-start.1 = (bf16[1,2048,768]{2,1,0:T(8,128)(2,1)S(1)}, bf16[1,2048,768]{2,1,0:T(8,128)(2,1)}, u32[]{:S(2)}) copy-start(bf16[1,2048,768]{2,1,0:T(8,128)(2,1)} %param.15) | copy-start | bytes 9437188

commit v9 on v8

--- a/solution.py
+++ b/solution.py
@@ -232,8 +232,9 @@
         tokens, logit_grad, contract_rows, preferred_element_type=jnp.float32
     )
     part_rows = router_part.reshape(devices, 1, -1)
-    part_high = part_rows.astype(jnp.bfloat16)
-    part_low = (part_rows - part_high.astype(jnp.float32)).astype(jnp.bfloat16)
+    part_rounded = lax.reduce_precision(part_rows, exponent_bits=8, mantissa_bits=7)
+    part_high = part_rounded.astype(jnp.bfloat16)
+    part_low = (part_rows - part_rounded).astype(jnp.bfloat16)
     send_back = jnp.concatenate([grad_rows, part_high, part_low], axis=1)
     got_back = lax.all_to_all(send_back, axes, split_axis=0, concat_axis=0, tiled=True)
     back_rows = got_back[:, :capacity, :]

time: 443 us -> 443 us (level)
  no operation moved by 1% of the time
where the time goes in v9:
time: 443 us; the launch traced here: 437 us
  waiting for transfers between devices  269 us (61%)
  matrix products  85.5 us (19%)
  starting transfers between devices  27.8 us (6%)
  other arithmetic  27.3 us (6%)
  local copies, waits for them, and re-layouts  26.2 us (6%)
    all_to_all x1, waiting for transfers between devices, body(): lax.all_to_all(grid_cot, axes, split_axis=0, concat_axis=0, tiled=True)  105 us
    all_to_all x1, waiting for transfers between devices, body(): lax.all_to_all(send_back, axes, split_axis=0, concat_axis=0, tiled=True)  86.3 us
    all_to_all x1, waiting for transfers between devices, body(): lax.all_to_all(send_b, axes, split_axis=0, concat_axis=0, tiled=True)  53.6 us
    all_to_all x1, waiting for transfers between devices, body(): lax.all_to_all(grid_tokens[:, :, :half], axes, split_axis=0, concat_axis=...  18.7 us
    dot_general x1, matrix products, expert_from_cot(): lax.dot_general(scaled_cot, down_matrix, last_t, preferred_element_type=j...  13.1 us
    dot_general x1, matrix products, expert_from_cot(): lax.dot_general(hidden, scaled_cot, grid_rows, preferred_element_type=jnp...  11.5 us
  transfers between devices with their start and end apart: 6, of which 5 were waited for; matrix products, arithmetic and copies ran while one was open for 26% of the time, Pallas kernels for 0%

profile of v9, /device:TPU:0, one launch (start us, length us, event | category | flops | bytes accessed | tf_op | source)
XLA Modules:
  0.0 436.9 jit_solution(9140356387352724027)
XLA Ops:
  6.2 7.3 %all-to-all-start = ((bf16[32,1,36]{2,1,0:T(2,128)(2,1)}), bf16[32,1,36]{2,1,0:T(2,128)(2,1)S(1)}, u32[]{:S(2)}, u32[]{:S(2)}) async-start(bf16[32,1,36]{2,1,0:T(2,128)(2,1)} %all_to_all.32), calls=%async_computation | async-start | bytes 32768 | tf_op jit(solution)/shard_map/all_to_all | solution.py:189
  13.7 6.8 %fusion.29 = bf16[1152,128]{1,0:T(8,128)(2,1)} fusion(s32[128,8]{0,1:T(8,128)S(1)} %multiply_add_fusion.1), kind=kLoop, calls=%fused_computation.44 | loop fusion | flops 3391488 | bytes 299008 | tf_op jit(solution)/shard_map/reduce_sum | solution.py:29
  21.5 5.0 %convolution_convert_fusion.1 = bf16[32,36,2048]{2,1,0:T(8,128)(2,1)} fusion(bf16[32,36,128]{2,1,0:T(8,128)(2,1)S(1)} %reshape.194, bf16[128,2048]{1,0:T(8,128)(2,1)} %param.10), kind=kOutput, calls=%fused_computation.21 | convolution fusion | flops 606339072 | bytes 5537792 | tf_op jit(solution)/shard_map/dot_general | solution.py:192
  26.5 6.2 %all-to-all-start.1 = ((bf16[32,36,2048]{2,1,0:T(8,128)(2,1)}), bf16[32,36,2048]{2,1,0:T(8,128)(2,1)}, u32[]{:S(2)}, u32[]{:S(2)}) async-start(bf16[32,36,2048]{2,1,0:T(8,128)(2,1)} %convolution_convert_fusion.1), calls=%async_computation.1 | async-start | bytes 10485760 | tf_op jit(solution)/shard_map/all_to_all | solution.py:196
  32.7 4.3 multiply_convert_fusion.3
  40.6 4.9 %convolution_convert_fusion = bf16[32,36,2048]{2,1,0:T(8,128)(2,1)} fusion(bf16[32,36,128]{2,1,0:T(8,128)(2,1)S(1)} %reshape.194, bf16[128,2048]{1,0:T(8,128)(2,1)} %param.9), kind=kOutput, calls=%fused_computation.20 | convolution fusion | flops 606339072 | bytes 5537792 | tf_op jit(solution)/shard_map/dot_general | solution.py:197
  45.5 104.7 %all-to-all-done.1 = bf16[32,36,2048]{2,1,0:T(8,128)(2,1)} async-done(((bf16[32,36,2048]{2,1,0:T(8,128)(2,1)}), bf16[32,36,2048]{2,1,0:T(8,128)(2,1)}, u32[]{:S(2)}, u32[]{:S(2)}) %all-to-all-start.1) | async-done | bytes 4718624 | tf_op jit(solution)/shard_map/all_to_all | solution.py:196
  150.2 4.8 %fusion.65 = (bf16[32,36,1024]{2,1,0:T(8,128)(2,1)}, bf16[32,36,1024]{2,1,0:T(8,128)(2,1)S(1)}) fusion(bf16[32,36,2048]{2,1,0:T(8,128)(2,1)} %convolution_convert_fusion), kind=kLoop, calls=%fused_computation.91 | loop fusion | bytes 9437184 | tf_op jit(solution)/shard_map/slice | solution.py:203
  155.0 6.4 %fusion.1 = bf16[32,36]{1,0:T(8,128)(2,1)S(1)} fusion(bf16[32,36,2048]{2,1,0:T(8,128)(2,1)} %all-to-all-done.1, bf16[32,36,768]{2,1,0:T(8,128)(2,1)S(1)} %copy-done.5, bf16[1,768,2048]{2,1,0:T(8,128)(2,1)S(1)} %copy-done.8), kind=kOutput, calls=%fused_computation.3 | convolution fusion | flops 3635674112 | bytes 9636096 | tf_op jit(solution)/shard_map/dot_general | solution.py:141
  170.9 3.9 reshape.196
  174.8 53.6 %all-to-all-done.2 = bf16[32,37,1024]{2,1,0:T(8,128)(2,1)} async-done(((bf16[32,37,1024]{2,1,0:T(8,128)(2,1)}), bf16[32,37,1024]{2,1,0:T(8,128)(2,1)}, u32[]{:S(2)}, u32[]{:S(2)}) %all-to-all-start.2) | async-done | bytes 2424864 | tf_op jit(solution)/shard_map/all_to_all | solution.py:220
  232.2 13.1 %multiply_convert_fusion.1 = (bf16[32,36,768]{2,1,0:T(8,128)(2,1)}, bf16[32,36,768]{2,1,0:T(8,128)(2,1)}) fusion(f32[32,36,768]{2,1,0:T(8,128)} %reshape.197, f32[32,36,768]{2,1,0:T(8,128)} %reshape.196, bf16[1,768,2048]{2,1,0:T(8,128)(2,1)} %param.17, bf16[32,36,2048]{2,1,0:T(8,128)(2,1)} %all-to-all-done.1, f32[32,36]{1,0:T(8,128)S(1)} %convert_element_type.151), kind=kOutput, calls=%fused_computation.23 | convolution fusion | flops 3642458112 | bytes 18485760 | tf_op jit(solution)/shard_map/dot_general | solution.py:147
  245.3 6.0 %fusion.18 = f32[32,36,2048]{2,1,0:T(8,128)S(1)} fusion(bf16[32,36,768]{2,1,0:T(8,128)(2,1)} %get-tuple-element.39, bf16[1,2048,768]{2,1,0:T(8,128)(2,1)S(1)} %copy-done), kind=kOutput, calls=%fused_computation.35 | convolution fusion | flops 3623878656 | bytes 14352384 | tf_op jit(solution)/shard_map/dot_general | solution.py:155
  251.3 8.4 %add_convert_fusion = bf16[32,36,2048]{2,1,0:T(8,128)(2,1)} fusion(f32[32,36,2048]{2,1,0:T(8,128)S(1)} %fusion.18, bf16[32,36,768]{2,1,0:T(8,128)(2,1)} %get-tuple-element.38, bf16[1,2048,768]{2,1,0:T(8,128)(2,1)S(1)} %copy-done.9), kind=kOutput, calls=%fused_computation.4 | convolution fusion | flops 3628597248 | bytes 19070976 | tf_op jit(solution)/shard_map/dot_general | solution.py:156
  260.8 5.9 %fusion.7 = f32[1,128,8]{2,0,1:T(1,128)S(1)} fusion(bf16[1152,1,1]{0,1,2:T(2,128)(2,1)S(1)} %reshape.205, s32[1024]{0:T(1024)S(1)} %multiply_add_fusion), kind=kOutput, calls=%fused_computation.15 | convolution fusion | flops 3538944 | bytes 10496 | tf_op jit(solution)/shard_map/dot_general | solution.py:223
  268.4 6.5 %pad_maximum_fusion = bf16[32,38,2048]{2,1,0:T(8,128)(2,1)} fusion(bf16[32,1,2048]{2,1,0:T(2,128)(2,1)S(1)} %copy.67, bf16[32,1,2048]{2,1,0:T(2,128)(2,1)S(1)} %copy.66, bf16[32,36,2048]{2,1,0:T(8,128)(2,1)} %add_convert_fusion), kind=kLoop, calls=%fused_computation.8 | loop fusion | flops 14942208 | bytes 9961472 | tf_op jit(solution)/shard_map/concatenate | solution.py:238
  274.9 18.7 %all-to-all-done.4 = bf16[32,36,1024]{2,1,0:T(8,128)(2,1)} async-done(((bf16[32,36,1024]{2,1,0:T(8,128)(2,1)}), bf16[32,36,1024]{2,1,0:T(8,128)(2,1)}, u32[]{:S(2)}, u32[]{:S(2)}) %all-to-all-start.4) | async-done | bytes 2359328 | tf_op jit(solution)/shard_map/all_to_all | solution.py:202
  297.3 11.5 %fusion.22 = bf16[1,768,2048]{2,1,0:T(8,128)(2,1)} fusion(bf16[32,36,2048]{2,1,0:T(8,128)(2,1)} %all-to-all-done.1, f32[32,36]{1,0:T(8,128)S(1)} %convert_element_type.151, f32[32,36,768]{2,1,0:T(8,128)} %reshape.196, f32[32,36,768]{2,1,0:T(8,128)} %reshape.197), kind=kOutput, calls=%fused_computation.39 | convolution fusion | flops 3637837824 | bytes 14946816 | tf_op jit(solution)/shard_map/dot_general | solution.py:158
  308.8 4.1 fusion.44
  313.0 4.1 fusion.40
  317.0 4.0 fusion.45
  321.0 4.3 fusion.41
  328.4 86.3 %all-to-all-done.3 = bf16[32,38,2048]{2,1,0:T(8,128)(2,1)} async-done(((bf16[32,38,2048]{2,1,0:T(8,128)(2,1)}), bf16[32,38,2048]{2,1,0:T(8,128)(2,1)}, u32[]{:S(2)}, u32[]{:S(2)}) %all-to-all-start.3) | async-done | bytes 4980768 | tf_op jit(solution)/shard_map/all_to_all | solution.py:239
  425.7 5.7 %all-to-all-done.5 = f32[32,1,2048]{2,1,0:T(1,128)} async-done(((f32[32,1,2048]{2,1,0:T(1,128)}), f32[32,1,2048]{2,1,0:T(1,128)}, u32[]{:S(2)}, u32[]{:S(2)}) %all-to-all-start.5) | async-done | bytes 262176 | tf_op jit(solution)/shard_map/all_to_all | solution.py:246
  (72 shorter events, 49.3 us)
Async XLA Ops:
  0.6 244.6 %copy-start = (bf16[1,2048,768]{2,1,0:T(8,128)(2,1)S(1)}, bf16[1,2048,768]{2,1,0:T(8,128)(2,1)}, u32[]{:S(2)}) copy-start(bf16[1,2048,768]{2,1,0:T(8,128)(2,1)} %param.15) | copy-start | bytes 9437188
  0.6 13.0 %copy-start.7 = (s32[128,8]{0,1:T(8,128)S(1)}, s32[128,8]{0,1:T(8,128)}, u32[]{:S(2)}) copy-start(s32[128,8]{0,1:T(8,128)} %param.11) | copy-start | bytes 12292
  6.2 20.3 %all-to-all-start = ((bf16[32,1,36]{2,1,0:T(2,128)(2,1)}), bf16[32,1,36]{2,1,0:T(2,128)(2,1)S(1)}, u32[]{:S(2)}, u32[]{:S(2)}) async-start(bf16[32,1,36]{2,1,0:T(2,128)(2,1)} %all_to_all.32), calls=%async_computation | async-start | bytes 32768 | tf_op jit(solution)/shard_map/all_to_all | solution.py:189
  21.5 19.1 %copy-start.2 = (bf16[32,36,128]{2,1,0:T(8,128)(2,1)}, bf16[32,36,128]{2,1,0:T(8,128)(2,1)S(1)}, u32[]{:S(2)}) copy-start(bf16[32,36,128]{2,1,0:T(8,128)(2,1)S(1)} %reshape.194) | copy-start | bytes 884740
  26.5 123.7 %all-to-all-start.1 = ((bf16[32,36,2048]{2,1,0:T(8,128)(2,1)}), bf16[32,36,2048]{2,1,0:T(8,128)(2,1)}, u32[]{:S(2)}, u32[]{:S(2)}) async-start(bf16[32,36,2048]{2,1,0:T(8,128)(2,1)} %convolution_convert_fusion.1), calls=%async_computation.1 | async-start | bytes 10485760 | tf_op jit(solution)/shard_map/all_to_all | solution.py:196
  150.2 4.8 %copy-start.5 = (bf16[32,36,768]{2,1,0:T(8,128)(2,1)S(1)}, bf16[32,36,768]{2,1,0:T(8,128)(2,1)}, u32[]{:S(2)}) copy-start(bf16[32,36,768]{2,1,0:T(8,128)(2,1)} %convert_element_type.165) | copy-start | bytes 5308420
  150.2 4.8 %copy-start.8 = (bf16[1,768,2048]{2,1,0:T(8,128)(2,1)S(1)}, bf16[1,768,2048]{2,1,0:T(8,128)(2,1)}, u32[]{:S(2)}) copy-start(bf16[1,768,2048]{2,1,0:T(8,128)(2,1)} %param.17) | copy-start | bytes 9437188
  163.5 64.9 %all-to-all-start.2 = ((bf16[32,37,1024]{2,1,0:T(8,128)(2,1)}), bf16[32,37,1024]{2,1,0:T(8,128)(2,1)}, u32[]{:S(2)}, u32[]{:S(2)}) async-start(bf16[32,37,1024]{2,1,0:T(8,128)(2,1)} %pad_maximum_fusion.3), calls=%async_computation.2 | async-start | bytes 5242880 | tf_op jit(solution)/shard_map/all_to_all | solution.py:220
  228.4 65.1 %all-to-all-start.4 = ((bf16[32,36,1024]{2,1,0:T(8,128)(2,1)}), bf16[32,36,1024]{2,1,0:T(8,128)(2,1)}, u32[]{:S(2)}, u32[]{:S(2)}) async-start(bf16[32,36,1024]{2,1,0:T(8,128)(2,1)} %get-tuple-element.40), calls=%async_computation.4 | async-start | bytes 5242880 | tf_op jit(solution)/shard_map/all_to_all | solution.py:202
  245.3 6.1 %copy-start.9 = (bf16[1,2048,768]{2,1,0:T(8,128)(2,1)S(1)}, bf16[1,2048,768]{2,1,0:T(8,128)(2,1)}, u32[]{:S(2)}) copy-start(bf16[1,2048,768]{2,1,0:T(8,128)(2,1)} %param.16) | copy-start | bytes 9437188
  251.3 15.6 %copy-start.4 = (bf16[128,2048]{1,0:T(8,128)(2,1)S(1)}, bf16[128,2048]{1,0:T(8,128)(2,1)}, u32[]{:S(2)}) copy-start(bf16[128,2048]{1,0:T(8,128)(2,1)} %param.9) | copy-start | bytes 1572868
  293.6 121.1 %all-to-all-start.3 = ((bf16[32,38,2048]{2,1,0:T(8,128)(2,1)}), bf16[32,38,2048]{2,1,0:T(8,128)(2,1)}, u32[]{:S(2)}, u32[]{:S(2)}) async-start(bf16[32,38,2048]{2,1,0:T(8,128)(2,1)} %pad_maximum_fusion), calls=%async_computation.3 | async-start | bytes 10485760 | tf_op jit(solution)/shard_map/all_to_all | solution.py:239
  297.3 11.5 %copy-start.10 = (bf16[32,36,768]{2,1,0:T(8,128)(2,1)S(1)}, bf16[32,36,768]{2,1,0:T(8,128)(2,1)}, u32[]{:S(2)}) copy-start(bf16[32,36,768]{2,1,0:T(8,128)(2,1)} %get-tuple-element.38) | copy-start | bytes 5308420
  308.8 4.2 copy-start.11
  325.3 95.7 %copy-start.3 = (bf16[32,36,128]{2,1,0:T(8,128)(2,1)S(1)}, bf16[32,36,128]{2,1,0:T(8,128)(2,1)}, u32[]{:S(2)}) copy-start(bf16[32,36,128]{2,1,0:T(8,128)(2,1)} %copy-done.2) | copy-start | bytes 884740
  417.7 13.7 %all-to-all-start.5 = ((f32[32,1,2048]{2,1,0:T(1,128)}), f32[32,1,2048]{2,1,0:T(1,128)}, u32[]{:S(2)}, u32[]{:S(2)}) async-start(f32[32,1,2048]{2,1,0:T(1,128)} %broadcast_in_dim.33), calls=%async_computation.5 | async-start | bytes 524288 | tf_op jit(solution)/shard_map/all_to_all | solution.py:246
  421.0 3.5 copy-start.6
  421.0 15.6 %copy-start.1 = (bf16[1,2048,768]{2,1,0:T(8,128)(2,1)S(1)}, bf16[1,2048,768]{2,1,0:T(8,128)(2,1)}, u32[]{:S(2)}) copy-start(bf16[1,2048,768]{2,1,0:T(8,128)(2,1)} %param.15) | copy-start | bytes 9437188

commit v10 on v9

--- a/solution.py
+++ b/solution.py
@@ -186,14 +186,14 @@
     send_weight = jnp.dot(slot_table, probs_low, preferred_element_type=jnp.float32).astype(
         jnp.bfloat16
     )
-    got_weight = lax.all_to_all(
-        send_weight.reshape(experts, capacity), axes, split_axis=0, concat_axis=0, tiled=True
-    )
+    weight_row = jnp.pad(send_weight.reshape(experts, capacity), ((0, 0), (0, width - capacity)))
     grid_cot = jnp.dot(grid_table, cotangent, preferred_element_type=jnp.float32).astype(
         jnp.bfloat16
     )
-    got_weight, grid_cot = lax.optimization_barrier((got_weight, grid_cot))
-    got_cot = lax.all_to_all(grid_cot, axes, split_axis=0, concat_axis=0, tiled=True)
+    send_cot = jnp.concatenate([grid_cot, weight_row[:, None, :]], axis=1)
+    got_cot_w = lax.all_to_all(send_cot, axes, split_axis=0, concat_axis=0, tiled=True)
+    got_cot = got_cot_w[:, :capacity, :]
+    got_weight = got_cot_w[:, capacity, :capacity]
     grid_tokens = jnp.dot(grid_table, tokens, preferred_element_type=jnp.float32).astype(
         jnp.bfloat16
     )
@@ -217,6 +217,7 @@
     ).astype(jnp.bfloat16)
     dot_row = jnp.pad(slot_route_dot, ((0, 0), (0, half - capacity)))[:, None, :]
     send_b = jnp.concatenate([grid_tokens[:, :, half:], dot_row], axis=1)
+    send_b, got_tokens_a = lax.optimization_barrier((send_b, got_tokens_a))
     got_b = lax.all_to_all(send_b, axes, split_axis=0, concat_axis=0, tiled=True)
     got_tokens_b = got_b[:, :capacity, :]
     route_dot = got_b[:, capacity, :capacity].reshape(-1)

time: 443 us -> 448 us (1.011)
  starting transfers between devices: 27.8 us -> 22 us
    all_to_all x1, waiting for transfers between devices: 53.6 us -> 25 us  [body(): lax.all_to_all(send_b, axes, split_axis=0, concat_axis=0, tiled=True)]
    all_to_all x1, waiting for transfers between devices: 18.7 us -> 42.7 us  [body(): lax.all_to_all(grid_tokens[:, :, :half], axes, split_axis=0, concat_axis=...]
    all_to_all x2 -> x1, waiting for transfers between devices: 105 us -> 113 us  [body(): lax.all_to_all(send_cot, axes, split_axis=0, concat_axis=0, tiled=True)]
    all_to_all x2 -> x1, starting transfers between devices: 13.5 us -> 7.41 us  [body(): lax.all_to_all(send_cot, axes, split_axis=0, concat_axis=0, tiled=True)]
  transfers between devices with their start and end apart: 6 -> 5, of which waited for: 5 -> 5; matrix products, arithmetic and copies ran while one was open for 26% -> 22% of each run, Pallas kernels for 0% -> 0%
where the time goes in v10:
time: 448 us; the launch traced here: 440 us
  waiting for transfers between devices  272 us (61%)
  matrix products  85.4 us (19%)
  other arithmetic  31.5 us (7%)
  local copies, waits for them, and re-layouts  27.2 us (6%)
  starting transfers between devices  22 us (5%)
    all_to_all x1, waiting for transfers between devices, body(): lax.all_to_all(send_cot, axes, split_axis=0, concat_axis=0, tiled=True)  113 us
    all_to_all x1, waiting for transfers between devices, body(): lax.all_to_all(send_back, axes, split_axis=0, concat_axis=0, tiled=True)  86.3 us
    all_to_all x1, waiting for transfers between devices, body(): lax.all_to_all(grid_tokens[:, :, :half], axes, split_axis=0, concat_axis=...  42.7 us
    all_to_all x1, waiting for transfers between devices, body(): lax.all_to_all(send_b, axes, split_axis=0, concat_axis=0, tiled=True)  25 us
    dot_general x1, matrix products, expert_from_cot(): lax.dot_general(scaled_cot, down_matrix, last_t, preferred_element_type=j...  13.2 us
    dot_general x1, matrix products, expert_from_cot(): lax.dot_general(hidden, scaled_cot, grid_rows, preferred_element_type=jnp...  11.5 us
  transfers between devices with their start and end apart: 5, of which 5 were waited for; matrix products, arithmetic and copies ran while one was open for 22% of the time, Pallas kernels for 0%

profile of v10, /device:TPU:0, one launch (start us, length us, event | category | flops | bytes accessed | tf_op | source)
XLA Modules:
  0.0 439.5 jit_solution(15690355902326055954)
XLA Ops:
  6.7 6.7 %fusion.29 = bf16[1152,128]{1,0:T(8,128)(2,1)} fusion(s32[128,8]{0,1:T(8,128)S(1)} %multiply_add_fusion.1), kind=kLoop, calls=%fused_computation.45 | loop fusion | flops 3391488 | bytes 299008 | tf_op jit(solution)/shard_map/reduce_sum | solution.py:29
  20.5 7.4 %all-to-all-start = ((bf16[32,37,2048]{2,1,0:T(8,128)(2,1)}), bf16[32,37,2048]{2,1,0:T(8,128)(2,1)}, u32[]{:S(2)}, u32[]{:S(2)}) async-start(bf16[32,37,2048]{2,1,0:T(8,128)(2,1)} %pad_maximum_fusion), calls=%async_computation | async-start | bytes 10485760 | tf_op jit(solution)/shard_map/all_to_all | solution.py:194
  27.9 4.9 %convolution_convert_fusion = bf16[32,36,2048]{2,1,0:T(8,128)(2,1)} fusion(bf16[32,36,128]{2,1,0:T(8,128)(2,1)S(1)} %reshape.199, bf16[128,2048]{1,0:T(8,128)(2,1)} %param.9), kind=kOutput, calls=%fused_computation.21 | convolution fusion | flops 606339072 | bytes 5537792 | tf_op jit(solution)/shard_map/dot_general | solution.py:197
  32.8 112.6 %all-to-all-done = bf16[32,37,2048]{2,1,0:T(8,128)(2,1)} async-done(((bf16[32,37,2048]{2,1,0:T(8,128)(2,1)}), bf16[32,37,2048]{2,1,0:T(8,128)(2,1)}, u32[]{:S(2)}, u32[]{:S(2)}) %all-to-all-start) | async-done | bytes 4849696 | tf_op jit(solution)/shard_map/all_to_all | solution.py:194
  145.4 5.5 %fusion.65 = (bf16[32,36,1024]{2,1,0:T(8,128)(2,1)}, bf16[32,36,1024]{2,1,0:T(8,128)(2,1)}) fusion(bf16[32,36,2048]{2,1,0:T(8,128)(2,1)} %convolution_convert_fusion), kind=kLoop, calls=%fused_computation.93 | loop fusion | bytes 9437184 | tf_op jit(solution)/shard_map/slice | solution.py:203
  154.7 4.4 multiply_convert_fusion.3
  162.6 8.6 %fusion.1 = bf16[32,36]{1,0:T(8,128)(2,1)S(1)} fusion(bf16[32,36,2048]{2,1,0:T(8,128)(2,1)} %bitcast.91, bf16[32,36,768]{2,1,0:T(8,128)(2,1)} %convert_element_type.175, bf16[1,768,2048]{2,1,0:T(8,128)(2,1)} %param.17), kind=kOutput, calls=%fused_computation.3 | convolution fusion | flops 3635674112 | bytes 9636096 | tf_op jit(solution)/shard_map/dot_general | solution.py:141
  173.4 42.7 %all-to-all-done.1 = bf16[32,36,1024]{2,1,0:T(8,128)(2,1)} async-done(((bf16[32,36,1024]{2,1,0:T(8,128)(2,1)}), bf16[32,36,1024]{2,1,0:T(8,128)(2,1)}, u32[]{:S(2)}, u32[]{:S(2)}) %all-to-all-start.1) | async-done | bytes 2359328 | tf_op jit(solution)/shard_map/all_to_all | solution.py:202
  216.0 3.8 all-to-all-start.2
  219.8 3.9 reshape.204
  223.7 3.9 reshape.203
  228.4 13.2 %multiply_convert_fusion.1 = (bf16[32,36,768]{2,1,0:T(8,128)(2,1)}, bf16[32,36,768]{2,1,0:T(8,128)(2,1)}) fusion(f32[32,36,768]{2,1,0:T(8,128)} %reshape.204, f32[32,36,768]{2,1,0:T(8,128)} %reshape.203, bf16[1,768,2048]{2,1,0:T(8,128)(2,1)} %param.17, bf16[32,36,2048]{2,1,0:T(8,128)(2,1)} %bitcast.91, f32[32,36]{1,0:T(8,128)S(1)} %bitcast.92), kind=kOutput, calls=%fused_computation.24 | convolution fusion | flops 3642458112 | bytes 18485760 | tf_op jit(solution)/shard_map/dot_general | solution.py:147
  241.6 6.0 %fusion.18 = f32[32,36,2048]{2,1,0:T(8,128)S(1)} fusion(bf16[32,36,768]{2,1,0:T(8,128)(2,1)} %get-tuple-element.34, bf16[1,2048,768]{2,1,0:T(8,128)(2,1)S(1)} %copy-done), kind=kOutput, calls=%fused_computation.36 | convolution fusion | flops 3623878656 | bytes 14352384 | tf_op jit(solution)/shard_map/dot_general | solution.py:155
  247.7 8.5 %add_convert_fusion = bf16[32,36,2048]{2,1,0:T(8,128)(2,1)} fusion(f32[32,36,2048]{2,1,0:T(8,128)S(1)} %fusion.18, bf16[32,36,768]{2,1,0:T(8,128)(2,1)} %get-tuple-element.33, bf16[1,2048,768]{2,1,0:T(8,128)(2,1)S(1)} %copy-done.9), kind=kOutput, calls=%fused_computation.4 | convolution fusion | flops 3628597248 | bytes 19070976 | tf_op jit(solution)/shard_map/dot_general | solution.py:156
  256.1 25.0 %all-to-all-done.2 = bf16[32,37,1024]{2,1,0:T(8,128)(2,1)} async-done(((bf16[32,37,1024]{2,1,0:T(8,128)(2,1)}), bf16[32,37,1024]{2,1,0:T(8,128)(2,1)}, u32[]{:S(2)}, u32[]{:S(2)}) %all-to-all-start.2) | async-done | bytes 2424864 | tf_op jit(solution)/shard_map/all_to_all | solution.py:221
  282.2 5.9 %fusion.7 = f32[1,128,8]{2,0,1:T(1,128)S(1)} fusion(bf16[1152,1,1]{0,1,2:T(2,128)(2,1)S(1)} %reshape.212, s32[1024]{0:T(1024)S(1)} %multiply_add_fusion), kind=kOutput, calls=%fused_computation.16 | convolution fusion | flops 3538944 | bytes 10496 | tf_op jit(solution)/shard_map/dot_general | solution.py:224
  289.8 6.5 %pad_maximum_fusion.1 = bf16[32,38,2048]{2,1,0:T(8,128)(2,1)} fusion(bf16[32,1,2048]{2,1,0:T(2,128)(2,1)S(1)} %copy.58, bf16[32,1,2048]{2,1,0:T(2,128)(2,1)S(1)} %copy.57, bf16[32,36,2048]{2,1,0:T(8,128)(2,1)} %add_convert_fusion), kind=kLoop, calls=%fused_computation.9 | loop fusion | flops 14942208 | bytes 9961472 | tf_op jit(solution)/shard_map/concatenate | solution.py:239
  300.0 11.5 %fusion.22 = bf16[1,768,2048]{2,1,0:T(8,128)(2,1)} fusion(bf16[32,36,2048]{2,1,0:T(8,128)(2,1)} %bitcast.91, f32[32,36]{1,0:T(8,128)S(1)} %bitcast.93, f32[32,36,768]{2,1,0:T(8,128)} %reshape.203, f32[32,36,768]{2,1,0:T(8,128)} %reshape.204), kind=kOutput, calls=%fused_computation.40 | convolution fusion | flops 3637837824 | bytes 14946816 | tf_op jit(solution)/shard_map/dot_general | solution.py:158
  311.5 4.1 fusion.44
  315.6 4.1 fusion.40
  319.7 4.0 fusion.45
  323.7 4.3 fusion.41
  331.1 86.3 %all-to-all-done.3 = bf16[32,38,2048]{2,1,0:T(8,128)(2,1)} async-done(((bf16[32,38,2048]{2,1,0:T(8,128)(2,1)}), bf16[32,38,2048]{2,1,0:T(8,128)(2,1)}, u32[]{:S(2)}, u32[]{:S(2)}) %all-to-all-start.3) | async-done | bytes 4980768 | tf_op jit(solution)/shard_map/all_to_all | solution.py:240
  428.4 5.7 %all-to-all-done.4 = f32[32,1,2048]{2,1,0:T(1,128)} async-done(((f32[32,1,2048]{2,1,0:T(1,128)}), f32[32,1,2048]{2,1,0:T(1,128)}, u32[]{:S(2)}, u32[]{:S(2)}) %all-to-all-start.4) | async-done | bytes 262176 | tf_op jit(solution)/shard_map/all_to_all | solution.py:247
  (72 shorter events, 49.0 us)
Async XLA Ops:
  0.6 241.0 %copy-start = (bf16[1,2048,768]{2,1,0:T(8,128)(2,1)S(1)}, bf16[1,2048,768]{2,1,0:T(8,128)(2,1)}, u32[]{:S(2)}) copy-start(bf16[1,2048,768]{2,1,0:T(8,128)(2,1)} %param.15) | copy-start | bytes 9437188
  0.6 5.1 %copy-start.8 = (s32[128,8]{0,1:T(8,128)S(1)}, s32[128,8]{0,1:T(8,128)}, u32[]{:S(2)}) copy-start(s32[128,8]{0,1:T(8,128)} %param.11) | copy-start | bytes 12292
  14.4 13.5 %copy-start.3 = (bf16[32,36,128]{2,1,0:T(8,128)(2,1)}, bf16[32,36,128]{2,1,0:T(8,128)(2,1)S(1)}, u32[]{:S(2)}) copy-start(bf16[32,36,128]{2,1,0:T(8,128)(2,1)S(1)} %reshape.199) | copy-start | bytes 884740
  14.5 2.7 copy-start.6
  20.5 124.9 %all-to-all-start = ((bf16[32,37,2048]{2,1,0:T(8,128)(2,1)}), bf16[32,37,2048]{2,1,0:T(8,128)(2,1)}, u32[]{:S(2)}, u32[]{:S(2)}) async-start(bf16[32,37,2048]{2,1,0:T(8,128)(2,1)} %pad_maximum_fusion), calls=%async_computation | async-start | bytes 10485760 | tf_op jit(solution)/shard_map/all_to_all | solution.py:194
  150.9 65.1 %all-to-all-start.1 = ((bf16[32,36,1024]{2,1,0:T(8,128)(2,1)}), bf16[32,36,1024]{2,1,0:T(8,128)(2,1)}, u32[]{:S(2)}, u32[]{:S(2)}) async-start(bf16[32,36,1024]{2,1,0:T(8,128)(2,1)} %get-tuple-element.35), calls=%async_computation.1 | async-start | bytes 5242880 | tf_op jit(solution)/shard_map/all_to_all | solution.py:202
  162.6 8.7 %copy-start.2 = (bf16[32,36,1024]{2,1,0:T(8,128)(2,1)S(1)}, bf16[32,36,1024]{2,1,0:T(8,128)(2,1)}, u32[]{:S(2)}) copy-start(bf16[32,36,1024]{2,1,0:T(8,128)(2,1)} %get-tuple-element.36) | copy-start | bytes 7077892
  216.0 65.1 %all-to-all-start.2 = ((bf16[32,37,1024]{2,1,0:T(8,128)(2,1)}), bf16[32,37,1024]{2,1,0:T(8,128)(2,1)}, u32[]{:S(2)}, u32[]{:S(2)}) async-start(bf16[32,37,1024]{2,1,0:T(8,128)(2,1)} %pad_maximum_fusion.4), calls=%async_computation.2 | async-start | bytes 5242880 | tf_op jit(solution)/shard_map/all_to_all | solution.py:221
  241.6 6.1 %copy-start.9 = (bf16[1,2048,768]{2,1,0:T(8,128)(2,1)S(1)}, bf16[1,2048,768]{2,1,0:T(8,128)(2,1)}, u32[]{:S(2)}) copy-start(bf16[1,2048,768]{2,1,0:T(8,128)(2,1)} %param.16) | copy-start | bytes 9437188
  247.7 40.6 %copy-start.5 = (bf16[128,2048]{1,0:T(8,128)(2,1)S(1)}, bf16[128,2048]{1,0:T(8,128)(2,1)}, u32[]{:S(2)}) copy-start(bf16[128,2048]{1,0:T(8,128)(2,1)} %param.9) | copy-start | bytes 1572868
  296.2 121.1 %all-to-all-start.3 = ((bf16[32,38,2048]{2,1,0:T(8,128)(2,1)}), bf16[32,38,2048]{2,1,0:T(8,128)(2,1)}, u32[]{:S(2)}, u32[]{:S(2)}) async-start(bf16[32,38,2048]{2,1,0:T(8,128)(2,1)} %pad_maximum_fusion.1), calls=%async_computation.3 | async-start | bytes 10485760 | tf_op jit(solution)/shard_map/all_to_all | solution.py:240
  300.0 11.5 %copy-start.10 = (bf16[32,36,768]{2,1,0:T(8,128)(2,1)S(1)}, bf16[32,36,768]{2,1,0:T(8,128)(2,1)}, u32[]{:S(2)}) copy-start(bf16[32,36,768]{2,1,0:T(8,128)(2,1)} %get-tuple-element.33) | copy-start | bytes 5308420
  311.5 4.2 copy-start.11
  328.0 95.7 %copy-start.4 = (bf16[32,36,128]{2,1,0:T(8,128)(2,1)S(1)}, bf16[32,36,128]{2,1,0:T(8,128)(2,1)}, u32[]{:S(2)}) copy-start(bf16[32,36,128]{2,1,0:T(8,128)(2,1)} %copy-done.3) | copy-start | bytes 884740
  420.4 13.7 %all-to-all-start.4 = ((f32[32,1,2048]{2,1,0:T(1,128)}), f32[32,1,2048]{2,1,0:T(1,128)}, u32[]{:S(2)}, u32[]{:S(2)}) async-start(f32[32,1,2048]{2,1,0:T(1,128)} %broadcast_in_dim.36), calls=%async_computation.4 | async-start | bytes 524288 | tf_op jit(solution)/shard_map/all_to_all | solution.py:247
  423.7 3.5 copy-start.7
  423.7 15.6 %copy-start.1 = (bf16[1,2048,768]{2,1,0:T(8,128)(2,1)S(1)}, bf16[1,2048,768]{2,1,0:T(8,128)(2,1)}, u32[]{:S(2)}) copy-start(bf16[1,2048,768]{2,1,0:T(8,128)(2,1)} %param.15) | copy-start | bytes 9437188

commit v11 on v10

--- a/solution.py
+++ b/solution.py
@@ -129,18 +129,26 @@
     return (grad_tokens, router_part)
 
 
-def expert_from_cot(cot_rows, weight_rows, gate_pre, up_pre, gate_matrix, up_matrix, down_matrix):
+def expert_local(gate_pre, up_pre, down_matrix):
     last = (((2,), (0,)), ((), ()))
+    gate_value = gate_pre.astype(jnp.float32)
+    sigmoid_gate = jax.nn.sigmoid(gate_value)
+    hidden = (gate_value * sigmoid_gate * up_pre.astype(jnp.float32)).astype(jnp.bfloat16)
+    expert_out = lax.dot_general(
+        hidden, down_matrix, last, preferred_element_type=jnp.float32
+    ).astype(jnp.bfloat16)
+    return hidden, expert_out
+
+
+def expert_from_cot(
+    cot_rows, weight_rows, gate_pre, up_pre, gate_matrix, up_matrix, down_matrix, hidden
+):
     last_t = (((2,), (1,)), ((), ()))
     grid_rows = (((0, 1), (0, 1)), ((), ()))
     gate_value = gate_pre.astype(jnp.float32)
     up_value = up_pre.astype(jnp.float32)
     sigmoid_gate = jax.nn.sigmoid(gate_value)
     silu_gate = gate_value * sigmoid_gate
-    hidden = (silu_gate * up_value).astype(jnp.bfloat16)
-    expert_out = lax.dot_general(
-        hidden, down_matrix, last, preferred_element_type=jnp.float32
-    ).astype(jnp.bfloat16)
     scaled_cot = (
         weight_rows.astype(jnp.float32)[:, :, None] * cot_rows.astype(jnp.float32)
     ).astype(jnp.bfloat16)
@@ -158,7 +166,7 @@
     grad_down_w = lax.dot_general(
         hidden, scaled_cot, grid_rows, preferred_element_type=jnp.float32
     ).astype(jnp.bfloat16)
-    return (grad_rows, expert_out, grad_gate_pre, grad_up_pre, grad_down_w)
+    return (grad_rows, grad_gate_pre, grad_up_pre, grad_down_w)
 
 
 def body(
@@ -192,6 +200,10 @@
     )
     send_cot = jnp.concatenate([grid_cot, weight_row[:, None, :]], axis=1)
     got_cot_w = lax.all_to_all(send_cot, axes, split_axis=0, concat_axis=0, tiled=True)
+    gate_grid = gate_saved[0].reshape(experts, capacity, -1)
+    up_grid = up_saved[0].reshape(experts, capacity, -1)
+    hidden, expert_out = expert_local(gate_grid, up_grid, down_weight[0])
+    got_cot_w, hidden, expert_out = lax.optimization_barrier((got_cot_w, hidden, expert_out))
     got_cot = got_cot_w[:, :capacity, :]
     got_weight = got_cot_w[:, capacity, :capacity]
     grid_tokens = jnp.dot(grid_table, tokens, preferred_element_type=jnp.float32).astype(
@@ -203,21 +215,21 @@
         grid_tokens[:, :, :half], axes, split_axis=0, concat_axis=0, tiled=True
     )
     cot_rows = got_cot
-    grad_rows, expert_out, grad_gate_pre, grad_up_pre, grad_down_w = expert_from_cot(
+    grad_rows, grad_gate_pre, grad_up_pre, grad_down_w = expert_from_cot(
         cot_rows,
         got_weight,
-        gate_saved[0].reshape(experts, capacity, -1),
-        up_saved[0].reshape(experts, capacity, -1),
+        gate_grid,
+        up_grid,
         gate_weight[0],
         up_weight[0],
         down_weight[0],
+        hidden,
     )
     slot_route_dot = jnp.sum(
         cot_rows.astype(jnp.float32) * expert_out.astype(jnp.float32), axis=2
     ).astype(jnp.bfloat16)
     dot_row = jnp.pad(slot_route_dot, ((0, 0), (0, half - capacity)))[:, None, :]
     send_b = jnp.concatenate([grid_tokens[:, :, half:], dot_row], axis=1)
-    send_b, got_tokens_a = lax.optimization_barrier((send_b, got_tokens_a))
     got_b = lax.all_to_all(send_b, axes, split_axis=0, concat_axis=0, tiled=True)
     got_tokens_b = got_b[:, :capacity, :]
     route_dot = got_b[:, capacity, :capacity].reshape(-1)

time: 448 us -> 437 us (0.975)
  waiting for transfers between devices: 272 us -> 261 us
  other arithmetic: 31.5 us -> 40.4 us
  matrix products: 85.4 us -> 78.9 us
    all_to_all x1, waiting for transfers between devices: 25 us -> 60.5 us  [body(): lax.all_to_all(send_b, axes, split_axis=0, concat_axis=0, tiled=True)]
    all_to_all x1, waiting for transfers between devices: 113 us -> 85.9 us  [body(): lax.all_to_all(send_cot, axes, split_axis=0, concat_axis=0, tiled=True)]
    all_to_all x1, waiting for transfers between devices: 42.7 us -> 19.6 us  [body(): lax.all_to_all(grid_tokens[:, :, :half], axes, split_axis=0, concat_axis=...]
    convert_element_type x1 -> x2, other arithmetic: 4.37 us -> 9.1 us  [expert_local(): (gate_value * sigmoid_gate * up_pre.astype(jnp.float32)).astype(jnp.bfloa...]
  transfers between devices with their start and end apart: 5 -> 5, of which waited for: 5 -> 5; matrix products, arithmetic and copies ran while one was open for 22% -> 25% of each run, Pallas kernels for 0% -> 0%
where the time goes in v11:
time: 437 us; the launch traced here: 430 us
  waiting for transfers between devices  261 us (60%)
  matrix products  78.9 us (18%)
  other arithmetic  40.4 us (9%)
  local copies, waits for them, and re-layouts  26.6 us (6%)
  starting transfers between devices  22 us (5%)
    all_to_all x1, waiting for transfers between devices, body(): lax.all_to_all(send_back, axes, split_axis=0, concat_axis=0, tiled=True)  89 us
    all_to_all x1, waiting for transfers between devices, body(): lax.all_to_all(send_cot, axes, split_axis=0, concat_axis=0, tiled=True)  85.9 us
    all_to_all x1, waiting for transfers between devices, body(): lax.all_to_all(send_b, axes, split_axis=0, concat_axis=0, tiled=True)  60.5 us
    all_to_all x1, waiting for transfers between devices, body(): lax.all_to_all(grid_tokens[:, :, :half], axes, split_axis=0, concat_axis=...  19.6 us
    dot_general x1, matrix products, expert_from_cot(): lax.dot_general(scaled_cot, down_matrix, last_t, preferred_element_type=j...  10.5 us
    dot_general x1, matrix products, expert_from_cot(): lax.dot_general(grad_up_pre, up_matrix, last_t, preferred_element_type=jn...  9.15 us
    convert_element_type x2, other arithmetic, expert_local(): (gate_value * sigmoid_gate * up_pre.astype(jnp.float32)).astype(jnp.bfloa...  9.1 us
    dot_general x1, matrix products, expert_from_cot(): lax.dot_general(hidden, scaled_cot, grid_rows, preferred_element_type=jnp...  8.77 us
  transfers between devices with their start and end apart: 5, of which 5 were waited for; matrix products, arithmetic and copies ran while one was open for 25% of the time, Pallas kernels for 0%

profile of v11, /device:TPU:0, one launch (start us, length us, event | category | flops | bytes accessed | tf_op | source)
XLA Modules:
  0.0 429.9 jit_solution(937565131480380106)
XLA Ops:
  6.7 6.7 %fusion.29 = bf16[1152,128]{1,0:T(8,128)(2,1)} fusion(s32[128,8]{0,1:T(8,128)S(1)} %multiply_add_fusion.1), kind=kLoop, calls=%fused_computation.46 | loop fusion | flops 3391488 | bytes 299008 | tf_op jit(solution)/shard_map/reduce_sum | solution.py:29
  20.3 7.6 %all-to-all-start = ((bf16[32,37,2048]{2,1,0:T(8,128)(2,1)}), bf16[32,37,2048]{2,1,0:T(8,128)(2,1)}, u32[]{:S(2)}, u32[]{:S(2)}) async-start(bf16[32,37,2048]{2,1,0:T(8,128)(2,1)} %pad_maximum_fusion), calls=%async_computation | async-start | bytes 10485760 | tf_op jit(solution)/shard_map/all_to_all | solution.py:202
  28.0 3.9 reshape.202
  35.7 4.3 multiply_convert_fusion.3
  43.6 5.0 %convolution_convert_fusion = bf16[32,36,2048]{2,1,0:T(8,128)(2,1)} fusion(bf16[32,36,128]{2,1,0:T(8,128)(2,1)S(1)} %reshape.199, bf16[128,2048]{1,0:T(8,128)(2,1)} %param.9), kind=kOutput, calls=%fused_computation.21 | convolution fusion | flops 606339072 | bytes 5537792 | tf_op jit(solution)/shard_map/dot_general | solution.py:209
  48.7 4.8 %multiply_convert_fusion.2 = bf16[32,36,768]{2,1,0:T(8,128)(2,1)} fusion(f32[32,36,768]{2,1,0:T(8,128)} %reshape.203, f32[32,36,768]{2,1,0:T(8,128)S(1)} %copy-done.2), kind=kLoop, calls=%fused_computation.26 | loop fusion | flops 5308416 | bytes 8847360 | tf_op jit(solution)/shard_map/convert_element_type | solution.py:136
  53.5 6.1 %convolution_convert_fusion.1 = bf16[32,36,2048]{2,1,0:T(8,128)(2,1)} fusion(bf16[32,36,768]{2,1,0:T(8,128)(2,1)S(1)} %copy-done.5, bf16[1,768,2048]{2,1,0:T(8,128)(2,1)S(1)} %copy-done), kind=kOutput, calls=%fused_computation.22 | convolution fusion | flops 3626237952 | bytes 9633792 | tf_op jit(solution)/shard_map/dot_general | solution.py:137
  59.5 85.9 %all-to-all-done = bf16[32,37,2048]{2,1,0:T(8,128)(2,1)} async-done(((bf16[32,37,2048]{2,1,0:T(8,128)(2,1)}), bf16[32,37,2048]{2,1,0:T(8,128)(2,1)}, u32[]{:S(2)}, u32[]{:S(2)}) %all-to-all-start) | async-done | bytes 4849696 | tf_op jit(solution)/shard_map/all_to_all | solution.py:202
  145.5 4.8 %fusion.63 = (bf16[32,36,1024]{2,1,0:T(8,128)(2,1)}, bf16[32,36,1024]{2,1,0:T(8,128)(2,1)S(1)}) fusion(bf16[32,36,2048]{2,1,0:T(8,128)(2,1)} %convolution_convert_fusion), kind=kLoop, calls=%fused_computation.93 | loop fusion | bytes 9437184 | tf_op jit(solution)/shard_map/slice | solution.py:215
  150.3 4.0 fusion.1
  160.8 60.5 %all-to-all-done.1 = bf16[32,37,1024]{2,1,0:T(8,128)(2,1)} async-done(((bf16[32,37,1024]{2,1,0:T(8,128)(2,1)}), bf16[32,37,1024]{2,1,0:T(8,128)(2,1)}, u32[]{:S(2)}, u32[]{:S(2)}) %all-to-all-start.1) | async-done | bytes 2424864 | tf_op jit(solution)/shard_map/all_to_all | solution.py:233
  225.1 10.5 %multiply_convert_fusion = (bf16[32,36,768]{2,1,0:T(8,128)(2,1)S(1)}, bf16[32,36,768]{2,1,0:T(8,128)(2,1)S(1)}) fusion(f32[32,36,768]{2,1,0:T(8,128)} %reshape.202, f32[32,36,768]{2,1,0:T(8,128)} %reshape.203, bf16[1,768,2048]{2,1,0:T(8,128)(2,1)S(1)} %copy-done, bf16[32,36,2048]{2,1,0:T(8,128)(2,1)} %bitcast.92, f32[32,36]{1,0:T(8,128)S(1)} %bitcast.95), kind=kOutput, calls=%fused_computation.24 | convolution fusion | flops 3642458112 | bytes 18485760 | tf_op jit(solution)/shard_map/dot_general | solution.py:155
  235.6 7.0 %fusion.18 = f32[32,36,2048]{2,1,0:T(8,128)} fusion(bf16[32,36,768]{2,1,0:T(8,128)(2,1)S(1)} %get-tuple-element.36, bf16[1,2048,768]{2,1,0:T(8,128)(2,1)S(1)} %copy-done.9), kind=kOutput, calls=%fused_computation.37 | convolution fusion | flops 3623878656 | bytes 14352384 | tf_op jit(solution)/shard_map/dot_general | solution.py:163
  242.6 9.1 %add_convert_fusion = bf16[32,36,2048]{2,1,0:T(8,128)(2,1)} fusion(f32[32,36,2048]{2,1,0:T(8,128)} %fusion.18, bf16[32,36,768]{2,1,0:T(8,128)(2,1)S(1)} %get-tuple-element.35, bf16[1,2048,768]{2,1,0:T(8,128)(2,1)S(1)} %copy-done.10), kind=kOutput, calls=%fused_computation.4 | convolution fusion | flops 3628597248 | bytes 19070976 | tf_op jit(solution)/shard_map/dot_general | solution.py:164
  252.8 5.9 %fusion.7 = f32[1,128,8]{2,0,1:T(1,128)S(1)} fusion(bf16[1152,1,1]{0,1,2:T(2,128)(2,1)S(1)} %reshape.212, s32[1024]{0:T(1024)S(1)} %multiply_add_fusion), kind=kOutput, calls=%fused_computation.16 | convolution fusion | flops 3538944 | bytes 10496 | tf_op jit(solution)/shard_map/dot_general | solution.py:236
  260.3 6.4 %pad_maximum_fusion.1 = bf16[32,38,2048]{2,1,0:T(8,128)(2,1)} fusion(bf16[32,1,2048]{2,1,0:T(2,128)(2,1)S(1)} %copy.58, bf16[32,1,2048]{2,1,0:T(2,128)(2,1)S(1)} %copy.57, bf16[32,36,2048]{2,1,0:T(8,128)(2,1)} %add_convert_fusion), kind=kLoop, calls=%fused_computation.9 | loop fusion | flops 14942208 | bytes 9961472 | tf_op jit(solution)/shard_map/concatenate | solution.py:251
  266.8 19.6 %all-to-all-done.3 = bf16[32,36,1024]{2,1,0:T(8,128)(2,1)} async-done(((bf16[32,36,1024]{2,1,0:T(8,128)(2,1)}), bf16[32,36,1024]{2,1,0:T(8,128)(2,1)}, u32[]{:S(2)}, u32[]{:S(2)}) %all-to-all-start.3) | async-done | bytes 2359328 | tf_op jit(solution)/shard_map/all_to_all | solution.py:214
  290.2 8.8 %fusion.22 = bf16[1,768,2048]{2,1,0:T(8,128)(2,1)} fusion(bf16[32,36,768]{2,1,0:T(8,128)(2,1)S(1)} %copy-done.4, bf16[32,36,2048]{2,1,0:T(8,128)(2,1)} %bitcast.92, f32[32,36]{1,0:T(8,128)S(1)} %bitcast.96), kind=kOutput, calls=%fused_computation.41 | convolution fusion | flops 3632529408 | bytes 9638400 | tf_op jit(solution)/shard_map/dot_general | solution.py:166
  299.0 4.2 fusion.44
  303.2 4.1 fusion.40
  307.3 4.1 fusion.45
  311.3 4.1 fusion.41
  318.6 89.0 %all-to-all-done.2 = bf16[32,38,2048]{2,1,0:T(8,128)(2,1)} async-done(((bf16[32,38,2048]{2,1,0:T(8,128)(2,1)}), bf16[32,38,2048]{2,1,0:T(8,128)(2,1)}, u32[]{:S(2)}, u32[]{:S(2)}) %all-to-all-start.2) | async-done | bytes 4980768 | tf_op jit(solution)/shard_map/all_to_all | solution.py:252
  418.7 5.7 %all-to-all-done.4 = f32[32,1,2048]{2,1,0:T(1,128)} async-done(((f32[32,1,2048]{2,1,0:T(1,128)}), f32[32,1,2048]{2,1,0:T(1,128)}, u32[]{:S(2)}, u32[]{:S(2)}) %all-to-all-start.4) | async-done | bytes 262176 | tf_op jit(solution)/shard_map/all_to_all | solution.py:259
  (85 shorter events, 56.5 us)
Async XLA Ops:
  0.6 52.8 %copy-start = (bf16[1,768,2048]{2,1,0:T(8,128)(2,1)S(1)}, bf16[1,768,2048]{2,1,0:T(8,128)(2,1)}, u32[]{:S(2)}) copy-start(bf16[1,768,2048]{2,1,0:T(8,128)(2,1)} %param.17) | copy-start | bytes 9437188
  0.6 5.1 %copy-start.8 = (s32[128,8]{0,1:T(8,128)S(1)}, s32[128,8]{0,1:T(8,128)}, u32[]{:S(2)}) copy-start(s32[128,8]{0,1:T(8,128)} %param.11) | copy-start | bytes 12292
  14.4 2.6 copy-start.6
  20.3 125.1 %all-to-all-start = ((bf16[32,37,2048]{2,1,0:T(8,128)(2,1)}), bf16[32,37,2048]{2,1,0:T(8,128)(2,1)}, u32[]{:S(2)}, u32[]{:S(2)}) async-start(bf16[32,37,2048]{2,1,0:T(8,128)(2,1)} %pad_maximum_fusion), calls=%async_computation | async-start | bytes 10485760 | tf_op jit(solution)/shard_map/all_to_all | solution.py:202
  43.6 5.0 %copy-start.2 = (f32[32,36,768]{2,1,0:T(8,128)S(1)}, f32[32,36,768]{2,1,0:T(8,128)}, u32[]{:S(2)}) copy-start(f32[32,36,768]{2,1,0:T(8,128)} %reshape.202) | copy-start | bytes 10616836
  48.7 4.8 %copy-start.5 = (bf16[32,36,768]{2,1,0:T(8,128)(2,1)S(1)}, bf16[32,36,768]{2,1,0:T(8,128)(2,1)}, u32[]{:S(2)}) copy-start(bf16[32,36,768]{2,1,0:T(8,128)(2,1)} %convert_element_type.170) | copy-start | bytes 5308420
  145.5 4.8 %slice-start = ((s8[5242880]{0:T(1024)(128)(4,1)}), s8[4194304]{0:T(1024)(128)(4,1)S(1)}, s32[]{:S(2)}) async-start(s8[5242880]{0:T(1024)(128)(4,1)} %bitcast.93), calls=%async_computation.5 | async-start | bytes 8388608
  145.5 4.8 %slice-start.1 = ((s8[5242880]{0:T(1024)(128)(4,1)}), s8[1048576]{0:T(1024)(128)(4,1)S(1)}, s32[]{:S(2)}) async-start(s8[5242880]{0:T(1024)(128)(4,1)} %bitcast.93), calls=%async_computation.6 | async-start | bytes 2097152
  156.4 64.9 %all-to-all-start.1 = ((bf16[32,37,1024]{2,1,0:T(8,128)(2,1)}), bf16[32,37,1024]{2,1,0:T(8,128)(2,1)}, u32[]{:S(2)}, u32[]{:S(2)}) async-start(bf16[32,37,1024]{2,1,0:T(8,128)(2,1)} %pad_maximum_fusion.4), calls=%async_computation.1 | async-start | bytes 5242880 | tf_op jit(solution)/shard_map/all_to_all | solution.py:233
  221.3 65.1 %all-to-all-start.3 = ((bf16[32,36,1024]{2,1,0:T(8,128)(2,1)}), bf16[32,36,1024]{2,1,0:T(8,128)(2,1)}, u32[]{:S(2)}, u32[]{:S(2)}) async-start(bf16[32,36,1024]{2,1,0:T(8,128)(2,1)} %get-tuple-element.37), calls=%async_computation.3 | async-start | bytes 5242880 | tf_op jit(solution)/shard_map/all_to_all | solution.py:214
  225.1 10.5 %copy-start.9 = (bf16[1,2048,768]{2,1,0:T(8,128)(2,1)S(1)}, bf16[1,2048,768]{2,1,0:T(8,128)(2,1)}, u32[]{:S(2)}) copy-start(bf16[1,2048,768]{2,1,0:T(8,128)(2,1)} %param.15) | copy-start | bytes 9437188
  235.5 7.0 %copy-start.13 = (bf16[32,36,768]{2,1,0:T(8,128)(2,1)}, bf16[32,36,768]{2,1,0:T(8,128)(2,1)S(1)}, u32[]{:S(2)}) copy-start(bf16[32,36,768]{2,1,0:T(8,128)(2,1)S(1)} %get-tuple-element.36) | copy-start | bytes 5308420
  235.6 7.0 %copy-start.11 = (bf16[32,36,768]{2,1,0:T(8,128)(2,1)}, bf16[32,36,768]{2,1,0:T(8,128)(2,1)S(1)}, u32[]{:S(2)}) copy-start(bf16[32,36,768]{2,1,0:T(8,128)(2,1)S(1)} %get-tuple-element.35) | copy-start | bytes 5308420
  235.6 7.0 %copy-start.10 = (bf16[1,2048,768]{2,1,0:T(8,128)(2,1)S(1)}, bf16[1,2048,768]{2,1,0:T(8,128)(2,1)}, u32[]{:S(2)}) copy-start(bf16[1,2048,768]{2,1,0:T(8,128)(2,1)} %param.16) | copy-start | bytes 9437188
  242.6 16.3 %copy-start.3 = (bf16[128,2048]{1,0:T(8,128)(2,1)S(1)}, bf16[128,2048]{1,0:T(8,128)(2,1)}, u32[]{:S(2)}) copy-start(bf16[128,2048]{1,0:T(8,128)(2,1)} %param.9) | copy-start | bytes 1572868
  266.8 23.4 %copy-start.4 = (bf16[32,36,768]{2,1,0:T(8,128)(2,1)S(1)}, bf16[32,36,768]{2,1,0:T(8,128)(2,1)}, u32[]{:S(2)}) copy-start(bf16[32,36,768]{2,1,0:T(8,128)(2,1)} %multiply_convert_fusion.2) | copy-start | bytes 5308420
  286.4 121.3 %all-to-all-start.2 = ((bf16[32,38,2048]{2,1,0:T(8,128)(2,1)}), bf16[32,38,2048]{2,1,0:T(8,128)(2,1)}, u32[]{:S(2)}, u32[]{:S(2)}) async-start(bf16[32,38,2048]{2,1,0:T(8,128)(2,1)} %pad_maximum_fusion.1), calls=%async_computation.2 | async-start | bytes 10485760 | tf_op jit(solution)/shard_map/all_to_all | solution.py:252
  290.2 8.8 %copy-start.12 = (bf16[32,36,768]{2,1,0:T(8,128)(2,1)S(1)}, bf16[32,36,768]{2,1,0:T(8,128)(2,1)}, u32[]{:S(2)}) copy-start(bf16[32,36,768]{2,1,0:T(8,128)(2,1)} %copy-done.11) | copy-start | bytes 5308420
  299.0 4.2 copy-start.14
  410.7 13.7 %all-to-all-start.4 = ((f32[32,1,2048]{2,1,0:T(1,128)}), f32[32,1,2048]{2,1,0:T(1,128)}, u32[]{:S(2)}, u32[]{:S(2)}) async-start(f32[32,1,2048]{2,1,0:T(1,128)} %broadcast_in_dim.36), calls=%async_computation.4 | async-start | bytes 524288 | tf_op jit(solution)/shard_map/all_to_all | solution.py:259
  414.0 3.5 copy-start.7
  414.0 15.6 %copy-start.1 = (bf16[1,768,2048]{2,1,0:T(8,128)(2,1)S(1)}, bf16[1,768,2048]{2,1,0:T(8,128)(2,1)}, u32[]{:S(2)}) copy-start(bf16[1,768,2048]{2,1,0:T(8,128)(2,1)} %param.17) | copy-start | bytes 9437188

commit v12 on v11

--- a/solution.py
+++ b/solution.py
@@ -26,9 +26,17 @@
     slot_table = (
         jnp.arange(experts * capacity, dtype=jnp.int32)[:, None] == target[None, :]
     ).astype(jnp.bfloat16)
-    token_table = jnp.sum(
-        slot_table.reshape(experts * capacity, routes.shape[0], routes.shape[1]), axis=2
-    )
+    pair_token = jnp.arange(pairs, dtype=jnp.int32) // routes.shape[1]
+    token_code = jnp.stack(
+        [pair_token // 16, pair_token % 16, jnp.ones_like(pair_token)], axis=1
+    ).astype(jnp.bfloat16)
+    slot_code = jnp.dot(slot_table, token_code, preferred_element_type=jnp.float32)
+    slot_token = (slot_code[:, 0] * 16.0 + slot_code[:, 1]).astype(jnp.int32)
+    filled = slot_code[:, 2] > 0.5
+    token_table = (
+        (slot_token[:, None] == jnp.arange(routes.shape[0], dtype=jnp.int32)[None, :])
+        & filled[:, None]
+    ).astype(jnp.bfloat16)
     return (slot_table, token_table)
 
 

time: 437 us -> 427 us (0.977)
  other arithmetic: 40.4 us -> 33.6 us
    reduce_sum x1 -> x0, other arithmetic: 6.73 us -> none  [route_tables(): jnp.sum(slot_table.reshape(experts * capacity, routes.shape[0], routes.sh...]
where the time goes in v12:
time: 427 us; the launch traced here: 422 us
  waiting for transfers between devices  261 us (61%)
  matrix products  79.5 us (19%)
  other arithmetic  33.6 us (8%)
  local copies, waits for them, and re-layouts  25 us (6%)
  starting transfers between devices  22.1 us (5%)
    all_to_all x1, waiting for transfers between devices, body(): lax.all_to_all(send_back, axes, split_axis=0, concat_axis=0, tiled=True)  88.3 us
    all_to_all x1, waiting for transfers between devices, body(): lax.all_to_all(send_cot, axes, split_axis=0, concat_axis=0, tiled=True)  86.4 us
    all_to_all x1, waiting for transfers between devices, body(): lax.all_to_all(send_b, axes, split_axis=0, concat_axis=0, tiled=True)  60.5 us
    all_to_all x1, waiting for transfers between devices, body(): lax.all_to_all(grid_tokens[:, :, :half], axes, split_axis=0, concat_axis=...  20 us
    dot_general x1, matrix products, expert_from_cot(): lax.dot_general(scaled_cot, down_matrix, last_t, preferred_element_type=j...  10.4 us
    convert_element_type x2, other arithmetic, expert_local(): (gate_value * sigmoid_gate * up_pre.astype(jnp.float32)).astype(jnp.bfloa...  9.11 us
    dot_general x1, matrix products, expert_from_cot(): lax.dot_general(hidden, scaled_cot, grid_rows, preferred_element_type=jnp...  8.99 us
    dot_general x1, matrix products, expert_from_cot(): lax.dot_general(grad_up_pre, up_matrix, last_t, preferred_element_type=jn...  8.86 us
  transfers between devices with their start and end apart: 5, of which 5 were waited for; matrix products, arithmetic and copies ran while one was open for 25% of the time, Pallas kernels for 0%

profile of v12, /device:TPU:0, one launch (start us, length us, event | category | flops | bytes accessed | tf_op | source)
XLA Modules:
  0.0 422.3 jit_solution(2869565643890102443)
XLA Ops:
  12.6 7.9 %all-to-all-start = ((bf16[32,37,2048]{2,1,0:T(8,128)(2,1)}), bf16[32,37,2048]{2,1,0:T(8,128)(2,1)}, u32[]{:S(2)}, u32[]{:S(2)}) async-start(bf16[32,37,2048]{2,1,0:T(8,128)(2,1)} %pad_maximum_fusion), calls=%async_computation | async-start | bytes 10485760 | tf_op jit(solution)/shard_map/all_to_all | solution.py:210
  20.5 3.9 reshape.304
  24.4 3.8 reshape.305
  28.3 4.3 %multiply_convert_fusion.3 = bf16[1,1152,768]{2,1,0:T(8,128)(2,1)} fusion(bf16[1,1152,768]{2,1,0:T(8,128)(2,1)} %param.14, bf16[1,1152,768]{2,1,0:T(8,128)(2,1)} %param.13), kind=kLoop, calls=%fused_computation.28 | loop fusion | flops 7077888 | bytes 5308416 | tf_op jit(solution)/shard_map/convert_element_type | solution.py:144
  36.2 4.5 %convolution_convert_fusion = bf16[32,36,2048]{2,1,0:T(8,128)(2,1)} fusion(bf16[128,2048]{1,0:T(8,128)(2,1)} %param.9, s32[32,36]{1,0:T(8,128)S(1)} %eq.78, pred[32,36]{1,0:T(8,128)(4,1)S(1)} %and.77), kind=kOutput, calls=%fused_computation.20 | convolution fusion | flops 606633984 | bytes 5248640 | tf_op jit(solution)/shard_map/dot_general | solution.py:217
  40.7 4.8 %multiply_convert_fusion.2 = bf16[32,36,768]{2,1,0:T(8,128)(2,1)} fusion(f32[32,36,768]{2,1,0:T(8,128)} %reshape.305, f32[32,36,768]{2,1,0:T(8,128)S(1)} %copy-done.2), kind=kLoop, calls=%fused_computation.25 | loop fusion | flops 5308416 | bytes 8847360 | tf_op jit(solution)/shard_map/convert_element_type | solution.py:144
  45.5 6.1 %convolution_convert_fusion.1 = bf16[32,36,2048]{2,1,0:T(8,128)(2,1)} fusion(bf16[32,36,768]{2,1,0:T(8,128)(2,1)S(1)} %copy-done.5, bf16[1,768,2048]{2,1,0:T(8,128)(2,1)S(1)} %copy-done), kind=kOutput, calls=%fused_computation.21 | convolution fusion | flops 3626237952 | bytes 9633792 | tf_op jit(solution)/shard_map/dot_general | solution.py:145
  51.6 86.4 %all-to-all-done = bf16[32,37,2048]{2,1,0:T(8,128)(2,1)} async-done(((bf16[32,37,2048]{2,1,0:T(8,128)(2,1)}), bf16[32,37,2048]{2,1,0:T(8,128)(2,1)}, u32[]{:S(2)}, u32[]{:S(2)}) %all-to-all-start) | async-done | bytes 4849696 | tf_op jit(solution)/shard_map/all_to_all | solution.py:210
  138.0 4.8 %fusion.83 = (bf16[32,36,1024]{2,1,0:T(8,128)(2,1)}, bf16[32,36,1024]{2,1,0:T(8,128)(2,1)S(1)}) fusion(bf16[32,36,2048]{2,1,0:T(8,128)(2,1)} %convolution_convert_fusion), kind=kLoop, calls=%fused_computation.121 | loop fusion | bytes 9437184 | tf_op jit(solution)/shard_map/slice | solution.py:223
  142.8 4.0 fusion.1
  153.3 60.5 %all-to-all-done.1 = bf16[32,37,1024]{2,1,0:T(8,128)(2,1)} async-done(((bf16[32,37,1024]{2,1,0:T(8,128)(2,1)}), bf16[32,37,1024]{2,1,0:T(8,128)(2,1)}, u32[]{:S(2)}, u32[]{:S(2)}) %all-to-all-start.1) | async-done | bytes 2424864 | tf_op jit(solution)/shard_map/all_to_all | solution.py:241
  217.5 10.4 %multiply_convert_fusion = (bf16[32,36,768]{2,1,0:T(8,128)(2,1)S(1)}, bf16[32,36,768]{2,1,0:T(8,128)(2,1)S(1)}) fusion(f32[32,36,768]{2,1,0:T(8,128)} %reshape.304, f32[32,36,768]{2,1,0:T(8,128)} %reshape.305, bf16[1,768,2048]{2,1,0:T(8,128)(2,1)S(1)} %copy-done, bf16[32,36,2048]{2,1,0:T(8,128)(2,1)} %bitcast.90, f32[32,36]{1,0:T(8,128)S(1)} %bitcast.93), kind=kOutput, calls=%fused_computation.23 | convolution fusion | flops 3642458112 | bytes 18485760 | tf_op jit(solution)/shard_map/dot_general | solution.py:163
  228.0 7.0 %fusion.18 = f32[32,36,2048]{2,1,0:T(8,128)} fusion(bf16[32,36,768]{2,1,0:T(8,128)(2,1)S(1)} %get-tuple-element.36, bf16[1,2048,768]{2,1,0:T(8,128)(2,1)S(1)} %copy-done.8), kind=kOutput, calls=%fused_computation.36 | convolution fusion | flops 3623878656 | bytes 14352384 | tf_op jit(solution)/shard_map/dot_general | solution.py:171
  235.0 8.9 %add_convert_fusion = bf16[32,36,2048]{2,1,0:T(8,128)(2,1)} fusion(f32[32,36,2048]{2,1,0:T(8,128)} %fusion.18, bf16[32,36,768]{2,1,0:T(8,128)(2,1)S(1)} %get-tuple-element.35, bf16[1,2048,768]{2,1,0:T(8,128)(2,1)S(1)} %copy-done.9), kind=kOutput, calls=%fused_computation.4 | convolution fusion | flops 3628597248 | bytes 19070976 | tf_op jit(solution)/shard_map/dot_general | solution.py:172
  244.9 5.9 %fusion.7 = f32[1,128,8]{2,0,1:T(1,128)S(1)} fusion(bf16[1152,1,1]{0,1,2:T(2,128)(2,1)S(1)} %reshape.314, s32[1024]{0:T(1024)S(1)} %multiply_add_fusion), kind=kOutput, calls=%fused_computation.15 | convolution fusion | flops 3538944 | bytes 10496 | tf_op jit(solution)/shard_map/dot_general | solution.py:244
  252.5 6.4 %pad_maximum_fusion.1 = bf16[32,38,2048]{2,1,0:T(8,128)(2,1)} fusion(bf16[32,1,2048]{2,1,0:T(2,128)(2,1)S(1)} %copy.49, bf16[32,1,2048]{2,1,0:T(2,128)(2,1)S(1)} %copy.48, bf16[32,36,2048]{2,1,0:T(8,128)(2,1)} %add_convert_fusion), kind=kLoop, calls=%fused_computation.9 | loop fusion | flops 14942208 | bytes 9961472 | tf_op jit(solution)/shard_map/concatenate | solution.py:259
  258.9 20.0 %all-to-all-done.3 = bf16[32,36,1024]{2,1,0:T(8,128)(2,1)} async-done(((bf16[32,36,1024]{2,1,0:T(8,128)(2,1)}), bf16[32,36,1024]{2,1,0:T(8,128)(2,1)}, u32[]{:S(2)}, u32[]{:S(2)}) %all-to-all-start.3) | async-done | bytes 2359328 | tf_op jit(solution)/shard_map/all_to_all | solution.py:222
  282.5 9.0 %fusion.22 = bf16[1,768,2048]{2,1,0:T(8,128)(2,1)} fusion(bf16[32,36,768]{2,1,0:T(8,128)(2,1)S(1)} %copy-done.4, bf16[32,36,2048]{2,1,0:T(8,128)(2,1)} %bitcast.90, f32[32,36]{1,0:T(8,128)S(1)} %bitcast.94), kind=kOutput, calls=%fused_computation.40 | convolution fusion | flops 3632529408 | bytes 9638400 | tf_op jit(solution)/shard_map/dot_general | solution.py:174
  291.5 4.2 fusion.44
  295.8 4.1 fusion.40
  299.8 4.1 fusion.45
  305.8 4.1 fusion.41
  311.7 88.3 %all-to-all-done.2 = bf16[32,38,2048]{2,1,0:T(8,128)(2,1)} async-done(((bf16[32,38,2048]{2,1,0:T(8,128)(2,1)}), bf16[32,38,2048]{2,1,0:T(8,128)(2,1)}, u32[]{:S(2)}, u32[]{:S(2)}) %all-to-all-start.2) | async-done | bytes 4980768 | tf_op jit(solution)/shard_map/all_to_all | solution.py:260
  411.1 5.7 %all-to-all-done.4 = f32[32,1,2048]{2,1,0:T(1,128)} async-done(((f32[32,1,2048]{2,1,0:T(1,128)}), f32[32,1,2048]{2,1,0:T(1,128)}, u32[]{:S(2)}, u32[]{:S(2)}) %all-to-all-start.4) | async-done | bytes 262176 | tf_op jit(solution)/shard_map/all_to_all | solution.py:267
  (86 shorter events, 51.9 us)
Async XLA Ops:
  0.6 44.9 %copy-start = (bf16[1,768,2048]{2,1,0:T(8,128)(2,1)S(1)}, bf16[1,768,2048]{2,1,0:T(8,128)(2,1)}, u32[]{:S(2)}) copy-start(bf16[1,768,2048]{2,1,0:T(8,128)(2,1)} %param.17) | copy-start | bytes 9437188
  0.6 4.2 copy-start.7
  12.6 125.4 %all-to-all-start = ((bf16[32,37,2048]{2,1,0:T(8,128)(2,1)}), bf16[32,37,2048]{2,1,0:T(8,128)(2,1)}, u32[]{:S(2)}, u32[]{:S(2)}) async-start(bf16[32,37,2048]{2,1,0:T(8,128)(2,1)} %pad_maximum_fusion), calls=%async_computation | async-start | bytes 10485760 | tf_op jit(solution)/shard_map/all_to_all | solution.py:210
  36.2 4.5 %copy-start.2 = (f32[32,36,768]{2,1,0:T(8,128)S(1)}, f32[32,36,768]{2,1,0:T(8,128)}, u32[]{:S(2)}) copy-start(f32[32,36,768]{2,1,0:T(8,128)} %reshape.304) | copy-start | bytes 10616836
  40.7 4.8 %copy-start.5 = (bf16[32,36,768]{2,1,0:T(8,128)(2,1)S(1)}, bf16[32,36,768]{2,1,0:T(8,128)(2,1)}, u32[]{:S(2)}) copy-start(bf16[32,36,768]{2,1,0:T(8,128)(2,1)} %convert_element_type.171) | copy-start | bytes 5308420
  138.0 4.8 %slice-start = ((s8[5242880]{0:T(1024)(128)(4,1)}), s8[4194304]{0:T(1024)(128)(4,1)S(1)}, s32[]{:S(2)}) async-start(s8[5242880]{0:T(1024)(128)(4,1)} %bitcast.91), calls=%async_computation.5 | async-start | bytes 8388608
  138.0 4.8 %slice-start.1 = ((s8[5242880]{0:T(1024)(128)(4,1)}), s8[1048576]{0:T(1024)(128)(4,1)S(1)}, s32[]{:S(2)}) async-start(s8[5242880]{0:T(1024)(128)(4,1)} %bitcast.91), calls=%async_computation.6 | async-start | bytes 2097152
  148.9 64.9 %all-to-all-start.1 = ((bf16[32,37,1024]{2,1,0:T(8,128)(2,1)}), bf16[32,37,1024]{2,1,0:T(8,128)(2,1)}, u32[]{:S(2)}, u32[]{:S(2)}) async-start(bf16[32,37,1024]{2,1,0:T(8,128)(2,1)} %pad_maximum_fusion.4), calls=%async_computation.1 | async-start | bytes 5242880 | tf_op jit(solution)/shard_map/all_to_all | solution.py:241
  213.8 65.1 %all-to-all-start.3 = ((bf16[32,36,1024]{2,1,0:T(8,128)(2,1)}), bf16[32,36,1024]{2,1,0:T(8,128)(2,1)}, u32[]{:S(2)}, u32[]{:S(2)}) async-start(bf16[32,36,1024]{2,1,0:T(8,128)(2,1)} %get-tuple-element.37), calls=%async_computation.3 | async-start | bytes 5242880 | tf_op jit(solution)/shard_map/all_to_all | solution.py:222
  217.5 10.5 %copy-start.8 = (bf16[1,2048,768]{2,1,0:T(8,128)(2,1)S(1)}, bf16[1,2048,768]{2,1,0:T(8,128)(2,1)}, u32[]{:S(2)}) copy-start(bf16[1,2048,768]{2,1,0:T(8,128)(2,1)} %param.15) | copy-start | bytes 9437188
  228.0 7.0 %copy-start.12 = (bf16[32,36,768]{2,1,0:T(8,128)(2,1)}, bf16[32,36,768]{2,1,0:T(8,128)(2,1)S(1)}, u32[]{:S(2)}) copy-start(bf16[32,36,768]{2,1,0:T(8,128)(2,1)S(1)} %get-tuple-element.36) | copy-start | bytes 5308420
  228.0 7.0 %copy-start.10 = (bf16[32,36,768]{2,1,0:T(8,128)(2,1)}, bf16[32,36,768]{2,1,0:T(8,128)(2,1)S(1)}, u32[]{:S(2)}) copy-start(bf16[32,36,768]{2,1,0:T(8,128)(2,1)S(1)} %get-tuple-element.35) | copy-start | bytes 5308420
  228.0 7.0 %copy-start.9 = (bf16[1,2048,768]{2,1,0:T(8,128)(2,1)S(1)}, bf16[1,2048,768]{2,1,0:T(8,128)(2,1)}, u32[]{:S(2)}) copy-start(bf16[1,2048,768]{2,1,0:T(8,128)(2,1)} %param.16) | copy-start | bytes 9437188
  235.0 16.0 %copy-start.3 = (bf16[128,2048]{1,0:T(8,128)(2,1)S(1)}, bf16[128,2048]{1,0:T(8,128)(2,1)}, u32[]{:S(2)}) copy-start(bf16[128,2048]{1,0:T(8,128)(2,1)} %param.9) | copy-start | bytes 1572868
  258.9 23.6 %copy-start.4 = (bf16[32,36,768]{2,1,0:T(8,128)(2,1)S(1)}, bf16[32,36,768]{2,1,0:T(8,128)(2,1)}, u32[]{:S(2)}) copy-start(bf16[32,36,768]{2,1,0:T(8,128)(2,1)} %multiply_convert_fusion.2) | copy-start | bytes 5308420
  278.9 121.1 %all-to-all-start.2 = ((bf16[32,38,2048]{2,1,0:T(8,128)(2,1)}), bf16[32,38,2048]{2,1,0:T(8,128)(2,1)}, u32[]{:S(2)}, u32[]{:S(2)}) async-start(bf16[32,38,2048]{2,1,0:T(8,128)(2,1)} %pad_maximum_fusion.1), calls=%async_computation.2 | async-start | bytes 10485760 | tf_op jit(solution)/shard_map/all_to_all | solution.py:260
  282.5 9.0 %copy-start.11 = (bf16[32,36,768]{2,1,0:T(8,128)(2,1)S(1)}, bf16[32,36,768]{2,1,0:T(8,128)(2,1)}, u32[]{:S(2)}) copy-start(bf16[32,36,768]{2,1,0:T(8,128)(2,1)} %copy-done.10) | copy-start | bytes 5308420
  291.5 4.2 %copy-start.13 = (bf16[32,36,768]{2,1,0:T(8,128)(2,1)S(1)}, bf16[32,36,768]{2,1,0:T(8,128)(2,1)}, u32[]{:S(2)}) copy-start(bf16[32,36,768]{2,1,0:T(8,128)(2,1)} %copy-done.12) | copy-start | bytes 5308420
  403.1 13.7 %all-to-all-start.4 = ((f32[32,1,2048]{2,1,0:T(1,128)}), f32[32,1,2048]{2,1,0:T(1,128)}, u32[]{:S(2)}, u32[]{:S(2)}) async-start(f32[32,1,2048]{2,1,0:T(1,128)} %broadcast_in_dim.36), calls=%async_computation.4 | async-start | bytes 524288 | tf_op jit(solution)/shard_map/all_to_all | solution.py:267
  406.4 3.5 copy-start.6
  406.5 15.6 %copy-start.1 = (bf16[1,768,2048]{2,1,0:T(8,128)(2,1)S(1)}, bf16[1,768,2048]{2,1,0:T(8,128)(2,1)}, u32[]{:S(2)}) copy-start(bf16[1,768,2048]{2,1,0:T(8,128)(2,1)} %param.17) | copy-start | bytes 9437188

commit v13 on v12

--- a/solution.py
+++ b/solution.py
@@ -202,11 +202,19 @@
     send_weight = jnp.dot(slot_table, probs_low, preferred_element_type=jnp.float32).astype(
         jnp.bfloat16
     )
-    weight_row = jnp.pad(send_weight.reshape(experts, capacity), ((0, 0), (0, width - capacity)))
-    grid_cot = jnp.dot(grid_table, cotangent, preferred_element_type=jnp.float32).astype(
-        jnp.bfloat16
-    )
-    send_cot = jnp.concatenate([grid_cot, weight_row[:, None, :]], axis=1)
+    weight_rows = jnp.pad(send_weight.reshape(experts, capacity), ((0, 0), (0, width - capacity)))
+    cot_ext = jnp.concatenate([cotangent, weight_rows], axis=0)
+    pick_weight = (
+        jnp.arange(experts, dtype=jnp.int32)[:, None] == jnp.arange(experts, dtype=jnp.int32)[None, :]
+    ).astype(jnp.bfloat16)
+    table_ext = jnp.concatenate(
+        [
+            jnp.pad(grid_table, ((0, 0), (0, 0), (0, experts))),
+            jnp.pad(pick_weight, ((0, 0), (grid_table.shape[2], 0)))[:, None, :],
+        ],
+        axis=1,
+    )
+    send_cot = jnp.dot(table_ext, cot_ext, preferred_element_type=jnp.float32).astype(jnp.bfloat16)
     got_cot_w = lax.all_to_all(send_cot, axes, split_axis=0, concat_axis=0, tiled=True)
     gate_grid = gate_saved[0].reshape(experts, capacity, -1)
     up_grid = up_saved[0].reshape(experts, capacity, -1)

time: 427 us -> 426 us (level)
  no operation moved by 1% of the time
where the time goes in v13:
time: 426 us; the launch traced here: 421 us
  waiting for transfers between devices  261 us (61%)
  matrix products  81.5 us (19%)
  other arithmetic  30.9 us (7%)
  local copies, waits for them, and re-layouts  24.8 us (6%)
  starting transfers between devices  22.1 us (5%)
    all_to_all x1, waiting for transfers between devices, body(): lax.all_to_all(send_back, axes, split_axis=0, concat_axis=0, tiled=True)  88.3 us
    all_to_all x1, waiting for transfers between devices, body(): lax.all_to_all(send_cot, axes, split_axis=0, concat_axis=0, tiled=True)  86.4 us
    all_to_all x1, waiting for transfers between devices, body(): lax.all_to_all(send_b, axes, split_axis=0, concat_axis=0, tiled=True)  60.5 us
    all_to_all x1, waiting for transfers between devices, body(): lax.all_to_all(grid_tokens[:, :, :half], axes, split_axis=0, concat_axis=...  19.9 us
    dot_general x1, matrix products, expert_from_cot(): lax.dot_general(scaled_cot, down_matrix, last_t, preferred_element_type=j...  10.5 us
    convert_element_type x2, other arithmetic, expert_local(): (gate_value * sigmoid_gate * up_pre.astype(jnp.float32)).astype(jnp.bfloa...  9.11 us
    dot_general x1, matrix products, expert_from_cot(): lax.dot_general(hidden, scaled_cot, grid_rows, preferred_element_type=jnp...  8.98 us
    dot_general x1, matrix products, expert_from_cot(): lax.dot_general(grad_up_pre, up_matrix, last_t, preferred_element_type=jn...  8.86 us
  transfers between devices with their start and end apart: 5, of which 5 were waited for; matrix products, arithmetic and copies ran while one was open for 25% of the time, Pallas kernels for 0%

profile of v13, /device:TPU:0, one launch (start us, length us, event | category | flops | bytes accessed | tf_op | source)
XLA Modules:
  0.0 421.4 jit_solution(15360649206301942256)
XLA Ops:
  6.8 4.9 %convolution_convert_fusion.2 = bf16[32,37,2048]{2,1,0:T(8,128)(2,1)} fusion(pred[32,36,128]{2,1,0:T(8,128)(4,1)S(1)} %fusion.60, pred[32,1,160]{2,1,0:T(4,128)(4,1)S(1)} %copy.44, bf16[32,36]{1,0:T(8,128)(2,1)S(1)} %reshape.315, bf16[128,2048]{1,0:T(8,128)(2,1)} %param.10), kind=kOutput, calls=%fused_computation.21 | convolution fusion | flops 780526592 | bytes 5528832 | tf_op jit(solution)/shard_map/dot_general | solution.py:217
  11.6 7.9 %all-to-all-start = ((bf16[32,37,2048]{2,1,0:T(8,128)(2,1)}), bf16[32,37,2048]{2,1,0:T(8,128)(2,1)}, u32[]{:S(2)}, u32[]{:S(2)}) async-start(bf16[32,37,2048]{2,1,0:T(8,128)(2,1)} %convolution_convert_fusion.2), calls=%async_computation | async-start | bytes 10485760 | tf_op jit(solution)/shard_map/all_to_all | solution.py:218
  19.6 3.9 reshape.317
  27.3 4.3 %multiply_convert_fusion.3 = bf16[1,1152,768]{2,1,0:T(8,128)(2,1)} fusion(bf16[1,1152,768]{2,1,0:T(8,128)(2,1)} %param.14, bf16[1,1152,768]{2,1,0:T(8,128)(2,1)} %param.13), kind=kLoop, calls=%fused_computation.27 | loop fusion | flops 7077888 | bytes 5308416 | tf_op jit(solution)/shard_map/convert_element_type | solution.py:144
  35.2 4.5 %convolution_convert_fusion = bf16[32,36,2048]{2,1,0:T(8,128)(2,1)} fusion(bf16[128,2048]{1,0:T(8,128)(2,1)} %param.9, s32[32,36]{1,0:T(8,128)S(1)} %eq.92, pred[32,36]{1,0:T(8,128)(4,1)S(1)} %and.78), kind=kOutput, calls=%fused_computation.19 | convolution fusion | flops 606633984 | bytes 5248640 | tf_op jit(solution)/shard_map/dot_general | solution.py:225
  39.8 4.8 %multiply_convert_fusion.2 = bf16[32,36,768]{2,1,0:T(8,128)(2,1)} fusion(f32[32,36,768]{2,1,0:T(8,128)} %reshape.318, f32[32,36,768]{2,1,0:T(8,128)S(1)} %copy-done.2), kind=kLoop, calls=%fused_computation.24 | loop fusion | flops 5308416 | bytes 8847360 | tf_op jit(solution)/shard_map/convert_element_type | solution.py:144
  44.6 6.1 %convolution_convert_fusion.1 = bf16[32,36,2048]{2,1,0:T(8,128)(2,1)} fusion(bf16[32,36,768]{2,1,0:T(8,128)(2,1)S(1)} %copy-done.5, bf16[1,768,2048]{2,1,0:T(8,128)(2,1)S(1)} %copy-done), kind=kOutput, calls=%fused_computation.20 | convolution fusion | flops 3626237952 | bytes 9633792 | tf_op jit(solution)/shard_map/dot_general | solution.py:145
  50.6 86.4 %all-to-all-done = bf16[32,37,2048]{2,1,0:T(8,128)(2,1)} async-done(((bf16[32,37,2048]{2,1,0:T(8,128)(2,1)}), bf16[32,37,2048]{2,1,0:T(8,128)(2,1)}, u32[]{:S(2)}, u32[]{:S(2)}) %all-to-all-start) | async-done | bytes 4849696 | tf_op jit(solution)/shard_map/all_to_all | solution.py:218
  137.1 4.8 %fusion.88 = (bf16[32,36,1024]{2,1,0:T(8,128)(2,1)}, bf16[32,36,1024]{2,1,0:T(8,128)(2,1)S(1)}) fusion(bf16[32,36,2048]{2,1,0:T(8,128)(2,1)} %convolution_convert_fusion), kind=kLoop, calls=%fused_computation.128 | loop fusion | bytes 9437184 | tf_op jit(solution)/shard_map/slice | solution.py:231
  141.9 4.0 fusion.1
  152.4 60.5 %all-to-all-done.1 = bf16[32,37,1024]{2,1,0:T(8,128)(2,1)} async-done(((bf16[32,37,1024]{2,1,0:T(8,128)(2,1)}), bf16[32,37,1024]{2,1,0:T(8,128)(2,1)}, u32[]{:S(2)}, u32[]{:S(2)}) %all-to-all-start.1) | async-done | bytes 2424864 | tf_op jit(solution)/shard_map/all_to_all | solution.py:249
  216.6 10.5 %multiply_convert_fusion = (bf16[32,36,768]{2,1,0:T(8,128)(2,1)S(1)}, bf16[32,36,768]{2,1,0:T(8,128)(2,1)S(1)}) fusion(f32[32,36,768]{2,1,0:T(8,128)} %reshape.317, f32[32,36,768]{2,1,0:T(8,128)} %reshape.318, bf16[1,768,2048]{2,1,0:T(8,128)(2,1)S(1)} %copy-done, bf16[32,36,2048]{2,1,0:T(8,128)(2,1)} %bitcast.90, f32[32,36]{1,0:T(8,128)S(1)} %bitcast.93), kind=kOutput, calls=%fused_computation.22 | convolution fusion | flops 3642458112 | bytes 18485760 | tf_op jit(solution)/shard_map/dot_general | solution.py:163
  227.1 7.0 %fusion.18 = f32[32,36,2048]{2,1,0:T(8,128)} fusion(bf16[32,36,768]{2,1,0:T(8,128)(2,1)S(1)} %get-tuple-element.36, bf16[1,2048,768]{2,1,0:T(8,128)(2,1)S(1)} %copy-done.8), kind=kOutput, calls=%fused_computation.35 | convolution fusion | flops 3623878656 | bytes 14352384 | tf_op jit(solution)/shard_map/dot_general | solution.py:171
  234.1 8.9 %add_convert_fusion = bf16[32,36,2048]{2,1,0:T(8,128)(2,1)} fusion(f32[32,36,2048]{2,1,0:T(8,128)} %fusion.18, bf16[32,36,768]{2,1,0:T(8,128)(2,1)S(1)} %get-tuple-element.35, bf16[1,2048,768]{2,1,0:T(8,128)(2,1)S(1)} %copy-done.9), kind=kOutput, calls=%fused_computation.4 | convolution fusion | flops 3628597248 | bytes 19070976 | tf_op jit(solution)/shard_map/dot_general | solution.py:172
  244.0 5.9 %fusion.7 = f32[1,128,8]{2,0,1:T(1,128)S(1)} fusion(bf16[1152,1,1]{0,1,2:T(2,128)(2,1)S(1)} %reshape.327, s32[1024]{0:T(1024)S(1)} %multiply_add_fusion), kind=kOutput, calls=%fused_computation.14 | convolution fusion | flops 3538944 | bytes 10496 | tf_op jit(solution)/shard_map/dot_general | solution.py:252
  251.6 6.4 %pad_maximum_fusion = bf16[32,38,2048]{2,1,0:T(8,128)(2,1)} fusion(bf16[32,1,2048]{2,1,0:T(2,128)(2,1)S(1)} %copy.49, bf16[32,1,2048]{2,1,0:T(2,128)(2,1)S(1)} %copy.48, bf16[32,36,2048]{2,1,0:T(8,128)(2,1)} %add_convert_fusion), kind=kLoop, calls=%fused_computation.8 | loop fusion | flops 14942208 | bytes 9961472 | tf_op jit(solution)/shard_map/concatenate | solution.py:267
  258.0 19.9 %all-to-all-done.3 = bf16[32,36,1024]{2,1,0:T(8,128)(2,1)} async-done(((bf16[32,36,1024]{2,1,0:T(8,128)(2,1)}), bf16[32,36,1024]{2,1,0:T(8,128)(2,1)}, u32[]{:S(2)}, u32[]{:S(2)}) %all-to-all-start.3) | async-done | bytes 2359328 | tf_op jit(solution)/shard_map/all_to_all | solution.py:230
  281.6 9.0 %fusion.22 = bf16[1,768,2048]{2,1,0:T(8,128)(2,1)} fusion(bf16[32,36,768]{2,1,0:T(8,128)(2,1)S(1)} %copy-done.4, bf16[32,36,2048]{2,1,0:T(8,128)(2,1)} %bitcast.90, f32[32,36]{1,0:T(8,128)S(1)} %bitcast.94), kind=kOutput, calls=%fused_computation.39 | convolution fusion | flops 3632529408 | bytes 9638400 | tf_op jit(solution)/shard_map/dot_general | solution.py:174
  290.6 4.2 fusion.44
  294.8 4.1 fusion.40
  298.9 4.1 fusion.41
  304.8 4.1 fusion.45
  310.8 88.3 %all-to-all-done.2 = bf16[32,38,2048]{2,1,0:T(8,128)(2,1)} async-done(((bf16[32,38,2048]{2,1,0:T(8,128)(2,1)}), bf16[32,38,2048]{2,1,0:T(8,128)(2,1)}, u32[]{:S(2)}, u32[]{:S(2)}) %all-to-all-start.2) | async-done | bytes 4980768 | tf_op jit(solution)/shard_map/all_to_all | solution.py:268
  410.1 5.7 %all-to-all-done.4 = f32[32,1,2048]{2,1,0:T(1,128)} async-done(((f32[32,1,2048]{2,1,0:T(1,128)}), f32[32,1,2048]{2,1,0:T(1,128)}, u32[]{:S(2)}, u32[]{:S(2)}) %all-to-all-start.4) | async-done | bytes 262176 | tf_op jit(solution)/shard_map/all_to_all | solution.py:275
  (87 shorter events, 50.0 us)
Async XLA Ops:
  0.6 44.0 %copy-start = (bf16[1,768,2048]{2,1,0:T(8,128)(2,1)S(1)}, bf16[1,768,2048]{2,1,0:T(8,128)(2,1)}, u32[]{:S(2)}) copy-start(bf16[1,768,2048]{2,1,0:T(8,128)(2,1)} %param.17) | copy-start | bytes 9437188
  0.6 4.0 copy-start.7
  11.6 125.4 %all-to-all-start = ((bf16[32,37,2048]{2,1,0:T(8,128)(2,1)}), bf16[32,37,2048]{2,1,0:T(8,128)(2,1)}, u32[]{:S(2)}, u32[]{:S(2)}) async-start(bf16[32,37,2048]{2,1,0:T(8,128)(2,1)} %convolution_convert_fusion.2), calls=%async_computation | async-start | bytes 10485760 | tf_op jit(solution)/shard_map/all_to_all | solution.py:218
  35.2 4.5 %copy-start.2 = (f32[32,36,768]{2,1,0:T(8,128)S(1)}, f32[32,36,768]{2,1,0:T(8,128)}, u32[]{:S(2)}) copy-start(f32[32,36,768]{2,1,0:T(8,128)} %reshape.317) | copy-start | bytes 10616836
  39.8 4.8 %copy-start.5 = (bf16[32,36,768]{2,1,0:T(8,128)(2,1)S(1)}, bf16[32,36,768]{2,1,0:T(8,128)(2,1)}, u32[]{:S(2)}) copy-start(bf16[32,36,768]{2,1,0:T(8,128)(2,1)} %convert_element_type.177) | copy-start | bytes 5308420
  137.1 4.8 %slice-start = ((s8[5242880]{0:T(1024)(128)(4,1)}), s8[4194304]{0:T(1024)(128)(4,1)S(1)}, s32[]{:S(2)}) async-start(s8[5242880]{0:T(1024)(128)(4,1)} %bitcast.91), calls=%async_computation.5 | async-start | bytes 8388608
  137.1 4.8 %slice-start.1 = ((s8[5242880]{0:T(1024)(128)(4,1)}), s8[1048576]{0:T(1024)(128)(4,1)S(1)}, s32[]{:S(2)}) async-start(s8[5242880]{0:T(1024)(128)(4,1)} %bitcast.91), calls=%async_computation.6 | async-start | bytes 2097152
  148.0 64.9 %all-to-all-start.1 = ((bf16[32,37,1024]{2,1,0:T(8,128)(2,1)}), bf16[32,37,1024]{2,1,0:T(8,128)(2,1)}, u32[]{:S(2)}, u32[]{:S(2)}) async-start(bf16[32,37,1024]{2,1,0:T(8,128)(2,1)} %pad_maximum_fusion.3), calls=%async_computation.1 | async-start | bytes 5242880 | tf_op jit(solution)/shard_map/all_to_all | solution.py:249
  212.9 65.1 %all-to-all-start.3 = ((bf16[32,36,1024]{2,1,0:T(8,128)(2,1)}), bf16[32,36,1024]{2,1,0:T(8,128)(2,1)}, u32[]{:S(2)}, u32[]{:S(2)}) async-start(bf16[32,36,1024]{2,1,0:T(8,128)(2,1)} %get-tuple-element.37), calls=%async_computation.3 | async-start | bytes 5242880 | tf_op jit(solution)/shard_map/all_to_all | solution.py:230
  216.6 10.5 %copy-start.8 = (bf16[1,2048,768]{2,1,0:T(8,128)(2,1)S(1)}, bf16[1,2048,768]{2,1,0:T(8,128)(2,1)}, u32[]{:S(2)}) copy-start(bf16[1,2048,768]{2,1,0:T(8,128)(2,1)} %param.15) | copy-start | bytes 9437188
  227.1 7.0 %copy-start.12 = (bf16[32,36,768]{2,1,0:T(8,128)(2,1)}, bf16[32,36,768]{2,1,0:T(8,128)(2,1)S(1)}, u32[]{:S(2)}) copy-start(bf16[32,36,768]{2,1,0:T(8,128)(2,1)S(1)} %get-tuple-element.36) | copy-start | bytes 5308420
  227.1 7.0 %copy-start.10 = (bf16[32,36,768]{2,1,0:T(8,128)(2,1)}, bf16[32,36,768]{2,1,0:T(8,128)(2,1)S(1)}, u32[]{:S(2)}) copy-start(bf16[32,36,768]{2,1,0:T(8,128)(2,1)S(1)} %get-tuple-element.35) | copy-start | bytes 5308420
  227.1 7.0 %copy-start.9 = (bf16[1,2048,768]{2,1,0:T(8,128)(2,1)S(1)}, bf16[1,2048,768]{2,1,0:T(8,128)(2,1)}, u32[]{:S(2)}) copy-start(bf16[1,2048,768]{2,1,0:T(8,128)(2,1)} %param.16) | copy-start | bytes 9437188
  234.1 16.0 %copy-start.3 = (bf16[128,2048]{1,0:T(8,128)(2,1)S(1)}, bf16[128,2048]{1,0:T(8,128)(2,1)}, u32[]{:S(2)}) copy-start(bf16[128,2048]{1,0:T(8,128)(2,1)} %param.9) | copy-start | bytes 1572868
  258.0 23.5 %copy-start.4 = (bf16[32,36,768]{2,1,0:T(8,128)(2,1)S(1)}, bf16[32,36,768]{2,1,0:T(8,128)(2,1)}, u32[]{:S(2)}) copy-start(bf16[32,36,768]{2,1,0:T(8,128)(2,1)} %multiply_convert_fusion.2) | copy-start | bytes 5308420
  277.9 121.1 %all-to-all-start.2 = ((bf16[32,38,2048]{2,1,0:T(8,128)(2,1)}), bf16[32,38,2048]{2,1,0:T(8,128)(2,1)}, u32[]{:S(2)}, u32[]{:S(2)}) async-start(bf16[32,38,2048]{2,1,0:T(8,128)(2,1)} %pad_maximum_fusion), calls=%async_computation.2 | async-start | bytes 10485760 | tf_op jit(solution)/shard_map/all_to_all | solution.py:268
  281.6 9.0 %copy-start.11 = (bf16[32,36,768]{2,1,0:T(8,128)(2,1)S(1)}, bf16[32,36,768]{2,1,0:T(8,128)(2,1)}, u32[]{:S(2)}) copy-start(bf16[32,36,768]{2,1,0:T(8,128)(2,1)} %copy-done.10) | copy-start | bytes 5308420
  290.6 4.2 %copy-start.13 = (bf16[32,36,768]{2,1,0:T(8,128)(2,1)S(1)}, bf16[32,36,768]{2,1,0:T(8,128)(2,1)}, u32[]{:S(2)}) copy-start(bf16[32,36,768]{2,1,0:T(8,128)(2,1)} %copy-done.12) | copy-start | bytes 5308420
  402.2 13.7 %all-to-all-start.4 = ((f32[32,1,2048]{2,1,0:T(1,128)}), f32[32,1,2048]{2,1,0:T(1,128)}, u32[]{:S(2)}, u32[]{:S(2)}) async-start(f32[32,1,2048]{2,1,0:T(1,128)} %broadcast_in_dim.37), calls=%async_computation.4 | async-start | bytes 524288 | tf_op jit(solution)/shard_map/all_to_all | solution.py:275
  405.5 3.5 copy-start.6
  405.5 15.6 %copy-start.1 = (bf16[1,768,2048]{2,1,0:T(8,128)(2,1)S(1)}, bf16[1,768,2048]{2,1,0:T(8,128)(2,1)}, u32[]{:S(2)}) copy-start(bf16[1,768,2048]{2,1,0:T(8,128)(2,1)} %param.17) | copy-start | bytes 9437188

commit v14 on v13

--- a/solution.py
+++ b/solution.py
@@ -222,13 +222,16 @@
     got_cot_w, hidden, expert_out = lax.optimization_barrier((got_cot_w, hidden, expert_out))
     got_cot = got_cot_w[:, :capacity, :]
     got_weight = got_cot_w[:, capacity, :capacity]
-    grid_tokens = jnp.dot(grid_table, tokens, preferred_element_type=jnp.float32).astype(
-        jnp.bfloat16
-    )
-    got_cot, grid_tokens = lax.optimization_barrier((got_cot, grid_tokens))
     half = width // 2
+    tokens_a = jnp.dot(grid_table, tokens[:, :half], preferred_element_type=jnp.float32).astype(
+        jnp.bfloat16
+    )
+    tokens_b = jnp.dot(grid_table, tokens[:, half:], preferred_element_type=jnp.float32).astype(
+        jnp.bfloat16
+    )
+    got_cot, tokens_a, tokens_b = lax.optimization_barrier((got_cot, tokens_a, tokens_b))
     got_tokens_a = lax.all_to_all(
-        grid_tokens[:, :, :half], axes, split_axis=0, concat_axis=0, tiled=True
+        tokens_a, axes, split_axis=0, concat_axis=0, tiled=True
     )
     cot_rows = got_cot
     grad_rows, grad_gate_pre, grad_up_pre, grad_down_w = expert_from_cot(
@@ -245,7 +248,7 @@
         cot_rows.astype(jnp.float32) * expert_out.astype(jnp.float32), axis=2
     ).astype(jnp.bfloat16)
     dot_row = jnp.pad(slot_route_dot, ((0, 0), (0, half - capacity)))[:, None, :]
-    send_b = jnp.concatenate([grid_tokens[:, :, half:], dot_row], axis=1)
+    send_b = jnp.concatenate([tokens_b, dot_row], axis=1)
     got_b = lax.all_to_all(send_b, axes, split_axis=0, concat_axis=0, tiled=True)
     got_tokens_b = got_b[:, :capacity, :]
     route_dot = got_b[:, capacity, :capacity].reshape(-1)

time: 426 us -> 423 us (level)
  local copies, waits for them, and re-layouts: 24.8 us -> 20 us
    slice x1 -> x0, local copies, waits for them, and re-layouts: 4.78 us -> none  [body(): grid_tokens[:, :, :half]]
  transfers between devices with their start and end apart: 5 -> 5, of which waited for: 5 -> 5; matrix products, arithmetic and copies ran while one was open for 25% -> 26% of each run, Pallas kernels for 0% -> 0%
where the time goes in v14:
time: 423 us; the launch traced here: 418 us
  waiting for transfers between devices  259 us (61%)
  matrix products  83.4 us (20%)
  other arithmetic  32.5 us (8%)
  starting transfers between devices  22 us (5%)
  local copies, waits for them, and re-layouts  20 us (5%)
    all_to_all x1, waiting for transfers between devices, body(): lax.all_to_all(send_back, axes, split_axis=0, concat_axis=0, tiled=True)  88.3 us
    all_to_all x1, waiting for transfers between devices, body(): lax.all_to_all(send_cot, axes, split_axis=0, concat_axis=0, tiled=True)  84.5 us
    all_to_all x1, waiting for transfers between devices, body(): lax.all_to_all(send_b, axes, split_axis=0, concat_axis=0, tiled=True)  60.5 us
    all_to_all x1, waiting for transfers between devices, body(): lax.all_to_all(tokens_a, axes, split_axis=0, concat_axis=0, tiled=True)  19.9 us
    dot_general x1, matrix products, expert_from_cot(): lax.dot_general(scaled_cot, down_matrix, last_t, preferred_element_type=j...  10.5 us
    convert_element_type x2, other arithmetic, expert_local(): (gate_value * sigmoid_gate * up_pre.astype(jnp.float32)).astype(jnp.bfloa...  9.16 us
    dot_general x1, matrix products, expert_from_cot(): lax.dot_general(hidden, scaled_cot, grid_rows, preferred_element_type=jnp...  8.99 us
    dot_general x1, matrix products, expert_from_cot(): lax.dot_general(grad_up_pre, up_matrix, last_t, preferred_element_type=jn...  8.88 us
  transfers between devices with their start and end apart: 5, of which 5 were waited for; matrix products, arithmetic and copies ran while one was open for 26% of the time, Pallas kernels for 0%

profile of v14, /device:TPU:0, one launch (start us, length us, event | category | flops | bytes accessed | tf_op | source)
XLA Modules:
  0.0 418.1 jit_solution(10338175117200009697)
XLA Ops:
  6.8 4.9 %convolution_convert_fusion.1 = bf16[32,37,2048]{2,1,0:T(8,128)(2,1)} fusion(pred[32,36,128]{2,1,0:T(8,128)(4,1)S(1)} %fusion.60, pred[32,1,160]{2,1,0:T(4,128)(4,1)S(1)} %copy.44, bf16[32,36]{1,0:T(8,128)(2,1)S(1)} %reshape.315, bf16[128,2048]{1,0:T(8,128)(2,1)} %param.10), kind=kOutput, calls=%fused_computation.20 | convolution fusion | flops 780526592 | bytes 5528832 | tf_op jit(solution)/shard_map/dot_general | solution.py:217
  11.6 7.9 %all-to-all-start = ((bf16[32,37,2048]{2,1,0:T(8,128)(2,1)}), bf16[32,37,2048]{2,1,0:T(8,128)(2,1)}, u32[]{:S(2)}, u32[]{:S(2)}) async-start(bf16[32,37,2048]{2,1,0:T(8,128)(2,1)} %convolution_convert_fusion.1), calls=%async_computation | async-start | bytes 10485760 | tf_op jit(solution)/shard_map/all_to_all | solution.py:218
  19.6 3.9 reshape.317
  23.4 3.9 reshape.318
  27.4 4.3 %multiply_convert_fusion.3 = bf16[1,1152,768]{2,1,0:T(8,128)(2,1)} fusion(bf16[1,1152,768]{2,1,0:T(8,128)(2,1)} %param.14, bf16[1,1152,768]{2,1,0:T(8,128)(2,1)} %param.13), kind=kLoop, calls=%fused_computation.26 | loop fusion | flops 7077888 | bytes 5308416 | tf_op jit(solution)/shard_map/convert_element_type | solution.py:144
  41.7 4.9 %multiply_convert_fusion.2 = bf16[32,36,768]{2,1,0:T(8,128)(2,1)} fusion(f32[32,36,768]{2,1,0:T(8,128)} %reshape.318, f32[32,36,768]{2,1,0:T(8,128)S(1)} %copy-done.2), kind=kLoop, calls=%fused_computation.23 | loop fusion | flops 5308416 | bytes 8847360 | tf_op jit(solution)/shard_map/convert_element_type | solution.py:144
  46.5 6.1 %convolution_convert_fusion = bf16[32,36,2048]{2,1,0:T(8,128)(2,1)} fusion(bf16[32,36,768]{2,1,0:T(8,128)(2,1)S(1)} %copy-done.6, bf16[1,768,2048]{2,1,0:T(8,128)(2,1)S(1)} %copy-done), kind=kOutput, calls=%fused_computation.19 | convolution fusion | flops 3626237952 | bytes 9633792 | tf_op jit(solution)/shard_map/dot_general | solution.py:145
  52.6 84.5 %all-to-all-done = bf16[32,37,2048]{2,1,0:T(8,128)(2,1)} async-done(((bf16[32,37,2048]{2,1,0:T(8,128)(2,1)}), bf16[32,37,2048]{2,1,0:T(8,128)(2,1)}, u32[]{:S(2)}, u32[]{:S(2)}) %all-to-all-start) | async-done | bytes 4849696 | tf_op jit(solution)/shard_map/all_to_all | solution.py:218
  137.1 5.7 %fusion.1 = bf16[32,36]{1,0:T(8,128)(2,1)S(1)} fusion(bf16[32,36,2048]{2,1,0:T(8,128)(2,1)} %bitcast.93, bf16[32,36,2048]{2,1,0:T(8,128)(2,1)} %convolution_convert_fusion), kind=kLoop, calls=%fused_computation.3 | loop fusion | flops 9436032 | bytes 9439488 | tf_op jit(solution)/shard_map/reduce_sum | solution.py:247
  149.3 60.5 %all-to-all-done.1 = bf16[32,37,1024]{2,1,0:T(8,128)(2,1)} async-done(((bf16[32,37,1024]{2,1,0:T(8,128)(2,1)}), bf16[32,37,1024]{2,1,0:T(8,128)(2,1)}, u32[]{:S(2)}, u32[]{:S(2)}) %all-to-all-start.1) | async-done | bytes 2424864 | tf_op jit(solution)/shard_map/all_to_all | solution.py:252
  209.8 3.7 all-to-all-start.3
  213.5 10.5 %multiply_convert_fusion = (bf16[32,36,768]{2,1,0:T(8,128)(2,1)S(1)}, bf16[32,36,768]{2,1,0:T(8,128)(2,1)S(1)}) fusion(f32[32,36,768]{2,1,0:T(8,128)} %reshape.317, f32[32,36,768]{2,1,0:T(8,128)} %reshape.318, bf16[1,768,2048]{2,1,0:T(8,128)(2,1)S(1)} %copy-done, bf16[32,36,2048]{2,1,0:T(8,128)(2,1)} %bitcast.93, f32[32,36]{1,0:T(8,128)S(1)} %bitcast.94), kind=kOutput, calls=%fused_computation.21 | convolution fusion | flops 3642458112 | bytes 18485760 | tf_op jit(solution)/shard_map/dot_general | solution.py:163
  224.0 7.0 %fusion.18 = f32[32,36,2048]{2,1,0:T(8,128)} fusion(bf16[32,36,768]{2,1,0:T(8,128)(2,1)S(1)} %get-tuple-element.38, bf16[1,2048,768]{2,1,0:T(8,128)(2,1)S(1)} %copy-done.9), kind=kOutput, calls=%fused_computation.34 | convolution fusion | flops 3623878656 | bytes 14352384 | tf_op jit(solution)/shard_map/dot_general | solution.py:171
  231.0 8.9 %add_convert_fusion = bf16[32,36,2048]{2,1,0:T(8,128)(2,1)} fusion(f32[32,36,2048]{2,1,0:T(8,128)} %fusion.18, bf16[32,36,768]{2,1,0:T(8,128)(2,1)S(1)} %get-tuple-element.37, bf16[1,2048,768]{2,1,0:T(8,128)(2,1)S(1)} %copy-done.10), kind=kOutput, calls=%fused_computation.4 | convolution fusion | flops 3628597248 | bytes 19070976 | tf_op jit(solution)/shard_map/dot_general | solution.py:172
  240.9 5.9 %fusion.7 = f32[1,128,8]{2,0,1:T(1,128)S(1)} fusion(bf16[1152,1,1]{0,1,2:T(2,128)(2,1)S(1)} %reshape.328, s32[1024]{0:T(1024)S(1)} %multiply_add_fusion), kind=kOutput, calls=%fused_computation.14 | convolution fusion | flops 3538944 | bytes 10496 | tf_op jit(solution)/shard_map/dot_general | solution.py:255
  248.5 6.5 %pad_maximum_fusion = bf16[32,38,2048]{2,1,0:T(8,128)(2,1)} fusion(bf16[32,1,2048]{2,1,0:T(2,128)(2,1)S(1)} %copy.49, bf16[32,1,2048]{2,1,0:T(2,128)(2,1)S(1)} %copy.48, bf16[32,36,2048]{2,1,0:T(8,128)(2,1)} %add_convert_fusion), kind=kLoop, calls=%fused_computation.8 | loop fusion | flops 14942208 | bytes 9961472 | tf_op jit(solution)/shard_map/concatenate | solution.py:270
  255.0 19.9 %all-to-all-done.3 = bf16[32,36,1024]{2,1,0:T(8,128)(2,1)} async-done(((bf16[32,36,1024]{2,1,0:T(8,128)(2,1)}), bf16[32,36,1024]{2,1,0:T(8,128)(2,1)}, u32[]{:S(2)}, u32[]{:S(2)}) %all-to-all-start.3) | async-done | bytes 2359328 | tf_op jit(solution)/shard_map/all_to_all | solution.py:233
  278.5 9.0 %fusion.22 = bf16[1,768,2048]{2,1,0:T(8,128)(2,1)} fusion(bf16[32,36,768]{2,1,0:T(8,128)(2,1)S(1)} %copy-done.5, bf16[32,36,2048]{2,1,0:T(8,128)(2,1)} %bitcast.93, f32[32,36]{1,0:T(8,128)S(1)} %bitcast.95), kind=kOutput, calls=%fused_computation.38 | convolution fusion | flops 3632529408 | bytes 9638400 | tf_op jit(solution)/shard_map/dot_general | solution.py:174
  287.5 4.2 %fusion.44 = bf16[1,1024,768]{2,1,0:T(8,128)(2,1)S(1)} fusion(bf16[32,36,1024]{2,1,0:T(8,128)(2,1)} %all-to-all-done.3, bf16[32,36,768]{2,1,0:T(8,128)(2,1)S(1)} %copy-done.12), kind=kOutput, calls=%fused_computation.55 | convolution fusion | flops 1812725760 | bytes 5701632 | tf_op jit(solution)/shard_map/dot_general | solution.py:286
  291.7 4.1 fusion.40
  295.8 4.1 fusion.45
  301.7 4.1 fusion.41
  307.6 88.3 %all-to-all-done.2 = bf16[32,38,2048]{2,1,0:T(8,128)(2,1)} async-done(((bf16[32,38,2048]{2,1,0:T(8,128)(2,1)}), bf16[32,38,2048]{2,1,0:T(8,128)(2,1)}, u32[]{:S(2)}, u32[]{:S(2)}) %all-to-all-start.2) | async-done | bytes 4980768 | tf_op jit(solution)/shard_map/all_to_all | solution.py:271
  406.9 5.7 %all-to-all-done.4 = f32[32,1,2048]{2,1,0:T(1,128)} async-done(((f32[32,1,2048]{2,1,0:T(1,128)}), f32[32,1,2048]{2,1,0:T(1,128)}, u32[]{:S(2)}, u32[]{:S(2)}) %all-to-all-start.4) | async-done | bytes 262176 | tf_op jit(solution)/shard_map/all_to_all | solution.py:278
  (84 shorter events, 48.7 us)
Async XLA Ops:
  0.6 45.9 %copy-start = (bf16[1,768,2048]{2,1,0:T(8,128)(2,1)S(1)}, bf16[1,768,2048]{2,1,0:T(8,128)(2,1)}, u32[]{:S(2)}) copy-start(bf16[1,768,2048]{2,1,0:T(8,128)(2,1)} %param.17) | copy-start | bytes 9437188
  0.6 4.2 %copy-start.8 = (s32[128,8]{0,1:T(8,128)S(1)}, s32[128,8]{0,1:T(8,128)}, u32[]{:S(2)}) copy-start(s32[128,8]{0,1:T(8,128)} %param.11) | copy-start | bytes 12292
  11.6 125.4 %all-to-all-start = ((bf16[32,37,2048]{2,1,0:T(8,128)(2,1)}), bf16[32,37,2048]{2,1,0:T(8,128)(2,1)}, u32[]{:S(2)}, u32[]{:S(2)}) async-start(bf16[32,37,2048]{2,1,0:T(8,128)(2,1)} %convolution_convert_fusion.1), calls=%async_computation | async-start | bytes 10485760 | tf_op jit(solution)/shard_map/all_to_all | solution.py:218
  35.2 6.4 %copy-start.2 = (f32[32,36,768]{2,1,0:T(8,128)S(1)}, f32[32,36,768]{2,1,0:T(8,128)}, u32[]{:S(2)}) copy-start(f32[32,36,768]{2,1,0:T(8,128)} %reshape.317) | copy-start | bytes 10616836
  41.7 4.9 %copy-start.6 = (bf16[32,36,768]{2,1,0:T(8,128)(2,1)S(1)}, bf16[32,36,768]{2,1,0:T(8,128)(2,1)}, u32[]{:S(2)}) copy-start(bf16[32,36,768]{2,1,0:T(8,128)(2,1)} %convert_element_type.180) | copy-start | bytes 5308420
  137.1 5.8 %copy-start.3 = (bf16[32,36,1024]{2,1,0:T(8,128)(2,1)S(1)}, bf16[32,36,1024]{2,1,0:T(8,128)(2,1)}, u32[]{:S(2)}) copy-start(bf16[32,36,1024]{2,1,0:T(8,128)(2,1)} %convolution_convert_fusion.2) | copy-start | bytes 7077892
  144.9 64.9 %all-to-all-start.1 = ((bf16[32,37,1024]{2,1,0:T(8,128)(2,1)}), bf16[32,37,1024]{2,1,0:T(8,128)(2,1)}, u32[]{:S(2)}, u32[]{:S(2)}) async-start(bf16[32,37,1024]{2,1,0:T(8,128)(2,1)} %pad_maximum_fusion.3), calls=%async_computation.1 | async-start | bytes 5242880 | tf_op jit(solution)/shard_map/all_to_all | solution.py:252
  209.8 65.1 %all-to-all-start.3 = ((bf16[32,36,1024]{2,1,0:T(8,128)(2,1)}), bf16[32,36,1024]{2,1,0:T(8,128)(2,1)}, u32[]{:S(2)}, u32[]{:S(2)}) async-start(bf16[32,36,1024]{2,1,0:T(8,128)(2,1)} %convolution_convert_fusion.3), calls=%async_computation.3 | async-start | bytes 5242880 | tf_op jit(solution)/shard_map/all_to_all | solution.py:233
  213.5 10.5 %copy-start.9 = (bf16[1,2048,768]{2,1,0:T(8,128)(2,1)S(1)}, bf16[1,2048,768]{2,1,0:T(8,128)(2,1)}, u32[]{:S(2)}) copy-start(bf16[1,2048,768]{2,1,0:T(8,128)(2,1)} %param.15) | copy-start | bytes 9437188
  224.0 7.0 %copy-start.13 = (bf16[32,36,768]{2,1,0:T(8,128)(2,1)}, bf16[32,36,768]{2,1,0:T(8,128)(2,1)S(1)}, u32[]{:S(2)}) copy-start(bf16[32,36,768]{2,1,0:T(8,128)(2,1)S(1)} %get-tuple-element.38) | copy-start | bytes 5308420
  224.0 7.0 %copy-start.11 = (bf16[32,36,768]{2,1,0:T(8,128)(2,1)}, bf16[32,36,768]{2,1,0:T(8,128)(2,1)S(1)}, u32[]{:S(2)}) copy-start(bf16[32,36,768]{2,1,0:T(8,128)(2,1)S(1)} %get-tuple-element.37) | copy-start | bytes 5308420
  224.0 7.0 %copy-start.10 = (bf16[1,2048,768]{2,1,0:T(8,128)(2,1)S(1)}, bf16[1,2048,768]{2,1,0:T(8,128)(2,1)}, u32[]{:S(2)}) copy-start(bf16[1,2048,768]{2,1,0:T(8,128)(2,1)} %param.16) | copy-start | bytes 9437188
  231.0 16.0 %copy-start.4 = (bf16[128,2048]{1,0:T(8,128)(2,1)S(1)}, bf16[128,2048]{1,0:T(8,128)(2,1)}, u32[]{:S(2)}) copy-start(bf16[128,2048]{1,0:T(8,128)(2,1)} %param.9) | copy-start | bytes 1572868
  255.0 23.5 %copy-start.5 = (bf16[32,36,768]{2,1,0:T(8,128)(2,1)S(1)}, bf16[32,36,768]{2,1,0:T(8,128)(2,1)}, u32[]{:S(2)}) copy-start(bf16[32,36,768]{2,1,0:T(8,128)(2,1)} %multiply_convert_fusion.2) | copy-start | bytes 5308420
  274.8 121.1 %all-to-all-start.2 = ((bf16[32,38,2048]{2,1,0:T(8,128)(2,1)}), bf16[32,38,2048]{2,1,0:T(8,128)(2,1)}, u32[]{:S(2)}, u32[]{:S(2)}) async-start(bf16[32,38,2048]{2,1,0:T(8,128)(2,1)} %pad_maximum_fusion), calls=%async_computation.2 | async-start | bytes 10485760 | tf_op jit(solution)/shard_map/all_to_all | solution.py:271
  278.4 9.0 %copy-start.12 = (bf16[32,36,768]{2,1,0:T(8,128)(2,1)S(1)}, bf16[32,36,768]{2,1,0:T(8,128)(2,1)}, u32[]{:S(2)}) copy-start(bf16[32,36,768]{2,1,0:T(8,128)(2,1)} %copy-done.11) | copy-start | bytes 5308420
  287.5 4.2 %copy-start.14 = (bf16[32,36,768]{2,1,0:T(8,128)(2,1)S(1)}, bf16[32,36,768]{2,1,0:T(8,128)(2,1)}, u32[]{:S(2)}) copy-start(bf16[32,36,768]{2,1,0:T(8,128)(2,1)} %copy-done.13) | copy-start | bytes 5308420
  399.0 13.7 %all-to-all-start.4 = ((f32[32,1,2048]{2,1,0:T(1,128)}), f32[32,1,2048]{2,1,0:T(1,128)}, u32[]{:S(2)}, u32[]{:S(2)}) async-start(f32[32,1,2048]{2,1,0:T(1,128)} %broadcast_in_dim.37), calls=%async_computation.4 | async-start | bytes 524288 | tf_op jit(solution)/shard_map/all_to_all | solution.py:278
  402.3 3.5 copy-start.7
  402.3 15.6 %copy-start.1 = (bf16[1,768,2048]{2,1,0:T(8,128)(2,1)S(1)}, bf16[1,768,2048]{2,1,0:T(8,128)(2,1)}, u32[]{:S(2)}) copy-start(bf16[1,768,2048]{2,1,0:T(8,128)(2,1)} %param.17) | copy-start | bytes 9437188

commit v15 on v14

--- a/solution.py
+++ b/solution.py
@@ -273,11 +273,11 @@
     got_parts = got_back[:, capacity, :].astype(jnp.float32) + got_back[:, capacity + 1, :].astype(
         jnp.float32
     )
-    chunk_sum = jnp.sum(got_parts, axis=0, keepdims=True)
+    total_tokens = tokens.shape[0] * devices
+    chunk_sum = jnp.sum(got_parts, axis=0, keepdims=True) * (1.0 / math.sqrt(total_tokens))
     spread = jnp.broadcast_to(chunk_sum, got_parts.shape)
     got_sums = lax.all_to_all(spread, axes, split_axis=0, concat_axis=0, tiled=True)
-    total_tokens = tokens.shape[0] * devices
-    grad_router = got_sums.reshape(router_part.shape) * (1.0 / math.sqrt(total_tokens))
+    grad_router = got_sums.reshape(router_part.shape)
     grid_rows = (((0, 1), (0, 1)), ((), ()))
 
     def by_rows(pre):

time: 423 us -> 423 us (level)
  no operation moved by 1% of the time
where the time goes in v15:
time: 423 us; the launch traced here: 418 us
  waiting for transfers between devices  259 us (61%)
  matrix products  83.4 us (20%)
  other arithmetic  32.4 us (8%)
  starting transfers between devices  22 us (5%)
  local copies, waits for them, and re-layouts  20 us (5%)
    all_to_all x1, waiting for transfers between devices, body(): lax.all_to_all(send_back, axes, split_axis=0, concat_axis=0, tiled=True)  88.3 us
    all_to_all x1, waiting for transfers between devices, body(): lax.all_to_all(send_cot, axes, split_axis=0, concat_axis=0, tiled=True)  84.5 us
    all_to_all x1, waiting for transfers between devices, body(): lax.all_to_all(send_b, axes, split_axis=0, concat_axis=0, tiled=True)  60.5 us
    all_to_all x1, waiting for transfers between devices, body(): lax.all_to_all(tokens_a, axes, split_axis=0, concat_axis=0, tiled=True)  19.9 us
    dot_general x1, matrix products, expert_from_cot(): lax.dot_general(scaled_cot, down_matrix, last_t, preferred_element_type=j...  10.5 us
    convert_element_type x2, other arithmetic, expert_local(): (gate_value * sigmoid_gate * up_pre.astype(jnp.float32)).astype(jnp.bfloa...  9.16 us
    dot_general x1, matrix products, expert_from_cot(): lax.dot_general(hidden, scaled_cot, grid_rows, preferred_element_type=jnp...  8.99 us
    dot_general x1, matrix products, expert_from_cot(): lax.dot_general(grad_up_pre, up_matrix, last_t, preferred_element_type=jn...  8.88 us
  transfers between devices with their start and end apart: 5, of which 5 were waited for; matrix products, arithmetic and copies ran while one was open for 26% of the time, Pallas kernels for 0%

profile of v15, /device:TPU:0, one launch (start us, length us, event | category | flops | bytes accessed | tf_op | source)
XLA Modules:
  0.0 418.1 jit_solution(11897410826166436937)
XLA Ops:
  6.8 4.9 %convolution_convert_fusion.1 = bf16[32,37,2048]{2,1,0:T(8,128)(2,1)} fusion(pred[32,36,128]{2,1,0:T(8,128)(4,1)S(1)} %fusion.60, pred[32,1,160]{2,1,0:T(4,128)(4,1)S(1)} %copy.44, bf16[32,36]{1,0:T(8,128)(2,1)S(1)} %reshape.319, bf16[128,2048]{1,0:T(8,128)(2,1)} %param.10), kind=kOutput, calls=%fused_computation.20 | convolution fusion | flops 780526592 | bytes 5528832 | tf_op jit(solution)/shard_map/dot_general | solution.py:217
  11.6 7.9 %all-to-all-start = ((bf16[32,37,2048]{2,1,0:T(8,128)(2,1)}), bf16[32,37,2048]{2,1,0:T(8,128)(2,1)}, u32[]{:S(2)}, u32[]{:S(2)}) async-start(bf16[32,37,2048]{2,1,0:T(8,128)(2,1)} %convolution_convert_fusion.1), calls=%async_computation | async-start | bytes 10485760 | tf_op jit(solution)/shard_map/all_to_all | solution.py:218
  19.6 3.9 reshape.322
  23.4 3.9 reshape.323
  27.4 4.3 %multiply_convert_fusion.3 = bf16[1,1152,768]{2,1,0:T(8,128)(2,1)} fusion(bf16[1,1152,768]{2,1,0:T(8,128)(2,1)} %param.14, bf16[1,1152,768]{2,1,0:T(8,128)(2,1)} %param.13), kind=kLoop, calls=%fused_computation.26 | loop fusion | flops 7077888 | bytes 5308416 | tf_op jit(solution)/shard_map/convert_element_type | solution.py:144
  41.7 4.9 %multiply_convert_fusion.2 = bf16[32,36,768]{2,1,0:T(8,128)(2,1)} fusion(f32[32,36,768]{2,1,0:T(8,128)} %reshape.323, f32[32,36,768]{2,1,0:T(8,128)S(1)} %copy-done.2), kind=kLoop, calls=%fused_computation.23 | loop fusion | flops 5308416 | bytes 8847360 | tf_op jit(solution)/shard_map/convert_element_type | solution.py:144
  46.5 6.1 %convolution_convert_fusion = bf16[32,36,2048]{2,1,0:T(8,128)(2,1)} fusion(bf16[32,36,768]{2,1,0:T(8,128)(2,1)S(1)} %copy-done.6, bf16[1,768,2048]{2,1,0:T(8,128)(2,1)S(1)} %copy-done), kind=kOutput, calls=%fused_computation.19 | convolution fusion | flops 3626237952 | bytes 9633792 | tf_op jit(solution)/shard_map/dot_general | solution.py:145
  52.6 84.5 %all-to-all-done = bf16[32,37,2048]{2,1,0:T(8,128)(2,1)} async-done(((bf16[32,37,2048]{2,1,0:T(8,128)(2,1)}), bf16[32,37,2048]{2,1,0:T(8,128)(2,1)}, u32[]{:S(2)}, u32[]{:S(2)}) %all-to-all-start) | async-done | bytes 4849696 | tf_op jit(solution)/shard_map/all_to_all | solution.py:218
  137.1 5.7 %fusion.1 = bf16[32,36]{1,0:T(8,128)(2,1)S(1)} fusion(bf16[32,36,2048]{2,1,0:T(8,128)(2,1)} %bitcast.93, bf16[32,36,2048]{2,1,0:T(8,128)(2,1)} %convolution_convert_fusion), kind=kLoop, calls=%fused_computation.3 | loop fusion | flops 9436032 | bytes 9439488 | tf_op jit(solution)/shard_map/reduce_sum | solution.py:247
  149.3 60.5 %all-to-all-done.1 = bf16[32,37,1024]{2,1,0:T(8,128)(2,1)} async-done(((bf16[32,37,1024]{2,1,0:T(8,128)(2,1)}), bf16[32,37,1024]{2,1,0:T(8,128)(2,1)}, u32[]{:S(2)}, u32[]{:S(2)}) %all-to-all-start.1) | async-done | bytes 2424864 | tf_op jit(solution)/shard_map/all_to_all | solution.py:252
  209.8 3.7 all-to-all-start.3
  213.5 10.5 %multiply_convert_fusion = (bf16[32,36,768]{2,1,0:T(8,128)(2,1)S(1)}, bf16[32,36,768]{2,1,0:T(8,128)(2,1)S(1)}) fusion(f32[32,36,768]{2,1,0:T(8,128)} %reshape.322, f32[32,36,768]{2,1,0:T(8,128)} %reshape.323, bf16[1,768,2048]{2,1,0:T(8,128)(2,1)S(1)} %copy-done, bf16[32,36,2048]{2,1,0:T(8,128)(2,1)} %bitcast.93, f32[32,36]{1,0:T(8,128)S(1)} %bitcast.94), kind=kOutput, calls=%fused_computation.21 | convolution fusion | flops 3642458112 | bytes 18485760 | tf_op jit(solution)/shard_map/dot_general | solution.py:163
  224.0 7.0 %fusion.18 = f32[32,36,2048]{2,1,0:T(8,128)} fusion(bf16[32,36,768]{2,1,0:T(8,128)(2,1)S(1)} %get-tuple-element.38, bf16[1,2048,768]{2,1,0:T(8,128)(2,1)S(1)} %copy-done.9), kind=kOutput, calls=%fused_computation.34 | convolution fusion | flops 3623878656 | bytes 14352384 | tf_op jit(solution)/shard_map/dot_general | solution.py:171
  231.0 8.9 %add_convert_fusion = bf16[32,36,2048]{2,1,0:T(8,128)(2,1)} fusion(f32[32,36,2048]{2,1,0:T(8,128)} %fusion.18, bf16[32,36,768]{2,1,0:T(8,128)(2,1)S(1)} %get-tuple-element.37, bf16[1,2048,768]{2,1,0:T(8,128)(2,1)S(1)} %copy-done.10), kind=kOutput, calls=%fused_computation.4 | convolution fusion | flops 3628597248 | bytes 19070976 | tf_op jit(solution)/shard_map/dot_general | solution.py:172
  240.9 5.9 %fusion.7 = f32[1,128,8]{2,0,1:T(1,128)S(1)} fusion(bf16[1152,1,1]{0,1,2:T(2,128)(2,1)S(1)} %reshape.333, s32[1024]{0:T(1024)S(1)} %multiply_add_fusion), kind=kOutput, calls=%fused_computation.14 | convolution fusion | flops 3538944 | bytes 10496 | tf_op jit(solution)/shard_map/dot_general | solution.py:255
  248.5 6.5 %pad_maximum_fusion = bf16[32,38,2048]{2,1,0:T(8,128)(2,1)} fusion(bf16[32,1,2048]{2,1,0:T(2,128)(2,1)S(1)} %copy.49, bf16[32,1,2048]{2,1,0:T(2,128)(2,1)S(1)} %copy.48, bf16[32,36,2048]{2,1,0:T(8,128)(2,1)} %add_convert_fusion), kind=kLoop, calls=%fused_computation.8 | loop fusion | flops 14942208 | bytes 9961472 | tf_op jit(solution)/shard_map/concatenate | solution.py:270
  255.0 19.9 %all-to-all-done.3 = bf16[32,36,1024]{2,1,0:T(8,128)(2,1)} async-done(((bf16[32,36,1024]{2,1,0:T(8,128)(2,1)}), bf16[32,36,1024]{2,1,0:T(8,128)(2,1)}, u32[]{:S(2)}, u32[]{:S(2)}) %all-to-all-start.3) | async-done | bytes 2359328 | tf_op jit(solution)/shard_map/all_to_all | solution.py:233
  278.5 9.0 %fusion.22 = bf16[1,768,2048]{2,1,0:T(8,128)(2,1)} fusion(bf16[32,36,768]{2,1,0:T(8,128)(2,1)S(1)} %copy-done.5, bf16[32,36,2048]{2,1,0:T(8,128)(2,1)} %bitcast.93, f32[32,36]{1,0:T(8,128)S(1)} %bitcast.95), kind=kOutput, calls=%fused_computation.38 | convolution fusion | flops 3632529408 | bytes 9638400 | tf_op jit(solution)/shard_map/dot_general | solution.py:174
  287.5 4.2 %fusion.44 = bf16[1,1024,768]{2,1,0:T(8,128)(2,1)S(1)} fusion(bf16[32,36,1024]{2,1,0:T(8,128)(2,1)} %all-to-all-done.3, bf16[32,36,768]{2,1,0:T(8,128)(2,1)S(1)} %copy-done.12), kind=kOutput, calls=%fused_computation.55 | convolution fusion | flops 1812725760 | bytes 5701632 | tf_op jit(solution)/shard_map/dot_general | solution.py:286
  291.7 4.1 fusion.40
  295.8 4.1 fusion.45
  301.7 4.1 fusion.41
  307.6 88.3 %all-to-all-done.2 = bf16[32,38,2048]{2,1,0:T(8,128)(2,1)} async-done(((bf16[32,38,2048]{2,1,0:T(8,128)(2,1)}), bf16[32,38,2048]{2,1,0:T(8,128)(2,1)}, u32[]{:S(2)}, u32[]{:S(2)}) %all-to-all-start.2) | async-done | bytes 4980768 | tf_op jit(solution)/shard_map/all_to_all | solution.py:271
  406.9 5.7 %all-to-all-done.4 = f32[32,1,2048]{2,1,0:T(1,128)} async-done(((f32[32,1,2048]{2,1,0:T(1,128)}), f32[32,1,2048]{2,1,0:T(1,128)}, u32[]{:S(2)}, u32[]{:S(2)}) %all-to-all-start.4) | async-done | bytes 262176 | tf_op jit(solution)/shard_map/all_to_all | solution.py:279
  (85 shorter events, 48.6 us)
Async XLA Ops:
  0.6 45.9 %copy-start = (bf16[1,768,2048]{2,1,0:T(8,128)(2,1)S(1)}, bf16[1,768,2048]{2,1,0:T(8,128)(2,1)}, u32[]{:S(2)}) copy-start(bf16[1,768,2048]{2,1,0:T(8,128)(2,1)} %param.17) | copy-start | bytes 9437188
  0.6 4.2 %copy-start.8 = (s32[128,8]{0,1:T(8,128)S(1)}, s32[128,8]{0,1:T(8,128)}, u32[]{:S(2)}) copy-start(s32[128,8]{0,1:T(8,128)} %param.11) | copy-start | bytes 12292
  11.6 125.4 %all-to-all-start = ((bf16[32,37,2048]{2,1,0:T(8,128)(2,1)}), bf16[32,37,2048]{2,1,0:T(8,128)(2,1)}, u32[]{:S(2)}, u32[]{:S(2)}) async-start(bf16[32,37,2048]{2,1,0:T(8,128)(2,1)} %convolution_convert_fusion.1), calls=%async_computation | async-start | bytes 10485760 | tf_op jit(solution)/shard_map/all_to_all | solution.py:218
  35.2 6.4 %copy-start.2 = (f32[32,36,768]{2,1,0:T(8,128)S(1)}, f32[32,36,768]{2,1,0:T(8,128)}, u32[]{:S(2)}) copy-start(f32[32,36,768]{2,1,0:T(8,128)} %reshape.322) | copy-start | bytes 10616836
  41.7 4.9 %copy-start.6 = (bf16[32,36,768]{2,1,0:T(8,128)(2,1)S(1)}, bf16[32,36,768]{2,1,0:T(8,128)(2,1)}, u32[]{:S(2)}) copy-start(bf16[32,36,768]{2,1,0:T(8,128)(2,1)} %convert_element_type.180) | copy-start | bytes 5308420
  137.1 5.8 %copy-start.3 = (bf16[32,36,1024]{2,1,0:T(8,128)(2,1)S(1)}, bf16[32,36,1024]{2,1,0:T(8,128)(2,1)}, u32[]{:S(2)}) copy-start(bf16[32,36,1024]{2,1,0:T(8,128)(2,1)} %convolution_convert_fusion.2) | copy-start | bytes 7077892
  144.9 64.9 %all-to-all-start.1 = ((bf16[32,37,1024]{2,1,0:T(8,128)(2,1)}), bf16[32,37,1024]{2,1,0:T(8,128)(2,1)}, u32[]{:S(2)}, u32[]{:S(2)}) async-start(bf16[32,37,1024]{2,1,0:T(8,128)(2,1)} %pad_maximum_fusion.3), calls=%async_computation.1 | async-start | bytes 5242880 | tf_op jit(solution)/shard_map/all_to_all | solution.py:252
  209.8 65.1 %all-to-all-start.3 = ((bf16[32,36,1024]{2,1,0:T(8,128)(2,1)}), bf16[32,36,1024]{2,1,0:T(8,128)(2,1)}, u32[]{:S(2)}, u32[]{:S(2)}) async-start(bf16[32,36,1024]{2,1,0:T(8,128)(2,1)} %convolution_convert_fusion.3), calls=%async_computation.3 | async-start | bytes 5242880 | tf_op jit(solution)/shard_map/all_to_all | solution.py:233
  213.5 10.5 %copy-start.9 = (bf16[1,2048,768]{2,1,0:T(8,128)(2,1)S(1)}, bf16[1,2048,768]{2,1,0:T(8,128)(2,1)}, u32[]{:S(2)}) copy-start(bf16[1,2048,768]{2,1,0:T(8,128)(2,1)} %param.15) | copy-start | bytes 9437188
  224.0 7.0 %copy-start.13 = (bf16[32,36,768]{2,1,0:T(8,128)(2,1)}, bf16[32,36,768]{2,1,0:T(8,128)(2,1)S(1)}, u32[]{:S(2)}) copy-start(bf16[32,36,768]{2,1,0:T(8,128)(2,1)S(1)} %get-tuple-element.38) | copy-start | bytes 5308420
  224.0 7.0 %copy-start.11 = (bf16[32,36,768]{2,1,0:T(8,128)(2,1)}, bf16[32,36,768]{2,1,0:T(8,128)(2,1)S(1)}, u32[]{:S(2)}) copy-start(bf16[32,36,768]{2,1,0:T(8,128)(2,1)S(1)} %get-tuple-element.37) | copy-start | bytes 5308420
  224.0 7.0 %copy-start.10 = (bf16[1,2048,768]{2,1,0:T(8,128)(2,1)S(1)}, bf16[1,2048,768]{2,1,0:T(8,128)(2,1)}, u32[]{:S(2)}) copy-start(bf16[1,2048,768]{2,1,0:T(8,128)(2,1)} %param.16) | copy-start | bytes 9437188
  231.0 16.0 %copy-start.4 = (bf16[128,2048]{1,0:T(8,128)(2,1)S(1)}, bf16[128,2048]{1,0:T(8,128)(2,1)}, u32[]{:S(2)}) copy-start(bf16[128,2048]{1,0:T(8,128)(2,1)} %param.9) | copy-start | bytes 1572868
  255.0 23.5 %copy-start.5 = (bf16[32,36,768]{2,1,0:T(8,128)(2,1)S(1)}, bf16[32,36,768]{2,1,0:T(8,128)(2,1)}, u32[]{:S(2)}) copy-start(bf16[32,36,768]{2,1,0:T(8,128)(2,1)} %multiply_convert_fusion.2) | copy-start | bytes 5308420
  274.8 121.1 %all-to-all-start.2 = ((bf16[32,38,2048]{2,1,0:T(8,128)(2,1)}), bf16[32,38,2048]{2,1,0:T(8,128)(2,1)}, u32[]{:S(2)}, u32[]{:S(2)}) async-start(bf16[32,38,2048]{2,1,0:T(8,128)(2,1)} %pad_maximum_fusion), calls=%async_computation.2 | async-start | bytes 10485760 | tf_op jit(solution)/shard_map/all_to_all | solution.py:271
  278.4 9.0 %copy-start.12 = (bf16[32,36,768]{2,1,0:T(8,128)(2,1)S(1)}, bf16[32,36,768]{2,1,0:T(8,128)(2,1)}, u32[]{:S(2)}) copy-start(bf16[32,36,768]{2,1,0:T(8,128)(2,1)} %copy-done.11) | copy-start | bytes 5308420
  287.5 4.2 %copy-start.14 = (bf16[32,36,768]{2,1,0:T(8,128)(2,1)S(1)}, bf16[32,36,768]{2,1,0:T(8,128)(2,1)}, u32[]{:S(2)}) copy-start(bf16[32,36,768]{2,1,0:T(8,128)(2,1)} %copy-done.13) | copy-start | bytes 5308420
  399.0 13.7 %all-to-all-start.4 = ((f32[32,1,2048]{2,1,0:T(1,128)}), f32[32,1,2048]{2,1,0:T(1,128)}, u32[]{:S(2)}, u32[]{:S(2)}) async-start(f32[32,1,2048]{2,1,0:T(1,128)} %broadcast_in_dim.37), calls=%async_computation.4 | async-start | bytes 524288 | tf_op jit(solution)/shard_map/all_to_all | solution.py:279
  402.3 3.5 copy-start.7
  402.3 15.5 %copy-start.1 = (bf16[1,768,2048]{2,1,0:T(8,128)(2,1)S(1)}, bf16[1,768,2048]{2,1,0:T(8,128)(2,1)}, u32[]{:S(2)}) copy-start(bf16[1,768,2048]{2,1,0:T(8,128)(2,1)} %param.17) | copy-start | bytes 9437188
